TPU v7x, 32 devices: a whole 2x2x4 slice. The times are simulated.
32 devices in a mesh: prop: 2 (over x), tx: 4 (over y, core), ty: 4 (over z).
Axes of the slice: x: 2, y: 2, z: 4, core: 2. Of those that a mesh axis runs over, the one named last changes fastest.
Arguments:
- electric: float32 [3, 8, 32, 512], P(None, 'prop', 'ty', 'tx'), may hold values from -6 to 6
- magnetic: float32 [3, 8, 32, 512], P(None, 'prop', 'ty', 'tx'), may hold values from -6 to 6
- polarization: float32 [2, 3, 8, 32, 512], P(None, None, 'prop', 'ty', 'tx'), may hold values from -4 to 4
- current: float32 [2, 3, 8, 32, 512], P(None, None, 'prop', 'ty', 'tx'), may hold values from -4 to 4
- material: int32 [32, 512], P('ty', 'tx'), may hold values from 0 to 7
- advance: int32 [4], replicated, may hold values from 0 to 2, as said below
- permittivity: float32 [8], replicated, may hold values from 1.5 to 6
- nonlinear: float32 [8], replicated, may hold values from 0.05 to 0.5
- pole_strength: float32 [2, 8], replicated, may hold values from 0.3 to 3
- pole_frequency: float32 [2, 8], replicated, may hold values from 0.3 to 1.5
- pole_damping: float32 [2, 8], replicated, may hold values from 0.05 to 1
Outputs:
- electric_out: float32 [3, 8, 32, 512], P(None, 'prop', 'ty', 'tx')
- magnetic_out: float32 [3, 8, 32, 512], P(None, 'prop', 'ty', 'tx')
- polarization_out: float32 [2, 3, 8, 32, 512], P(None, None, 'prop', 'ty', 'tx')
- current_out: float32 [2, 3, 8, 32, 512], P(None, None, 'prop', 'ty', 'tx')
- column_energy: float32 [8, 32, 512], P('prop', 'ty', 'tx')
Inputs may be any that keep to these rules, and one draw needn't show every extreme that they name: `advance`: at least one of the 4 entries equals 2.
All inputs are finite; a program needn't handle non-finite values.
Results may differ from a plain program's by a relative error of at most 0.0001.
Values sent between devices are 32-bit elements; how exact they have to be, the bound alone decides.
No kernel may reach another device: no remote copies, remote signals or barrier semaphores. Data moves between devices by JAX's collectives and lax.ppermute only.
A program may use at most 64 MiB of HBM per device.

v0:
```python
import jax
import jax.numpy as jnp
from jax import lax
from jax.sharding import PartitionSpec as P

STEPS = 4
WSHIFT = 2


time_step = 0.5


def passed_along(value, axis, steps):
    count = lax.axis_size(axis)
    first, last = (max(0, -steps), min(count, count - steps))
    return lax.ppermute(value, axis, [(source, source + steps) for source in range(first, last)])


def extended_2(cells, sides, width):
    for axis, dim in sides:
        count = lax.axis_size(axis)
        ends = count - 1
        head = lax.slice_in_dim(cells, 0, width, axis=dim)
        tail = lax.slice_in_dim(cells, cells.shape[dim] - width, cells.shape[dim], axis=dim)
        cells = jnp.concatenate(
            [
                lax.ppermute(tail, axis, [(i, (i + 1) % count) for i in range(ends)]),
                cells,
                lax.ppermute(head, axis, [((i + 1) % count, i) for i in range(ends)]),
            ],
            axis=dim,
        )
    return cells


def entering(value, axis, join, neutral):
    count, mine = (lax.axis_size(axis), lax.axis_index(axis))
    pieces = lax.all_gather(value, axis)
    running = jnp.full_like(value, 0) + jnp.asarray(neutral, value.dtype)

    def step(position, running):
        longer = join(running, pieces[position])
        return jnp.where(position < mine, longer, running)

    return lax.fori_loop(0, count - 1, step, running)


def region(values, z_lo, z_hi, y_lo, y_hi, x_lo, x_hi):
    return values[:, z_lo:z_hi, y_lo:y_hi, x_lo:x_hi]


def curl_at(view, z_lo, z_hi, y_lo, y_hi, x_lo, x_hi):
    centre = region(view, z_lo, z_hi, y_lo, y_hi, x_lo, x_hi)
    step_z = region(view, z_lo + 1, z_hi + 1, y_lo, y_hi, x_lo, x_hi) - centre
    step_y = region(view, z_lo, z_hi, y_lo + 1, y_hi + 1, x_lo, x_hi) - centre
    step_x = region(view, z_lo, z_hi, y_lo, y_hi, x_lo + 1, x_hi + 1) - centre
    return jnp.stack([step_y[2] - step_z[1], step_z[0] - step_x[2], step_x[1] - step_y[0]])


def curl_behind(extended):
    centre = extended[:, 1:, 1:, 1:]
    back_z = centre - extended[:, :-1, 1:, 1:]
    back_y = centre - extended[:, 1:, :-1, 1:]
    back_x = centre - extended[:, 1:, 1:, :-1]
    return jnp.stack([back_y[2] - back_z[1], back_z[0] - back_x[2], back_x[1] - back_y[0]])


def move_planes(values, received, amount, dimension):
    joined = jnp.concatenate([values, received], axis=dimension)
    return lax.dynamic_slice_in_dim(joined, amount, values.shape[dimension], axis=dimension)


def front_of(values, dimension):
    return lax.slice_in_dim(values, 0, WSHIFT, axis=dimension)


def cell_lookup(selector, table):
    return jnp.sum(jnp.where(selector, table[:, None, None], jnp.float32(0.0)), axis=0)


def add_terms(earlier, later):
    return earlier + later


def edge_factor(length, face, dimension, total_dims):
    shape_one = [1] * total_dims
    shape_one[dimension] = length
    marks = lax.broadcasted_iota(jnp.int32, tuple(shape_one), dimension)
    return jnp.where(marks == 0, face, jnp.float32(1.0))


def shift_everything(electric_new, magnetic_c, polarization, current, amount):
    received_e, received_h, received_p, received_j = passed_along(
        (
            front_of(electric_new, 1),
            front_of(magnetic_c, 1),
            front_of(polarization, 2),
            front_of(current, 2),
        ),
        "prop",
        -1,
    )
    return (
        move_planes(electric_new, received_e, amount, 1),
        move_planes(magnetic_c, received_h, amount, 1),
        move_planes(polarization, received_p, amount, 2),
        move_planes(current, received_j, amount, 2),
    )


def body(
    electric,
    magnetic,
    polarization,
    current,
    material,
    advance,
    permittivity,
    nonlinear,
    pole_strength,
    pole_frequency,
    pole_damping,
):
    planes, rows, columns = (electric.shape[1], electric.shape[2], electric.shape[3])
    materials_count = permittivity.shape[0]
    selector = material[None] == lax.broadcasted_iota(
        jnp.int32, (materials_count, rows, columns), 0
    )
    eps_cell = cell_lookup(selector, permittivity)
    kerr_cell = cell_lookup(selector, nonlinear)
    strength = jnp.stack(
        [cell_lookup(selector, pole_strength[0]), cell_lookup(selector, pole_strength[1])]
    )[:, None, None]
    frequency = jnp.stack(
        [cell_lookup(selector, pole_frequency[0]), cell_lookup(selector, pole_frequency[1])]
    )
    damping = jnp.stack(
        [cell_lookup(selector, pole_damping[0]), cell_lookup(selector, pole_damping[1])]
    )
    half_damp = 0.5 * time_step * damping
    keep_rate = ((1.0 - half_damp) / (1.0 + half_damp))[:, None, None]
    drive_rate = (time_step * frequency * frequency / (1.0 + half_damp))[:, None, None]
    face_z = (lax.axis_index("prop") > 0).astype(jnp.float32)
    face_y = (lax.axis_index("ty") > 0).astype(jnp.float32)
    face_x = (lax.axis_index("tx") > 0).astype(jnp.float32)
    edge_mask = (
        edge_factor(planes + 1, face_z, 0, 3)
        * edge_factor(rows + 1, face_y, 1, 3)
        * edge_factor(columns + 1, face_x, 2, 3)
    )
    reach = 1
    electric_state = electric
    magnetic_state = magnetic
    for moment in range(STEPS):
        padded_e, padded_h = (
            extended_2(electric_state, (("prop", 1), ("tx", 3), ("ty", 2)), reach),
            extended_2(magnetic_state, (("prop", 1), ("tx", 3), ("ty", 2)), reach),
        )
        electric_c = padded_e[:, 1:-1, 1:-1, 1:-1]
        extended = region(
            padded_h, 0, planes + 1, 0, rows + 1, 0, columns + 1
        ) - time_step * curl_at(padded_e, 0, planes + 1, 0, rows + 1, 0, columns + 1)
        extended = extended * edge_mask[None]
        magnetic_c = extended[:, 1:, 1:, 1:]
        squared = jnp.sum(electric_c * electric_c, axis=0)
        current = keep_rate * current + drive_rate * (strength * electric_c[None] - polarization)
        polarization = polarization + time_step * current
        curl_h = curl_behind(extended)
        electric_new = electric_c + time_step * (curl_h - current[0] - current[1]) / (
            eps_cell + kerr_cell * squared
        )
        amount = advance[moment]
        electric_state, magnetic_state, polarization, current = shift_everything(
            electric_new, magnetic_c, polarization, current, amount
        )
    density = eps_cell * jnp.sum(electric_state * electric_state, axis=0) + jnp.sum(
        magnetic_state * magnetic_state, axis=0
    )
    totals = jnp.sum(density, axis=0)
    prefix = entering(totals, "prop", add_terms, jnp.zeros_like(totals))
    window_planes_count = jnp.float32(planes * lax.axis_size("prop"))
    column_energy = (prefix[None] + jnp.cumsum(density, axis=0)) / window_planes_count
    return (electric_state, magnetic_state, polarization, current, column_energy)


def solution(mesh):
    return jax.shard_map(
        body,
        mesh=mesh,
        in_specs=(
            P(None, "prop", "ty", "tx"),
            P(None, "prop", "ty", "tx"),
            P(None, None, "prop", "ty", "tx"),
            P(None, None, "prop", "ty", "tx"),
            P("ty", "tx"),
            P(),
            P(),
            P(),
            P(),
            P(),
            P(),
        ),
        out_specs=(
            P(None, "prop", "ty", "tx"),
            P(None, "prop", "ty", "tx"),
            P(None, None, "prop", "ty", "tx"),
            P(None, None, "prop", "ty", "tx"),
            P("prop", "ty", "tx"),
        ),
        check_vma=False,
    )
```

profile of v0, /device:TPU:4, one launch (start us, length us, event | category | flops | bytes accessed | tf_op | source)
XLA Modules:
  0.0 192.1 jit_solution(15622291023835284275)
XLA Ops:
  1.5 3.5 %collective-permute-start = (f32[3,1,8,128]{3,2,1,0:T(8,128)S(1)}, f32[3,1,8,128]{3,2,1,0:T(8,128)S(1)}, u32[]{:S(2)}, u32[]{:S(2)}) collective-permute-start(f32[3,1,8,128]{3,2,1,0:T(8,128)S(1)} %get-tuple-element.139), channel_id=1, source_target_pairs={{0,16},{1,17},{2,18},{3,19},{4,20},{5,21},{6,22},{7,23},{8,24},{9,... | collective-permute-start | bytes 36872 | tf_op jit(solution)/shard_map/ppermute | solution.py:27
  6.3 4.5 %collective-permute-start.5 = (f32[3,1,8,128]{3,2,1,0:T(8,128)S(1)}, f32[3,1,8,128]{3,2,1,0:T(8,128)S(1)}, u32[]{:S(2)}, u32[]{:S(2)}) collective-permute-start(f32[3,1,8,128]{3,2,1,0:T(8,128)S(1)} %get-tuple-element.137), channel_id=1, source_target_pairs={{0,16},{1,17},{2,18},{3,19},{4,20},{5,21},{6,22},{7,23},{8,24},{9,... | collective-permute-start | bytes 36872 | tf_op jit(solution)/shard_map/ppermute | solution.py:27
  25.4 2.5 %collective-permute-start.8 = (f32[3,6,8,1]{3,2,1,0:T(8,128)S(1)}, f32[3,6,8,1]{3,2,1,0:T(8,128)S(1)}, u32[]{:S(2)}, u32[]{:S(2)}) collective-permute-start(f32[3,6,8,1]{3,2,1,0:T(8,128)S(1)} %get-tuple-element.107), channel_id=1, source_target_pairs={{4,0},{8,4},{12,8},{5,1},{9,5},{13,9},{6,2},{10,6},{14,10},{7,3},{... | collective-permute-start | bytes 1736 | tf_op jit(solution)/shard_map/ppermute | solution.py:29
  33.8 3.5 %collective-permute-start.10 = (f32[3,6,1,130]{3,2,1,0:T(1,128)S(1)}, f32[3,6,1,130]{3,2,1,0:T(1,128)S(1)}, u32[]{:S(2)}, u32[]{:S(2)}) collective-permute-start(f32[3,6,1,130]{3,2,1,0:T(1,128)S(1)} %get-tuple-element.92), channel_id=1, source_target_pairs={{0,1},{1,2},{2,3},{4,5},{5,6},{6,7},{8,9},{9,10},{10,11},{12,13},{... | collective-permute-start | bytes 28088 | tf_op jit(solution)/shard_map/ppermute | solution.py:27
  37.5 3.5 %collective-permute-start.4 = (f32[3,6,1,130]{3,2,1,0:T(1,128)S(1)}, f32[3,6,1,130]{3,2,1,0:T(1,128)S(1)}, u32[]{:S(2)}, u32[]{:S(2)}) collective-permute-start(f32[3,6,1,130]{3,2,1,0:T(1,128)S(1)} %pad_maximum_fusion.72), channel_id=1, source_target_pairs={{0,1},{1,2},{2,3},{4,5},{5,6},{6,7},{8,9},{9,10},{10,11},{12,13},{... | collective-permute-start | bytes 28088 | tf_op jit(solution)/shard_map/ppermute | solution.py:27
  42.5 4.2 %collective-permute-done.9 = f32[3,6,1,130]{3,2,1,0:T(1,128)S(1)} collective-permute-done((f32[3,6,1,130]{3,2,1,0:T(1,128)S(1)}, f32[3,6,1,130]{3,2,1,0:T(1,128)S(1)}, u32[]{:S(2)}, u32[]{:S(2)}) %collective-permute-start.9) | collective-permute-done | bytes 9392 | tf_op jit(solution)/shard_map/ppermute | solution.py:29
  49.9 3.1 %collective-permute-done.12 = f32[3,2,8,128]{3,2,1,0:T(8,128)S(1)} collective-permute-done((f32[3,2,8,128]{3,2,1,0:T(8,128)S(1)}, f32[3,2,8,128]{3,2,1,0:T(8,128)S(1)}, u32[]{:S(2)}, u32[]{:S(2)}) %collective-permute-start.12) | collective-permute-done | bytes 24608 | tf_op jit(solution)/shard_map/ppermute | solution.py:16
  54.3 4.5 %collective-permute-start.13 = (f32[3,1,8,128]{3,2,1,0:T(8,128)S(1)}, f32[3,1,8,128]{3,2,1,0:T(8,128)S(1)}, u32[]{:S(2)}, u32[]{:S(2)}) collective-permute-start(f32[3,1,8,128]{3,2,1,0:T(8,128)S(1)} %get-tuple-element.129), channel_id=1, source_target_pairs={{0,16},{1,17},{2,18},{3,19},{4,20},{5,21},{6,22},{7,23},{8,24},{9,... | collective-permute-start | bytes 36872 | tf_op jit(solution)/shard_map/ppermute | solution.py:27
  60.2 4.5 %collective-permute-start.18 = (f32[3,1,8,128]{3,2,1,0:T(8,128)S(1)}, f32[3,1,8,128]{3,2,1,0:T(8,128)S(1)}, u32[]{:S(2)}, u32[]{:S(2)}) collective-permute-start(f32[3,1,8,128]{3,2,1,0:T(8,128)S(1)} %get-tuple-element.127), channel_id=1, source_target_pairs={{0,16},{1,17},{2,18},{3,19},{4,20},{5,21},{6,22},{7,23},{8,24},{9,... | collective-permute-start | bytes 36872 | tf_op jit(solution)/shard_map/ppermute | solution.py:27
  69.5 2.4 %collective-permute-start.20 = (f32[3,6,8,1]{3,2,1,0:T(8,128)S(1)}, f32[3,6,8,1]{3,2,1,0:T(8,128)S(1)}, u32[]{:S(2)}, u32[]{:S(2)}) collective-permute-start(f32[3,6,8,1]{3,2,1,0:T(8,128)S(1)} %get-tuple-element.102), channel_id=1, source_target_pairs={{0,4},{4,8},{8,12},{1,5},{5,9},{9,13},{2,6},{6,10},{10,14},{3,7},{... | collective-permute-start | bytes 1736 | tf_op jit(solution)/shard_map/ppermute | solution.py:27
  72.0 3.2 %collective-permute-start.16 = (f32[3,6,8,1]{3,2,1,0:T(8,128)S(1)}, f32[3,6,8,1]{3,2,1,0:T(8,128)S(1)}, u32[]{:S(2)}, u32[]{:S(2)}) collective-permute-start(f32[3,6,8,1]{3,2,1,0:T(8,128)S(1)} %get-tuple-element.105), channel_id=1, source_target_pairs={{4,0},{8,4},{12,8},{5,1},{9,5},{13,9},{6,2},{10,6},{14,10},{7,3},{... | collective-permute-start | bytes 1736 | tf_op jit(solution)/shard_map/ppermute | solution.py:29
  75.2 1.9 collective-permute-start.15
  77.3 3.5 %collective-permute-start.23 = (f32[3,6,1,130]{3,2,1,0:T(1,128)S(1)}, f32[3,6,1,130]{3,2,1,0:T(1,128)S(1)}, u32[]{:S(2)}, u32[]{:S(2)}) collective-permute-start(f32[3,6,1,130]{3,2,1,0:T(1,128)S(1)} %get-tuple-element.90), channel_id=1, source_target_pairs={{0,1},{1,2},{2,3},{4,5},{5,6},{6,7},{8,9},{9,10},{10,11},{12,13},{... | collective-permute-start | bytes 28088 | tf_op jit(solution)/shard_map/ppermute | solution.py:27
  81.0 3.5 %collective-permute-start.17 = (f32[3,6,1,130]{3,2,1,0:T(1,128)S(1)}, f32[3,6,1,130]{3,2,1,0:T(1,128)S(1)}, u32[]{:S(2)}, u32[]{:S(2)}) collective-permute-start(f32[3,6,1,130]{3,2,1,0:T(1,128)S(1)} %pad_maximum_fusion.65), channel_id=1, source_target_pairs={{0,1},{1,2},{2,3},{4,5},{5,6},{6,7},{8,9},{9,10},{10,11},{12,13},{... | collective-permute-start | bytes 28088 | tf_op jit(solution)/shard_map/ppermute | solution.py:27
  86.0 4.2 %collective-permute-done.22 = f32[3,6,1,130]{3,2,1,0:T(1,128)S(1)} collective-permute-done((f32[3,6,1,130]{3,2,1,0:T(1,128)S(1)}, f32[3,6,1,130]{3,2,1,0:T(1,128)S(1)}, u32[]{:S(2)}, u32[]{:S(2)}) %collective-permute-start.22) | collective-permute-done | bytes 9392 | tf_op jit(solution)/shard_map/ppermute | solution.py:29
  93.4 3.2 %collective-permute-done.27 = f32[3,2,8,128]{3,2,1,0:T(8,128)S(1)} collective-permute-done((f32[3,2,8,128]{3,2,1,0:T(8,128)S(1)}, f32[3,2,8,128]{3,2,1,0:T(8,128)S(1)}, u32[]{:S(2)}, u32[]{:S(2)}) %collective-permute-start.27) | collective-permute-done | bytes 24608 | tf_op jit(solution)/shard_map/ppermute | solution.py:16
  97.9 4.5 %collective-permute-start.28 = (f32[3,1,8,128]{3,2,1,0:T(8,128)S(1)}, f32[3,1,8,128]{3,2,1,0:T(8,128)S(1)}, u32[]{:S(2)}, u32[]{:S(2)}) collective-permute-start(f32[3,1,8,128]{3,2,1,0:T(8,128)S(1)} %get-tuple-element.122), channel_id=1, source_target_pairs={{0,16},{1,17},{2,18},{3,19},{4,20},{5,21},{6,22},{7,23},{8,24},{9,... | collective-permute-start | bytes 36872 | tf_op jit(solution)/shard_map/ppermute | solution.py:27
  103.8 4.5 %collective-permute-start.33 = (f32[3,1,8,128]{3,2,1,0:T(8,128)S(1)}, f32[3,1,8,128]{3,2,1,0:T(8,128)S(1)}, u32[]{:S(2)}, u32[]{:S(2)}) collective-permute-start(f32[3,1,8,128]{3,2,1,0:T(8,128)S(1)} %get-tuple-element.120), channel_id=1, source_target_pairs={{0,16},{1,17},{2,18},{3,19},{4,20},{5,21},{6,22},{7,23},{8,24},{9,... | collective-permute-start | bytes 36872 | tf_op jit(solution)/shard_map/ppermute | solution.py:27
  113.1 2.4 %collective-permute-start.35 = (f32[3,6,8,1]{3,2,1,0:T(8,128)S(1)}, f32[3,6,8,1]{3,2,1,0:T(8,128)S(1)}, u32[]{:S(2)}, u32[]{:S(2)}) collective-permute-start(f32[3,6,8,1]{3,2,1,0:T(8,128)S(1)} %get-tuple-element.98), channel_id=1, source_target_pairs={{0,4},{4,8},{8,12},{1,5},{5,9},{9,13},{2,6},{6,10},{10,14},{3,7},{... | collective-permute-start | bytes 1736 | tf_op jit(solution)/shard_map/ppermute | solution.py:27
  115.7 3.2 %collective-permute-start.31 = (f32[3,6,8,1]{3,2,1,0:T(8,128)S(1)}, f32[3,6,8,1]{3,2,1,0:T(8,128)S(1)}, u32[]{:S(2)}, u32[]{:S(2)}) collective-permute-start(f32[3,6,8,1]{3,2,1,0:T(8,128)S(1)} %get-tuple-element.101), channel_id=1, source_target_pairs={{4,0},{8,4},{12,8},{5,1},{9,5},{13,9},{6,2},{10,6},{14,10},{7,3},{... | collective-permute-start | bytes 1736 | tf_op jit(solution)/shard_map/ppermute | solution.py:29
  121.0 2.0 %collective-permute-start.38 = (f32[3,6,1,130]{3,2,1,0:T(1,128)S(1)}, f32[3,6,1,130]{3,2,1,0:T(1,128)S(1)}, u32[]{:S(2)}, u32[]{:S(2)}) collective-permute-start(f32[3,6,1,130]{3,2,1,0:T(1,128)S(1)} %get-tuple-element.88), channel_id=1, source_target_pairs={{0,1},{1,2},{2,3},{4,5},{5,6},{6,7},{8,9},{9,10},{10,11},{12,13},{... | collective-permute-start | bytes 28088 | tf_op jit(solution)/shard_map/ppermute | solution.py:27
  124.6 2.0 %collective-permute-start.32 = (f32[3,6,1,130]{3,2,1,0:T(1,128)S(1)}, f32[3,6,1,130]{3,2,1,0:T(1,128)S(1)}, u32[]{:S(2)}, u32[]{:S(2)}) collective-permute-start(f32[3,6,1,130]{3,2,1,0:T(1,128)S(1)} %pad_maximum_fusion.56), channel_id=1, source_target_pairs={{0,1},{1,2},{2,3},{4,5},{5,6},{6,7},{8,9},{9,10},{10,11},{12,13},{... | collective-permute-start | bytes 28088 | tf_op jit(solution)/shard_map/ppermute | solution.py:27
  128.2 4.2 %collective-permute-done.37 = f32[3,6,1,130]{3,2,1,0:T(1,128)S(1)} collective-permute-done((f32[3,6,1,130]{3,2,1,0:T(1,128)S(1)}, f32[3,6,1,130]{3,2,1,0:T(1,128)S(1)}, u32[]{:S(2)}, u32[]{:S(2)}) %collective-permute-start.37) | collective-permute-done | bytes 9392 | tf_op jit(solution)/shard_map/ppermute | solution.py:29
  135.6 3.2 %collective-permute-done.42 = f32[3,2,8,128]{3,2,1,0:T(8,128)S(1)} collective-permute-done((f32[3,2,8,128]{3,2,1,0:T(8,128)S(1)}, f32[3,2,8,128]{3,2,1,0:T(8,128)S(1)}, u32[]{:S(2)}, u32[]{:S(2)}) %collective-permute-start.42) | collective-permute-done | bytes 24608 | tf_op jit(solution)/shard_map/ppermute | solution.py:16
  140.1 4.5 %collective-permute-start.43 = (f32[3,1,8,128]{3,2,1,0:T(8,128)S(1)}, f32[3,1,8,128]{3,2,1,0:T(8,128)S(1)}, u32[]{:S(2)}, u32[]{:S(2)}) collective-permute-start(f32[3,1,8,128]{3,2,1,0:T(8,128)S(1)} %get-tuple-element.115), channel_id=1, source_target_pairs={{0,16},{1,17},{2,18},{3,19},{4,20},{5,21},{6,22},{7,23},{8,24},{9,... | collective-permute-start | bytes 36872 | tf_op jit(solution)/shard_map/ppermute | solution.py:27
  146.0 4.5 %collective-permute-start.48 = (f32[3,1,8,128]{3,2,1,0:T(8,128)S(1)}, f32[3,1,8,128]{3,2,1,0:T(8,128)S(1)}, u32[]{:S(2)}, u32[]{:S(2)}) collective-permute-start(f32[3,1,8,128]{3,2,1,0:T(8,128)S(1)} %get-tuple-element.113), channel_id=1, source_target_pairs={{0,16},{1,17},{2,18},{3,19},{4,20},{5,21},{6,22},{7,23},{8,24},{9,... | collective-permute-start | bytes 36872 | tf_op jit(solution)/shard_map/ppermute | solution.py:27
  154.0 2.4 %collective-permute-start.50 = (f32[3,6,8,1]{3,2,1,0:T(8,128)S(1)}, f32[3,6,8,1]{3,2,1,0:T(8,128)S(1)}, u32[]{:S(2)}, u32[]{:S(2)}) collective-permute-start(f32[3,6,8,1]{3,2,1,0:T(8,128)S(1)} %get-tuple-element.94), channel_id=1, source_target_pairs={{0,4},{4,8},{8,12},{1,5},{5,9},{9,13},{2,6},{6,10},{10,14},{3,7},{... | collective-permute-start | bytes 1736 | tf_op jit(solution)/shard_map/ppermute | solution.py:27
  156.5 3.2 %collective-permute-start.46 = (f32[3,6,8,1]{3,2,1,0:T(8,128)S(1)}, f32[3,6,8,1]{3,2,1,0:T(8,128)S(1)}, u32[]{:S(2)}, u32[]{:S(2)}) collective-permute-start(f32[3,6,8,1]{3,2,1,0:T(8,128)S(1)} %get-tuple-element.97), channel_id=1, source_target_pairs={{4,0},{8,4},{12,8},{5,1},{9,5},{13,9},{6,2},{10,6},{14,10},{7,3},{... | collective-permute-start | bytes 1736 | tf_op jit(solution)/shard_map/ppermute | solution.py:29
  159.7 1.9 collective-permute-start.45
  168.8 4.2 %collective-permute-done.52 = f32[3,6,1,130]{3,2,1,0:T(1,128)S(1)} collective-permute-done((f32[3,6,1,130]{3,2,1,0:T(1,128)S(1)}, f32[3,6,1,130]{3,2,1,0:T(1,128)S(1)}, u32[]{:S(2)}, u32[]{:S(2)}) %collective-permute-start.52) | collective-permute-done | bytes 9392 | tf_op jit(solution)/shard_map/ppermute | solution.py:29
  181.4 3.8 %collective-permute-done.57 = f32[3,2,8,128]{3,2,1,0:T(8,128)S(1)} collective-permute-done((f32[3,2,8,128]{3,2,1,0:T(8,128)S(1)}, f32[3,2,8,128]{3,2,1,0:T(8,128)S(1)}, u32[]{:S(2)}, u32[]{:S(2)}) %collective-permute-start.57) | collective-permute-done | bytes 24608 | tf_op jit(solution)/shard_map/ppermute | solution.py:16
  185.8 4.3 %all-gather = f32[16,128]{1,0:T(8,128)S(1)} all-gather(f32[8,128]{1,0:T(8,128)S(1)} %fusion.56), channel_id=2, replica_groups=mesh['prop'=2,'tx'=4,'ty'=4] {'prop'}, dimensions={0}, use_global_device_ids=true | all-gather | bytes 12288 | tf_op jit(solution)/shard_map/all_gather | solution.py:38
  (221 shorter events, 71.6 us)
Async XLA Ops:
  1.5 20.5 %collective-permute-start = (f32[3,1,8,128]{3,2,1,0:T(8,128)S(1)}, f32[3,1,8,128]{3,2,1,0:T(8,128)S(1)}, u32[]{:S(2)}, u32[]{:S(2)}) collective-permute-start(f32[3,1,8,128]{3,2,1,0:T(8,128)S(1)} %get-tuple-element.139), channel_id=1, source_target_pairs={{0,16},{1,17},{2,18},{3,19},{4,20},{5,21},{6,22},{7,23},{8,24},{9,... | collective-permute-start | bytes 36872 | tf_op jit(solution)/shard_map/ppermute | solution.py:27
  5.0 18.3 %collective-permute-start.1 = (f32[3,1,8,128]{3,2,1,0:T(8,128)S(1)}, f32[3,1,8,128]{3,2,1,0:T(8,128)S(1)}, u32[]{:S(2)}, u32[]{:S(2)}) collective-permute-start(f32[3,1,8,128]{3,2,1,0:T(8,128)S(1)} %get-tuple-element.138), channel_id=1, source_target_pairs={{16,0},{17,1},{18,2},{19,3},{20,4},{21,5},{22,6},{23,7},{24,8},{25... | collective-permute-start | bytes 36872 | tf_op jit(solution)/shard_map/ppermute | solution.py:29
  6.3 19.0 %collective-permute-start.5 = (f32[3,1,8,128]{3,2,1,0:T(8,128)S(1)}, f32[3,1,8,128]{3,2,1,0:T(8,128)S(1)}, u32[]{:S(2)}, u32[]{:S(2)}) collective-permute-start(f32[3,1,8,128]{3,2,1,0:T(8,128)S(1)} %get-tuple-element.137), channel_id=1, source_target_pairs={{0,16},{1,17},{2,18},{3,19},{4,20},{5,21},{6,22},{7,23},{8,24},{9,... | collective-permute-start | bytes 36872 | tf_op jit(solution)/shard_map/ppermute | solution.py:27
  10.9 14.5 %collective-permute-start.6 = (f32[3,1,8,128]{3,2,1,0:T(8,128)S(1)}, f32[3,1,8,128]{3,2,1,0:T(8,128)S(1)}, u32[]{:S(2)}, u32[]{:S(2)}) collective-permute-start(f32[3,1,8,128]{3,2,1,0:T(8,128)S(1)} %get-tuple-element.136), channel_id=1, source_target_pairs={{16,0},{17,1},{18,2},{19,3},{20,4},{21,5},{22,6},{23,7},{24,8},{25... | collective-permute-start | bytes 36872 | tf_op jit(solution)/shard_map/ppermute | solution.py:29
  13.4 46.8 %collective-permute-start.25 = (f32[2,3,2,8,128]{4,3,2,1,0:T(8,128)S(1)}, f32[2,3,2,8,128]{4,3,2,1,0:T(8,128)S(1)}, u32[]{:S(2)}, u32[]{:S(2)}) collective-permute-start(f32[2,3,2,8,128]{4,3,2,1,0:T(8,128)S(1)} %slice.733), channel_id=1, source_target_pairs={{16,0},{17,1},{18,2},{19,3},{20,4},{21,5},{22,6},{23,7},{24,8},{25... | collective-permute-start | bytes 147464 | tf_op jit(solution)/shard_map/ppermute | solution.py:16
  21.9 42.8 %collective-permute-start.24 = (f32[2,3,2,8,128]{4,3,2,1,0:T(8,128)S(1)}, f32[2,3,2,8,128]{4,3,2,1,0:T(8,128)S(1)}, u32[]{:S(2)}, u32[]{:S(2)}) collective-permute-start(f32[2,3,2,8,128]{4,3,2,1,0:T(8,128)S(1)} %slice.732), channel_id=1, source_target_pairs={{16,0},{17,1},{18,2},{19,3},{20,4},{21,5},{22,6},{23,7},{24,8},{25... | collective-permute-start | bytes 147464 | tf_op jit(solution)/shard_map/ppermute | solution.py:16
  23.4 13.9 %collective-permute-start.3 = (f32[3,6,8,1]{3,2,1,0:T(8,128)S(1)}, f32[3,6,8,1]{3,2,1,0:T(8,128)S(1)}, u32[]{:S(2)}, u32[]{:S(2)}) collective-permute-start(f32[3,6,8,1]{3,2,1,0:T(8,128)S(1)} %get-tuple-element.109), channel_id=1, source_target_pairs={{4,0},{8,4},{12,8},{5,1},{9,5},{13,9},{6,2},{10,6},{14,10},{7,3},{... | collective-permute-start | bytes 1736 | tf_op jit(solution)/shard_map/ppermute | solution.py:29
  33.8 8.4 %collective-permute-start.10 = (f32[3,6,1,130]{3,2,1,0:T(1,128)S(1)}, f32[3,6,1,130]{3,2,1,0:T(1,128)S(1)}, u32[]{:S(2)}, u32[]{:S(2)}) collective-permute-start(f32[3,6,1,130]{3,2,1,0:T(1,128)S(1)} %get-tuple-element.92), channel_id=1, source_target_pairs={{0,1},{1,2},{2,3},{4,5},{5,6},{6,7},{8,9},{9,10},{10,11},{12,13},{... | collective-permute-start | bytes 28088 | tf_op jit(solution)/shard_map/ppermute | solution.py:27
  37.5 9.4 %collective-permute-start.4 = (f32[3,6,1,130]{3,2,1,0:T(1,128)S(1)}, f32[3,6,1,130]{3,2,1,0:T(1,128)S(1)}, u32[]{:S(2)}, u32[]{:S(2)}) collective-permute-start(f32[3,6,1,130]{3,2,1,0:T(1,128)S(1)} %pad_maximum_fusion.72), channel_id=1, source_target_pairs={{0,1},{1,2},{2,3},{4,5},{5,6},{6,7},{8,9},{9,10},{10,11},{12,13},{... | collective-permute-start | bytes 28088 | tf_op jit(solution)/shard_map/ppermute | solution.py:27
  48.6 10.2 %collective-permute-start.11 = (f32[3,2,8,128]{3,2,1,0:T(8,128)S(1)}, f32[3,2,8,128]{3,2,1,0:T(8,128)S(1)}, u32[]{:S(2)}, u32[]{:S(2)}) collective-permute-start(f32[3,2,8,128]{3,2,1,0:T(8,128)S(1)} %slice.703), channel_id=1, source_target_pairs={{16,0},{17,1},{18,2},{19,3},{20,4},{21,5},{22,6},{23,7},{24,8},{25... | collective-permute-start | bytes 73736 | tf_op jit(solution)/shard_map/ppermute | solution.py:16
  53.0 16.5 %collective-permute-start.14 = (f32[3,1,8,128]{3,2,1,0:T(8,128)S(1)}, f32[3,1,8,128]{3,2,1,0:T(8,128)S(1)}, u32[]{:S(2)}, u32[]{:S(2)}) collective-permute-start(f32[3,1,8,128]{3,2,1,0:T(8,128)S(1)} %get-tuple-element.130), channel_id=1, source_target_pairs={{16,0},{17,1},{18,2},{19,3},{20,4},{21,5},{22,6},{23,7},{24,8},{25... | collective-permute-start | bytes 36872 | tf_op jit(solution)/shard_map/ppermute | solution.py:29
  54.3 17.7 %collective-permute-start.13 = (f32[3,1,8,128]{3,2,1,0:T(8,128)S(1)}, f32[3,1,8,128]{3,2,1,0:T(8,128)S(1)}, u32[]{:S(2)}, u32[]{:S(2)}) collective-permute-start(f32[3,1,8,128]{3,2,1,0:T(8,128)S(1)} %get-tuple-element.129), channel_id=1, source_target_pairs={{0,16},{1,17},{2,18},{3,19},{4,20},{5,21},{6,22},{7,23},{8,24},{9,... | collective-permute-start | bytes 36872 | tf_op jit(solution)/shard_map/ppermute | solution.py:27
  64.8 39.0 %collective-permute-start.40 = (f32[2,3,2,8,128]{4,3,2,1,0:T(8,128)S(1)}, f32[2,3,2,8,128]{4,3,2,1,0:T(8,128)S(1)}, u32[]{:S(2)}, u32[]{:S(2)}) collective-permute-start(f32[2,3,2,8,128]{4,3,2,1,0:T(8,128)S(1)} %slice.766), channel_id=1, source_target_pairs={{16,0},{17,1},{18,2},{19,3},{20,4},{21,5},{22,6},{23,7},{24,8},{25... | collective-permute-start | bytes 147464 | tf_op jit(solution)/shard_map/ppermute | solution.py:16
  66.2 42.2 %collective-permute-start.39 = (f32[2,3,2,8,128]{4,3,2,1,0:T(8,128)S(1)}, f32[2,3,2,8,128]{4,3,2,1,0:T(8,128)S(1)}, u32[]{:S(2)}, u32[]{:S(2)}) collective-permute-start(f32[2,3,2,8,128]{4,3,2,1,0:T(8,128)S(1)} %slice.765), channel_id=1, source_target_pairs={{16,0},{17,1},{18,2},{19,3},{20,4},{21,5},{22,6},{23,7},{24,8},{25... | collective-permute-start | bytes 147464 | tf_op jit(solution)/shard_map/ppermute | solution.py:16
  69.5 7.6 %collective-permute-start.20 = (f32[3,6,8,1]{3,2,1,0:T(8,128)S(1)}, f32[3,6,8,1]{3,2,1,0:T(8,128)S(1)}, u32[]{:S(2)}, u32[]{:S(2)}) collective-permute-start(f32[3,6,8,1]{3,2,1,0:T(8,128)S(1)} %get-tuple-element.102), channel_id=1, source_target_pairs={{0,4},{4,8},{8,12},{1,5},{5,9},{9,13},{2,6},{6,10},{10,14},{3,7},{... | collective-permute-start | bytes 1736 | tf_op jit(solution)/shard_map/ppermute | solution.py:27
  72.0 8.8 %collective-permute-start.16 = (f32[3,6,8,1]{3,2,1,0:T(8,128)S(1)}, f32[3,6,8,1]{3,2,1,0:T(8,128)S(1)}, u32[]{:S(2)}, u32[]{:S(2)}) collective-permute-start(f32[3,6,8,1]{3,2,1,0:T(8,128)S(1)} %get-tuple-element.105), channel_id=1, source_target_pairs={{4,0},{8,4},{12,8},{5,1},{9,5},{13,9},{6,2},{10,6},{14,10},{7,3},{... | collective-permute-start | bytes 1736 | tf_op jit(solution)/shard_map/ppermute | solution.py:29
  77.3 8.5 %collective-permute-start.23 = (f32[3,6,1,130]{3,2,1,0:T(1,128)S(1)}, f32[3,6,1,130]{3,2,1,0:T(1,128)S(1)}, u32[]{:S(2)}, u32[]{:S(2)}) collective-permute-start(f32[3,6,1,130]{3,2,1,0:T(1,128)S(1)} %get-tuple-element.90), channel_id=1, source_target_pairs={{0,1},{1,2},{2,3},{4,5},{5,6},{6,7},{8,9},{9,10},{10,11},{12,13},{... | collective-permute-start | bytes 28088 | tf_op jit(solution)/shard_map/ppermute | solution.py:27
  81.0 9.4 %collective-permute-start.17 = (f32[3,6,1,130]{3,2,1,0:T(1,128)S(1)}, f32[3,6,1,130]{3,2,1,0:T(1,128)S(1)}, u32[]{:S(2)}, u32[]{:S(2)}) collective-permute-start(f32[3,6,1,130]{3,2,1,0:T(1,128)S(1)} %pad_maximum_fusion.65), channel_id=1, source_target_pairs={{0,1},{1,2},{2,3},{4,5},{5,6},{6,7},{8,9},{9,10},{10,11},{12,13},{... | collective-permute-start | bytes 28088 | tf_op jit(solution)/shard_map/ppermute | solution.py:27
  92.1 10.4 %collective-permute-start.26 = (f32[3,2,8,128]{3,2,1,0:T(8,128)S(1)}, f32[3,2,8,128]{3,2,1,0:T(8,128)S(1)}, u32[]{:S(2)}, u32[]{:S(2)}) collective-permute-start(f32[3,2,8,128]{3,2,1,0:T(8,128)S(1)} %slice.736), channel_id=1, source_target_pairs={{16,0},{17,1},{18,2},{19,3},{20,4},{21,5},{22,6},{23,7},{24,8},{25... | collective-permute-start | bytes 73736 | tf_op jit(solution)/shard_map/ppermute | solution.py:16
  96.6 16.5 %collective-permute-start.29 = (f32[3,1,8,128]{3,2,1,0:T(8,128)S(1)}, f32[3,1,8,128]{3,2,1,0:T(8,128)S(1)}, u32[]{:S(2)}, u32[]{:S(2)}) collective-permute-start(f32[3,1,8,128]{3,2,1,0:T(8,128)S(1)} %get-tuple-element.123), channel_id=1, source_target_pairs={{16,0},{17,1},{18,2},{19,3},{20,4},{21,5},{22,6},{23,7},{24,8},{25... | collective-permute-start | bytes 36872 | tf_op jit(solution)/shard_map/ppermute | solution.py:29
  97.9 17.7 %collective-permute-start.28 = (f32[3,1,8,128]{3,2,1,0:T(8,128)S(1)}, f32[3,1,8,128]{3,2,1,0:T(8,128)S(1)}, u32[]{:S(2)}, u32[]{:S(2)}) collective-permute-start(f32[3,1,8,128]{3,2,1,0:T(8,128)S(1)} %get-tuple-element.122), channel_id=1, source_target_pairs={{0,16},{1,17},{2,18},{3,19},{4,20},{5,21},{6,22},{7,23},{8,24},{9,... | collective-permute-start | bytes 36872 | tf_op jit(solution)/shard_map/ppermute | solution.py:27
  108.5 37.5 %collective-permute-start.55 = (f32[2,3,2,8,128]{4,3,2,1,0:T(8,128)S(1)}, f32[2,3,2,8,128]{4,3,2,1,0:T(8,128)S(1)}, u32[]{:S(2)}, u32[]{:S(2)}) collective-permute-start(f32[2,3,2,8,128]{4,3,2,1,0:T(8,128)S(1)} %slice.799), channel_id=1, source_target_pairs={{16,0},{17,1},{18,2},{19,3},{20,4},{21,5},{22,6},{23,7},{24,8},{25... | collective-permute-start | bytes 147464 | tf_op jit(solution)/shard_map/ppermute | solution.py:16
  109.8 40.8 %collective-permute-start.54 = (f32[2,3,2,8,128]{4,3,2,1,0:T(8,128)S(1)}, f32[2,3,2,8,128]{4,3,2,1,0:T(8,128)S(1)}, u32[]{:S(2)}, u32[]{:S(2)}) collective-permute-start(f32[2,3,2,8,128]{4,3,2,1,0:T(8,128)S(1)} %slice.798), channel_id=1, source_target_pairs={{16,0},{17,1},{18,2},{19,3},{20,4},{21,5},{22,6},{23,7},{24,8},{25... | collective-permute-start | bytes 147464 | tf_op jit(solution)/shard_map/ppermute | solution.py:16
  124.6 7.9 %collective-permute-start.32 = (f32[3,6,1,130]{3,2,1,0:T(1,128)S(1)}, f32[3,6,1,130]{3,2,1,0:T(1,128)S(1)}, u32[]{:S(2)}, u32[]{:S(2)}) collective-permute-start(f32[3,6,1,130]{3,2,1,0:T(1,128)S(1)} %pad_maximum_fusion.56), channel_id=1, source_target_pairs={{0,1},{1,2},{2,3},{4,5},{5,6},{6,7},{8,9},{9,10},{10,11},{12,13},{... | collective-permute-start | bytes 28088 | tf_op jit(solution)/shard_map/ppermute | solution.py:27
  134.3 10.4 %collective-permute-start.41 = (f32[3,2,8,128]{3,2,1,0:T(8,128)S(1)}, f32[3,2,8,128]{3,2,1,0:T(8,128)S(1)}, u32[]{:S(2)}, u32[]{:S(2)}) collective-permute-start(f32[3,2,8,128]{3,2,1,0:T(8,128)S(1)} %slice.769), channel_id=1, source_target_pairs={{16,0},{17,1},{18,2},{19,3},{20,4},{21,5},{22,6},{23,7},{24,8},{25... | collective-permute-start | bytes 73736 | tf_op jit(solution)/shard_map/ppermute | solution.py:16
  138.8 17.6 %collective-permute-start.44 = (f32[3,1,8,128]{3,2,1,0:T(8,128)S(1)}, f32[3,1,8,128]{3,2,1,0:T(8,128)S(1)}, u32[]{:S(2)}, u32[]{:S(2)}) collective-permute-start(f32[3,1,8,128]{3,2,1,0:T(8,128)S(1)} %get-tuple-element.116), channel_id=1, source_target_pairs={{16,0},{17,1},{18,2},{19,3},{20,4},{21,5},{22,6},{23,7},{24,8},{25... | collective-permute-start | bytes 36872 | tf_op jit(solution)/shard_map/ppermute | solution.py:29
  140.1 16.3 %collective-permute-start.43 = (f32[3,1,8,128]{3,2,1,0:T(8,128)S(1)}, f32[3,1,8,128]{3,2,1,0:T(8,128)S(1)}, u32[]{:S(2)}, u32[]{:S(2)}) collective-permute-start(f32[3,1,8,128]{3,2,1,0:T(8,128)S(1)} %get-tuple-element.115), channel_id=1, source_target_pairs={{0,16},{1,17},{2,18},{3,19},{4,20},{5,21},{6,22},{7,23},{8,24},{9,... | collective-permute-start | bytes 36872 | tf_op jit(solution)/shard_map/ppermute | solution.py:27
  152.0 9.6 %collective-permute-start.51 = (f32[3,6,8,1]{3,2,1,0:T(8,128)S(1)}, f32[3,6,8,1]{3,2,1,0:T(8,128)S(1)}, u32[]{:S(2)}, u32[]{:S(2)}) collective-permute-start(f32[3,6,8,1]{3,2,1,0:T(8,128)S(1)} %get-tuple-element.95), channel_id=1, source_target_pairs={{4,0},{8,4},{12,8},{5,1},{9,5},{13,9},{6,2},{10,6},{14,10},{7,3},{... | collective-permute-start | bytes 1736 | tf_op jit(solution)/shard_map/ppermute | solution.py:29
  154.0 7.6 %collective-permute-start.50 = (f32[3,6,8,1]{3,2,1,0:T(8,128)S(1)}, f32[3,6,8,1]{3,2,1,0:T(8,128)S(1)}, u32[]{:S(2)}, u32[]{:S(2)}) collective-permute-start(f32[3,6,8,1]{3,2,1,0:T(8,128)S(1)} %get-tuple-element.94), channel_id=1, source_target_pairs={{0,4},{4,8},{8,12},{1,5},{5,9},{9,13},{2,6},{6,10},{10,14},{3,7},{... | collective-permute-start | bytes 1736 | tf_op jit(solution)/shard_map/ppermute | solution.py:27
  165.5 7.7 %collective-permute-start.47 = (f32[3,6,1,130]{3,2,1,0:T(1,128)S(1)}, f32[3,6,1,130]{3,2,1,0:T(1,128)S(1)}, u32[]{:S(2)}, u32[]{:S(2)}) collective-permute-start(f32[3,6,1,130]{3,2,1,0:T(1,128)S(1)} %pad_maximum_fusion.47), channel_id=1, source_target_pairs={{0,1},{1,2},{2,3},{4,5},{5,6},{6,7},{8,9},{9,10},{10,11},{12,13},{... | collective-permute-start | bytes 28088 | tf_op jit(solution)/shard_map/ppermute | solution.py:27
  176.8 14.0 %collective-permute-start.58 = (f32[2,3,2,8,128]{4,3,2,1,0:T(8,128)S(1)}, f32[2,3,2,8,128]{4,3,2,1,0:T(8,128)S(1)}, u32[]{:S(2)}, u32[]{:S(2)}) collective-permute-start(f32[2,3,2,8,128]{4,3,2,1,0:T(8,128)S(1)} %slice.804), channel_id=1, source_target_pairs={{16,0},{17,1},{18,2},{19,3},{20,4},{21,5},{22,6},{23,7},{24,8},{25... | collective-permute-start | bytes 147464 | tf_op jit(solution)/shard_map/ppermute | solution.py:16
  178.1 13.3 %collective-permute-start.59 = (f32[2,3,2,8,128]{4,3,2,1,0:T(8,128)S(1)}, f32[2,3,2,8,128]{4,3,2,1,0:T(8,128)S(1)}, u32[]{:S(2)}, u32[]{:S(2)}) collective-permute-start(f32[2,3,2,8,128]{4,3,2,1,0:T(8,128)S(1)} %slice.805), channel_id=1, source_target_pairs={{16,0},{17,1},{18,2},{19,3},{20,4},{21,5},{22,6},{23,7},{24,8},{25... | collective-permute-start | bytes 147464 | tf_op jit(solution)/shard_map/ppermute | solution.py:16
  (38 other events, 269.5 us)
where the time goes:
time: 194 us; the launch traced here: 192 us
  starting transfers between devices  130 us (67%)
  waiting for transfers between devices  36.3 us (19%)
  between operations  10 us (5%)
  other arithmetic  8.89 us (5%)
  blocking collectives  4.33 us (2%)
  local copies, waits for them, and re-layouts  3.05 us (2%)
    ppermute x24, starting transfers between devices, extended_2(): lax.ppermute(tail, axis, [(i, (i + 1) % count) for i in range(ends)])  73.7 us
    ppermute x20, starting transfers between devices, extended_2(): lax.ppermute(head, axis, [((i + 1) % count, i) for i in range(ends)])  35.2 us
    ppermute x16, starting transfers between devices, passed_along(): lax.ppermute(value, axis, [(source, source + steps) for source in range(f...  20.6 us
    ppermute x20, waiting for transfers between devices, extended_2(): lax.ppermute(head, axis, [((i + 1) % count, i) for i in range(ends)])  16.7 us
    ppermute x16, waiting for transfers between devices, passed_along(): lax.ppermute(value, axis, [(source, source + steps) for source in range(f...  13.2 us
    ppermute x24, waiting for transfers between devices, extended_2(): lax.ppermute(tail, axis, [(i, (i + 1) % count) for i in range(ends)])  6.39 us
    all_gather x1, blocking collectives, entering(): pieces = lax.all_gather(value, axis)  4.33 us
  transfers between devices with their start and end apart: 60, of which 12 were waited for; matrix products, arithmetic and copies ran while one was open for 5% of the time, Pallas kernels for 0%

commit v1 on v0

v1 whole, which is shorter than its diff:
```python
import jax
import jax.numpy as jnp
from jax import lax
from jax.sharding import PartitionSpec as P

STEPS = 4
WSHIFT = 2


time_step = 0.5


def from_offsets(value, axis, offsets):
    count, mine = (lax.axis_size(axis), lax.axis_index(axis))
    got = {}
    for k in offsets:
        if k in got:
            continue
        pairs = [(s, s - k) for s in range(count) if 0 <= s - k < count]
        if not pairs:
            got[k] = jnp.zeros_like(value)
            continue
        if -k in offsets and 2 * abs(k) >= count:
            pairs = pairs + [(s, s + k) for s in range(count) if 0 <= s + k < count]
            received = lax.ppermute(value, axis, pairs)
            for j in (k, -k):
                inside = jnp.logical_and(mine + j >= 0, mine + j < count)
                got[j] = jnp.where(inside, received, jnp.zeros_like(received))
            continue
        got[k] = lax.ppermute(value, axis, pairs)
    return got


def with_halo(cells, axis, dim, width):
    length = cells.shape[dim]
    head = lax.slice_in_dim(cells, 0, width, axis=dim)
    tail = lax.slice_in_dim(cells, length - width, length, axis=dim)
    below = from_offsets(tail, axis, (-1,))[-1]
    above = from_offsets(head, axis, (1,))[1]
    return jnp.concatenate([below, cells, above], axis=dim)


def upper_next(values, dimension):
    zeros_plane = jnp.zeros_like(lax.slice_in_dim(values, 0, 1, axis=dimension))
    rest = lax.slice_in_dim(values, 1, values.shape[dimension], axis=dimension)
    return jnp.concatenate([rest, zeros_plane], axis=dimension)


def lower_next(values, dimension):
    zeros_plane = jnp.zeros_like(lax.slice_in_dim(values, 0, 1, axis=dimension))
    rest = lax.slice_in_dim(values, 0, values.shape[dimension] - 1, axis=dimension)
    return jnp.concatenate([zeros_plane, rest], axis=dimension)


def forward_diff(values, dimension):
    return upper_next(values, dimension) - values


def backward_diff(values, dimension):
    return values - lower_next(values, dimension)


def curl_forward(field):
    field_x, field_y, field_z = field[0], field[1], field[2]
    return jnp.stack([forward_diff(field_z, 1) - forward_diff(field_y, 0),
                      forward_diff(field_x, 0) - forward_diff(field_z, 2),
                      forward_diff(field_y, 2) - forward_diff(field_x, 1)])


def curl_backward(field):
    field_x, field_y, field_z = field[0], field[1], field[2]
    return jnp.stack([backward_diff(field_z, 1) - backward_diff(field_y, 0),
                      backward_diff(field_x, 0) - backward_diff(field_z, 2),
                      backward_diff(field_y, 2) - backward_diff(field_x, 1)])


def advance_planes(values, amount, dimension):
    shape_pad = list(values.shape)
    shape_pad[dimension] = WSHIFT
    joined = jnp.concatenate([values, jnp.zeros(shape_pad, values.dtype)], axis=dimension)
    return lax.dynamic_slice_in_dim(joined, amount, values.shape[dimension], axis=dimension)


def cell_lookup(selector, table):
    return jnp.sum(jnp.where(selector, table[:, None, None], jnp.float32(0.0)), axis=0)


def inside_range(start, length, total, dimension, total_dims):
    shape_one = [1] * total_dims
    shape_one[dimension] = length
    marks = start + lax.broadcasted_iota(jnp.int32, tuple(shape_one), dimension)
    return jnp.logical_and(marks >= 0, marks < total)


def entering(value, axis):
    count, mine = (lax.axis_size(axis), lax.axis_index(axis))
    pieces = lax.all_gather(value, axis)
    running = jnp.zeros_like(value)
    for position in range(count - 1):
        running = jnp.where(position < mine, running + pieces[position], running)
    return running


def body(
    electric,
    magnetic,
    polarization,
    current,
    material,
    advance,
    permittivity,
    nonlinear,
    pole_strength,
    pole_frequency,
    pole_damping,
):
    planes, rows, columns = (electric.shape[1], electric.shape[2], electric.shape[3])
    n_prop, n_tx, n_ty = (lax.axis_size("prop"), lax.axis_size("tx"), lax.axis_size("ty"))
    total_z, total_y, total_x = (planes * n_prop, rows * n_ty, columns * n_tx)
    at_z, at_y, at_x = (lax.axis_index("prop"), lax.axis_index("ty"), lax.axis_index("tx"))
    halo = STEPS
    assert halo <= rows and halo <= columns

    state = jnp.concatenate(
        [
            electric,
            magnetic,
            polarization.reshape((-1,) + electric.shape[1:]),
            current.reshape((-1,) + electric.shape[1:]),
        ],
        axis=0,
    )

    below = -(-STEPS // planes)
    above = -(-(STEPS + STEPS * WSHIFT) // planes)
    whole_column = (below + above + 1) * planes >= total_z
    if whole_column:
        offsets = [k for k in range(-(n_prop - 1), n_prop) if k != 0]
        pieces = from_offsets(state, "prop", offsets)
        pieces[0] = state
        blocks = []
        for j in range(n_prop):
            block = jnp.zeros_like(state)
            for k, piece in pieces.items():
                block = jnp.where(at_z + k == j, piece, block)
            blocks.append(block)
        state = jnp.concatenate(blocks, axis=1)
        base_z = jnp.int32(0)
        own_z = at_z * planes
    else:
        offsets = [k for k in range(-below, above + 1) if k != 0]
        pieces = from_offsets(state, "prop", offsets)
        pieces[0] = state
        state = jnp.concatenate([pieces[k] for k in range(-below, above + 1)], axis=1)
        base_z = (at_z - below) * planes
        own_z = below * planes
    depth = state.shape[1]

    kinds = material.astype(jnp.float32)
    state = jnp.concatenate([state, jnp.broadcast_to(kinds[None, None], (1, depth, rows, columns))], axis=0)
    state = with_halo(state, "tx", 3, halo)
    state = with_halo(state, "ty", 2, halo)
    kinds = state[-1, 0].astype(jnp.int32)
    electric_b, magnetic_b = (state[0:3], state[3:6])
    polarization_b = state[6:12].reshape((2, 3) + state.shape[1:])
    current_b = state[12:18].reshape((2, 3) + state.shape[1:])

    ext_rows, ext_columns = (rows + 2 * halo, columns + 2 * halo)
    keep_mask = (
        inside_range(base_z, depth, total_z, 0, 3)
        & inside_range(at_y * rows - halo, ext_rows, total_y, 1, 3)
        & inside_range(at_x * columns - halo, ext_columns, total_x, 2, 3)
    ).astype(jnp.float32)

    materials_count = permittivity.shape[0]
    selector = kinds[None] == lax.broadcasted_iota(
        jnp.int32, (materials_count, ext_rows, ext_columns), 0
    )
    eps_cell = cell_lookup(selector, permittivity)
    kerr_cell = cell_lookup(selector, nonlinear)
    strength = jnp.stack(
        [cell_lookup(selector, pole_strength[0]), cell_lookup(selector, pole_strength[1])]
    )[:, None, None]
    frequency = jnp.stack(
        [cell_lookup(selector, pole_frequency[0]), cell_lookup(selector, pole_frequency[1])]
    )
    damping = jnp.stack(
        [cell_lookup(selector, pole_damping[0]), cell_lookup(selector, pole_damping[1])]
    )
    half_damp = 0.5 * time_step * damping
    keep_rate = ((1.0 - half_damp) / (1.0 + half_damp))[:, None, None]
    drive_rate = (time_step * frequency * frequency / (1.0 + half_damp))[:, None, None]

    for moment in range(STEPS):
        magnetic_b = (magnetic_b - time_step * curl_forward(electric_b)) * keep_mask[None]
        squared = jnp.sum(electric_b * electric_b, axis=0)
        current_b = keep_rate * current_b + drive_rate * (strength * electric_b[None] - polarization_b)
        polarization_b = polarization_b + time_step * current_b
        electric_b = electric_b + time_step * (
            curl_backward(magnetic_b) - current_b[0] - current_b[1]
        ) / (eps_cell + kerr_cell * squared)
        electric_b = electric_b * keep_mask[None]
        amount = advance[moment]
        electric_b = advance_planes(electric_b, amount, 1)
        magnetic_b = advance_planes(magnetic_b, amount, 1)
        polarization_b = advance_planes(polarization_b, amount, 2)
        current_b = advance_planes(current_b, amount, 2)

    def own(values, dim):
        values = lax.dynamic_slice_in_dim(values, own_z, planes, axis=dim)
        values = lax.slice_in_dim(values, halo, halo + rows, axis=dim + 1)
        return lax.slice_in_dim(values, halo, halo + columns, axis=dim + 2)

    density = eps_cell * jnp.sum(electric_b * electric_b, axis=0) + jnp.sum(
        magnetic_b * magnetic_b, axis=0
    )
    if whole_column:
        column_energy = own(jnp.cumsum(density, axis=0), 0) / jnp.float32(total_z)
    else:
        density = own(density, 0)
        prefix = entering(jnp.sum(density, axis=0), "prop")
        column_energy = (prefix[None] + jnp.cumsum(density, axis=0)) / jnp.float32(total_z)
    return (own(electric_b, 1), own(magnetic_b, 1), own(polarization_b, 2), own(current_b, 2), column_energy)


def solution(mesh):
    return jax.shard_map(
        body,
        mesh=mesh,
        in_specs=(
            P(None, "prop", "ty", "tx"),
            P(None, "prop", "ty", "tx"),
            P(None, None, "prop", "ty", "tx"),
            P(None, None, "prop", "ty", "tx"),
            P("ty", "tx"),
            P(),
            P(),
            P(),
            P(),
            P(),
            P(),
        ),
        out_specs=(
            P(None, "prop", "ty", "tx"),
            P(None, "prop", "ty", "tx"),
            P(None, None, "prop", "ty", "tx"),
            P(None, None, "prop", "ty", "tx"),
            P("prop", "ty", "tx"),
        ),
        check_vma=False,
    )
```

time: 194 us -> 60.4 us (0.31)
  the two profiles are of different devices: /device:TPU:4 before, /device:TPU:1 now
where the time goes in v1:
time: 60.4 us; the launch traced here: 59.9 us
  waiting for transfers between devices  18.3 us (30%)
  starting transfers between devices  13.1 us (22%)
  other arithmetic  10.3 us (17%)
  local copies, waits for them, and re-layouts  9.24 us (15%)
  between operations  9.04 us (15%)
    ppermute x4, waiting for transfers between devices, from_offsets(): got[k] = lax.ppermute(value, axis, pairs)  14.6 us
    ppermute x4, starting transfers between devices, from_offsets(): got[k] = lax.ppermute(value, axis, pairs)  11 us
    ppermute x1, waiting for transfers between devices, from_offsets(): received = lax.ppermute(value, axis, pairs)  3.68 us
    broadcast_in_dim x3, local copies, waits for them, and re-layouts, cell_lookup(): jnp.where(selector, table[:, None, None], jnp.float32(0.0))  2.27 us
    ppermute x1, starting transfers between devices, from_offsets(): received = lax.ppermute(value, axis, pairs)  2.11 us
    concatenate x2, other arithmetic, with_halo(): return jnp.concatenate([below, cells, above], axis=dim)  1.78 us
    slice x2, local copies, waits for them, and re-layouts, own(): return lax.slice_in_dim(values, halo, halo + columns, axis=dim + 2)  1.58 us
    ppermute x2, local copies, waits for them, and re-layouts, from_offsets(): got[k] = lax.ppermute(value, axis, pairs)  1.44 us
  transfers between devices with their start and end apart: 5, of which 3 were waited for; matrix products, arithmetic and copies ran while one was open for 8% of the time, Pallas kernels for 0%

profile of v1, /device:TPU:1, one launch (start us, length us, event | category | flops | bytes accessed | tf_op | source)
XLA Modules:
  0.0 59.9 jit_solution(13958646559191582439)
XLA Ops:
  0.6 1.0 %pad_maximum_fusion.3 = f32[18,4,8,128]{3,2,1,0:T(8,128)S(1)} fusion(f32[6,4,8,128]{3,2,1,0:T(8,128)} %bitcast.324, f32[6,4,8,128]{3,2,1,0:T(8,128)} %bitcast.326, f32[3,4,8,128]{3,2,1,0:T(8,128)} %param.12, f32[3,4,8,128]{3,2,1,0:T(8,128)} %param.11), kind=kLoop, calls=%fused_computation.99 | loop fusion | flops 221184 | bytes 589824 | tf_op jit(solution)/shard_map/concatenate | solution.py:124
  1.6 2.1 %collective-permute-start = (f32[18,4,8,128]{3,2,1,0:T(8,128)S(1)}, f32[18,4,8,128]{3,2,1,0:T(8,128)S(1)}, u32[]{:S(2)}, u32[]{:S(2)}) collective-permute-start(f32[18,4,8,128]{3,2,1,0:T(8,128)S(1)} %pad_maximum_fusion.3), channel_id=1, source_target_pairs={{0,16},{16,0},{1,17},{17,1},{2,18},{18,2},{3,19},{19,3},{4,20},{20... | collective-permute-start | bytes 884744 | tf_op jit(solution)/shard_map/ppermute | solution.py:25
  3.7 0.7 %convert_element_type.20 = f32[8,128]{1,0:T(8,128)S(1)} convert(s32[8,128]{1,0:T(8,128)} %param.15) | non-fusion elementwise | flops 1024 | bytes 8192 | tf_op jit(solution)/shard_map/convert_element_type | solution.py:159
  4.4 0.8 %slice_bitcast_fusion.33 = (f32[8]{0:T(128)S(1)}, f32[8]{0:T(128)S(1)}) fusion(f32[2,8]{1,0:T(2,128)} %param.21), kind=kLoop, calls=%fused_computation.200 | loop fusion | bytes 128 | tf_op jit(solution)/shard_map/jit(_where)/broadcast_in_dim | solution.py:85
  5.2 0.8 %slice_bitcast_fusion.31 = (f32[8]{0:T(128)S(1)}, f32[8]{0:T(128)S(1)}) fusion(f32[2,8]{1,0:T(2,128)} %param.20), kind=kLoop, calls=%fused_computation.198 | loop fusion | bytes 128 | tf_op jit(solution)/shard_map/jit(_where)/broadcast_in_dim | solution.py:85
  5.9 0.8 %slice_bitcast_fusion.29 = (f32[8]{0:T(128)S(1)}, f32[8]{0:T(128)S(1)}) fusion(f32[2,8]{1,0:T(2,128)} %param.19), kind=kLoop, calls=%fused_computation.196 | loop fusion | bytes 128 | tf_op jit(solution)/shard_map/jit(_where)/broadcast_in_dim | solution.py:85
  6.8 3.7 %collective-permute-done = f32[18,4,8,128]{3,2,1,0:T(8,128)S(1)} collective-permute-done((f32[18,4,8,128]{3,2,1,0:T(8,128)S(1)}, f32[18,4,8,128]{3,2,1,0:T(8,128)S(1)}, u32[]{:S(2)}, u32[]{:S(2)}) %collective-permute-start) | collective-permute-done | bytes 294944 | tf_op jit(solution)/shard_map/ppermute | solution.py:25
  10.4 1.0 %select_select_fusion.1 = (f32[18,4,8,128]{3,2,1,0:T(8,128)S(1)}, f32[18,4,8,128]{3,2,1,0:T(8,128)S(1)}) fusion(f32[18,4,8,128]{3,2,1,0:T(8,128)S(1)} %collective-permute-done, pred[]{:T(512)S(6)} %and.62, pred[]{:T(512)S(6)} %eq.28, pred[]{:T(512)S(6)} %and.61, pred[]{:T(512)S(6)} %eq.27, pred[]{:T(512)S(6)} %eq.26, f32[6,4,8,128]{3,2,1,0:T(8,128)} %bitcast.325, ...), kind=kLoop, calls=%fused_computation.101 | loop fusion | flops 811008 | bytes 1179656 | tf_op jit(solution)/shard_map/jit(_where)/select_n | solution.py:145
  11.5 0.2 fusion.73
  11.8 0.5 copy.43
  12.3 4.5 %collective-permute-start.1 = (f32[19,8,8,4]{0,2,3,1:T(8,128)S(1)}, f32[19,8,8,4]{0,2,3,1:T(8,128)S(1)}, u32[]{:S(2)}, u32[]{:S(2)}) collective-permute-start(f32[19,8,8,4]{0,2,3,1:T(8,128)S(1)} %copy.43), channel_id=1, source_target_pairs={{0,4},{4,8},{8,12},{1,5},{5,9},{9,13},{2,6},{6,10},{10,14},{3,7},{... | collective-permute-start | bytes 58376 | tf_op jit(solution)/shard_map/ppermute | solution.py:30
  16.8 0.5 copy.44
  17.4 1.9 %collective-permute-start.2 = (f32[19,8,8,4]{0,2,3,1:T(8,128)S(1)}, f32[19,8,8,4]{0,2,3,1:T(8,128)S(1)}, u32[]{:S(2)}, u32[]{:S(2)}) collective-permute-start(f32[19,8,8,4]{0,2,3,1:T(8,128)S(1)} %copy.44), channel_id=1, source_target_pairs={{4,0},{8,4},{12,8},{5,1},{9,5},{13,9},{6,2},{10,6},{14,10},{7,3},{... | collective-permute-start | bytes 58376 | tf_op jit(solution)/shard_map/ppermute | solution.py:30
  19.3 0.6 fusion.74
  27.7 0.7 %copy.45 = f32[19,8,8,4]{3,2,1,0:T(8,128)S(1)} copy(f32[19,8,8,4]{0,2,3,1:T(8,128)S(1)} %collective-permute-done.1) | data formatting | bytes 38912 | tf_op jit(solution)/shard_map/ppermute | solution.py:30
  28.4 0.7 %copy.46 = f32[19,8,8,4]{3,2,1,0:T(8,128)S(1)} copy(f32[19,8,8,4]{0,2,3,1:T(8,128)S(1)} %collective-permute-done.2) | data formatting | bytes 38912 | tf_op jit(solution)/shard_map/ppermute | solution.py:30
  29.2 0.6 pad_maximum_fusion.1
  29.7 0.3 fusion.72
  30.0 3.2 %collective-permute-start.3 = (f32[19,8,4,136]{3,2,1,0:T(4,128)S(1)}, f32[19,8,4,136]{3,2,1,0:T(4,128)S(1)}, u32[]{:S(2)}, u32[]{:S(2)}) collective-permute-start(f32[19,8,4,136]{3,2,1,0:T(4,128)S(1)} %get-tuple-element.57), channel_id=1, source_target_pairs={{0,1},{1,2},{2,3},{4,5},{5,6},{6,7},{8,9},{9,10},{10,11},{12,13},{... | collective-permute-start | bytes 992264 | tf_op jit(solution)/shard_map/ppermute | solution.py:30
  33.3 1.3 %collective-permute-start.4 = (f32[19,8,4,136]{3,2,1,0:T(4,128)S(1)}, f32[19,8,4,136]{3,2,1,0:T(4,128)S(1)}, u32[]{:S(2)}, u32[]{:S(2)}) collective-permute-start(f32[19,8,4,136]{3,2,1,0:T(4,128)S(1)} %get-tuple-element.58), channel_id=1, source_target_pairs={{1,0},{2,1},{3,2},{5,4},{6,5},{7,6},{9,8},{10,9},{11,10},{13,12},{... | collective-permute-start | bytes 992264 | tf_op jit(solution)/shard_map/ppermute | solution.py:30
  34.7 10.5 %collective-permute-done.3 = f32[19,8,4,136]{3,2,1,0:T(4,128)S(1)} collective-permute-done((f32[19,8,4,136]{3,2,1,0:T(4,128)S(1)}, f32[19,8,4,136]{3,2,1,0:T(4,128)S(1)}, u32[]{:S(2)}, u32[]{:S(2)}) %collective-permute-start.3) | collective-permute-done | bytes 330784 | tf_op jit(solution)/shard_map/ppermute | solution.py:30
  45.2 4.1 %collective-permute-done.4 = f32[19,8,4,136]{3,2,1,0:T(4,128)S(1)} collective-permute-done((f32[19,8,4,136]{3,2,1,0:T(4,128)S(1)}, f32[19,8,4,136]{3,2,1,0:T(4,128)S(1)}, u32[]{:S(2)}, u32[]{:S(2)}) %collective-permute-start.4) | collective-permute-done | bytes 330784 | tf_op jit(solution)/shard_map/ppermute | solution.py:30
  49.7 0.2 subtract_bitcast_fusion.23
  50.1 1.2 %pad_maximum_fusion = f32[19,8,16,136]{3,2,1,0:T(8,128)S(1)} fusion(f32[19,8,4,136]{3,2,1,0:T(4,128)S(1)} %collective-permute-done.4, f32[19,8,8,4]{3,2,1,0:T(8,128)S(1)} %copy.46, f32[1,8,8,128]{3,2,1,0:T(8,128)S(1)} %broadcast_in_dim.103, f32[18,4,8,128]{3,2,1,0:T(8,128)S(1)} %get-tuple-element.62, f32[18,4,8,128]{3,2,1,0:T(8,128)S(1)} %get-tuple-element.61, ...), kind=kLoop, calls=%fused_computation | loop fusion | flops 1984512 | bytes 2646016 | tf_op jit(solution)/shard_map/concatenate | solution.py:40
  51.7 0.4 copy-done.1
  52.6 0.3 multiply_add_fusion.3
  53.8 0.3 multiply_add_fusion.2
  55.3 0.3 multiply_add_fusion.1
  56.7 0.3 multiply_add_fusion
  57.6 0.7 %dynamic-slice_multiply_fusion = f32[4,8,128]{2,1,0:T(8,128)} fusion(f32[8,16,136]{2,1,0:T(8,128)S(1)} %fusion.50, s32[]{:T(128)S(6)} %select_n.137, s32[]{:T(128)S(6)} %add.350), kind=kLoop, calls=%fused_computation.189 | loop fusion | flops 4096 | bytes 32776 | tf_op jit(solution)/shard_map/div | solution.py:218
  58.3 0.8 %pad_dynamic-slice_fusion.27 = (f32[3,4,8,128]{3,2,1,0:T(8,128)}, f32[3,4,8,128]{3,2,1,0:T(8,128)}) fusion(s32[]{:T(128)S(6)} %dynamic_slice.77, s32[]{:T(128)S(6)} %add.350, f32[3,8,16,136]{3,2,1,0:T(8,128)S(1)} %fusion.11, f32[3,8,16,136]{3,2,1,0:T(8,128)S(1)} %fusion.20), kind=kLoop, calls=%fused_computation.41 | loop fusion | bytes 516104 | tf_op jit(solution)/shard_map/slice | solution.py:212
  59.1 0.8 %pad_dynamic-slice_fusion = (f32[2,3,4,8,128]{4,3,2,1,0:T(8,128)}, f32[2,3,4,8,128]{4,3,2,1,0:T(8,128)}) fusion(s32[]{:T(128)S(6)} %dynamic_slice.77, s32[]{:T(128)S(6)} %add.350, f32[2,3,8,16,136]{4,3,2,1,0:T(8,128)S(1)} %get-tuple-element.19, f32[2,3,8,16,136]{4,3,2,1,0:T(8,128)S(1)} %get-tuple-element.18), kind=kLoop, calls=%fused_computation.2 | loop fusion | bytes 1032200 | tf_op jit(solution)/shard_map/slice | solution.py:212
  (79 shorter events, 4.9 us)
Async XLA Ops:
  1.6 8.8 %collective-permute-start = (f32[18,4,8,128]{3,2,1,0:T(8,128)S(1)}, f32[18,4,8,128]{3,2,1,0:T(8,128)S(1)}, u32[]{:S(2)}, u32[]{:S(2)}) collective-permute-start(f32[18,4,8,128]{3,2,1,0:T(8,128)S(1)} %pad_maximum_fusion.3), channel_id=1, source_target_pairs={{0,16},{16,0},{1,17},{17,1},{2,18},{18,2},{3,19},{19,3},{4,20},{20... | collective-permute-start | bytes 884744 | tf_op jit(solution)/shard_map/ppermute | solution.py:25
  11.5 7.8 %copy-start = (s32[4]{0:T(128)S(1)}, s32[4]{0:T(128)}, u32[]{:S(2)}) copy-start(s32[4]{0:T(128)} %param.16) | copy-start | bytes 52
  12.3 15.4 %collective-permute-start.1 = (f32[19,8,8,4]{0,2,3,1:T(8,128)S(1)}, f32[19,8,8,4]{0,2,3,1:T(8,128)S(1)}, u32[]{:S(2)}, u32[]{:S(2)}) collective-permute-start(f32[19,8,8,4]{0,2,3,1:T(8,128)S(1)} %copy.43), channel_id=1, source_target_pairs={{0,4},{4,8},{8,12},{1,5},{5,9},{9,13},{2,6},{6,10},{10,14},{3,7},{... | collective-permute-start | bytes 58376 | tf_op jit(solution)/shard_map/ppermute | solution.py:30
  17.4 11.0 %collective-permute-start.2 = (f32[19,8,8,4]{0,2,3,1:T(8,128)S(1)}, f32[19,8,8,4]{0,2,3,1:T(8,128)S(1)}, u32[]{:S(2)}, u32[]{:S(2)}) collective-permute-start(f32[19,8,8,4]{0,2,3,1:T(8,128)S(1)} %copy.44), channel_id=1, source_target_pairs={{4,0},{8,4},{12,8},{5,1},{9,5},{13,9},{6,2},{10,6},{14,10},{7,3},{... | collective-permute-start | bytes 58376 | tf_op jit(solution)/shard_map/ppermute | solution.py:30
  30.0 15.1 %collective-permute-start.3 = (f32[19,8,4,136]{3,2,1,0:T(4,128)S(1)}, f32[19,8,4,136]{3,2,1,0:T(4,128)S(1)}, u32[]{:S(2)}, u32[]{:S(2)}) collective-permute-start(f32[19,8,4,136]{3,2,1,0:T(4,128)S(1)} %get-tuple-element.57), channel_id=1, source_target_pairs={{0,1},{1,2},{2,3},{4,5},{5,6},{6,7},{8,9},{9,10},{10,11},{12,13},{... | collective-permute-start | bytes 992264 | tf_op jit(solution)/shard_map/ppermute | solution.py:30
  33.3 16.0 %collective-permute-start.4 = (f32[19,8,4,136]{3,2,1,0:T(4,128)S(1)}, f32[19,8,4,136]{3,2,1,0:T(4,128)S(1)}, u32[]{:S(2)}, u32[]{:S(2)}) collective-permute-start(f32[19,8,4,136]{3,2,1,0:T(4,128)S(1)} %get-tuple-element.58), channel_id=1, source_target_pairs={{1,0},{2,1},{3,2},{5,4},{6,5},{7,6},{9,8},{10,9},{11,10},{13,12},{... | collective-permute-start | bytes 992264 | tf_op jit(solution)/shard_map/ppermute | solution.py:30
  51.5 0.7 %copy-start.1 = (f32[8]{0:T(128)S(1)}, f32[8]{0:T(128)}, u32[]{:S(2)}) copy-start(f32[8]{0:T(128)} %param.17) | copy-start | bytes 100
  51.5 0.7 %copy-start.2 = (f32[8]{0:T(128)S(1)}, f32[8]{0:T(128)}, u32[]{:S(2)}) copy-start(f32[8]{0:T(128)} %param.18) | copy-start | bytes 100

commit v2 on v1

--- a/solution.py
+++ b/solution.py
@@ -35,9 +35,20 @@
     length = cells.shape[dim]
     head = lax.slice_in_dim(cells, 0, width, axis=dim)
     tail = lax.slice_in_dim(cells, length - width, length, axis=dim)
-    below = from_offsets(tail, axis, (-1,))[-1]
-    above = from_offsets(head, axis, (1,))[1]
+    below = unpacked(from_offsets(packed(tail), axis, (-1,))[-1], tail.shape)
+    above = unpacked(from_offsets(packed(head), axis, (1,))[1], head.shape)
     return jnp.concatenate([below, cells, above], axis=dim)
+
+
+def packed(values):
+    lanes = 128
+    if values.size % lanes:
+        return values.reshape(-1)
+    return values.reshape(-1, lanes)
+
+
+def unpacked(values, shape):
+    return values.reshape(shape)
 
 
 def upper_next(values, dimension):

time: 60.4 us -> 57.7 us (0.955)
  waiting for transfers between devices: 18.3 us -> 11 us
  local copies, waits for them, and re-layouts: 9.24 us -> 13.7 us
    ppermute x4, waiting for transfers between devices: 14.6 us -> 7.35 us  [from_offsets(): got[k] = lax.ppermute(value, axis, pairs)]
    reshape x0 -> x8, local copies, waits for them, and re-layouts: none -> 6.95 us  [the longest x4 4.1 us: unpacked(): return values.reshape(shape)]
    ppermute x2 -> x0, local copies, waits for them, and re-layouts: 1.44 us -> none  [from_offsets(): got[k] = lax.ppermute(value, axis, pairs)]
  transfers between devices with their start and end apart: 5 -> 5, of which waited for: 3 -> 3; matrix products, arithmetic and copies ran while one was open for 8% -> 11% of each run, Pallas kernels for 0% -> 0%
where the time goes in v2:
time: 57.7 us; the launch traced here: 57.1 us
  local copies, waits for them, and re-layouts  13.7 us (24%)
  starting transfers between devices  13.2 us (23%)
  waiting for transfers between devices  11 us (19%)
  other arithmetic  10.1 us (18%)
  between operations  9.07 us (16%)
    ppermute x4, starting transfers between devices, from_offsets(): got[k] = lax.ppermute(value, axis, pairs)  11.1 us
    ppermute x4, waiting for transfers between devices, from_offsets(): got[k] = lax.ppermute(value, axis, pairs)  7.35 us
    reshape x4, local copies, waits for them, and re-layouts, unpacked(): return values.reshape(shape)  4.1 us
    ppermute x1, waiting for transfers between devices, from_offsets(): received = lax.ppermute(value, axis, pairs)  3.68 us
    reshape x4, local copies, waits for them, and re-layouts, packed(): return values.reshape(-1, lanes)  2.85 us
    broadcast_in_dim x3, local copies, waits for them, and re-layouts, cell_lookup(): jnp.where(selector, table[:, None, None], jnp.float32(0.0))  2.27 us
    ppermute x1, starting transfers between devices, from_offsets(): received = lax.ppermute(value, axis, pairs)  2.11 us
    concatenate x2, other arithmetic, with_halo(): return jnp.concatenate([below, cells, above], axis=dim)  1.75 us
  transfers between devices with their start and end apart: 5, of which 3 were waited for; matrix products, arithmetic and copies ran while one was open for 11% of the time, Pallas kernels for 0%

profile of v2, /device:TPU:1, one launch (start us, length us, event | category | flops | bytes accessed | tf_op | source)
XLA Modules:
  0.0 57.1 jit_solution(6703032158152035990)
XLA Ops:
  0.6 1.0 %pad_maximum_fusion.3 = f32[18,4,8,128]{3,2,1,0:T(8,128)S(1)} fusion(f32[6,4,8,128]{3,2,1,0:T(8,128)} %bitcast.328, f32[6,4,8,128]{3,2,1,0:T(8,128)} %bitcast.330, f32[3,4,8,128]{3,2,1,0:T(8,128)} %param.12, f32[3,4,8,128]{3,2,1,0:T(8,128)} %param.11), kind=kLoop, calls=%fused_computation.99 | loop fusion | flops 221184 | bytes 589824 | tf_op jit(solution)/shard_map/concatenate | solution.py:135
  1.6 2.1 %collective-permute-start = (f32[18,4,8,128]{3,2,1,0:T(8,128)S(1)}, f32[18,4,8,128]{3,2,1,0:T(8,128)S(1)}, u32[]{:S(2)}, u32[]{:S(2)}) collective-permute-start(f32[18,4,8,128]{3,2,1,0:T(8,128)S(1)} %pad_maximum_fusion.3), channel_id=1, source_target_pairs={{0,16},{16,0},{1,17},{17,1},{2,18},{18,2},{3,19},{19,3},{4,20},{20... | collective-permute-start | bytes 884744 | tf_op jit(solution)/shard_map/ppermute | solution.py:25
  3.7 0.7 %convert_element_type.20 = f32[8,128]{1,0:T(8,128)S(1)} convert(s32[8,128]{1,0:T(8,128)} %param.15) | non-fusion elementwise | flops 1024 | bytes 8192 | tf_op jit(solution)/shard_map/convert_element_type | solution.py:170
  4.4 0.8 %slice_bitcast_fusion.33 = (f32[8]{0:T(128)S(1)}, f32[8]{0:T(128)S(1)}) fusion(f32[2,8]{1,0:T(2,128)} %param.21), kind=kLoop, calls=%fused_computation.200 | loop fusion | bytes 128 | tf_op jit(solution)/shard_map/jit(_where)/broadcast_in_dim | solution.py:96
  5.2 0.8 %slice_bitcast_fusion.31 = (f32[8]{0:T(128)S(1)}, f32[8]{0:T(128)S(1)}) fusion(f32[2,8]{1,0:T(2,128)} %param.20), kind=kLoop, calls=%fused_computation.198 | loop fusion | bytes 128 | tf_op jit(solution)/shard_map/jit(_where)/broadcast_in_dim | solution.py:96
  5.9 0.8 %slice_bitcast_fusion.29 = (f32[8]{0:T(128)S(1)}, f32[8]{0:T(128)S(1)}) fusion(f32[2,8]{1,0:T(2,128)} %param.19), kind=kLoop, calls=%fused_computation.196 | loop fusion | bytes 128 | tf_op jit(solution)/shard_map/jit(_where)/broadcast_in_dim | solution.py:96
  6.8 3.7 %collective-permute-done = f32[18,4,8,128]{3,2,1,0:T(8,128)S(1)} collective-permute-done((f32[18,4,8,128]{3,2,1,0:T(8,128)S(1)}, f32[18,4,8,128]{3,2,1,0:T(8,128)S(1)}, u32[]{:S(2)}, u32[]{:S(2)}) %collective-permute-start) | collective-permute-done | bytes 294944 | tf_op jit(solution)/shard_map/ppermute | solution.py:25
  10.4 1.0 %select_select_fusion.1 = (f32[18,4,8,128]{3,2,1,0:T(8,128)S(1)}, f32[18,4,8,128]{3,2,1,0:T(8,128)S(1)}) fusion(f32[18,4,8,128]{3,2,1,0:T(8,128)S(1)} %collective-permute-done, pred[]{:T(512)S(6)} %and.62, pred[]{:T(512)S(6)} %eq.28, pred[]{:T(512)S(6)} %and.61, pred[]{:T(512)S(6)} %eq.27, pred[]{:T(512)S(6)} %eq.26, f32[6,4,8,128]{3,2,1,0:T(8,128)} %bitcast.329, ...), kind=kLoop, calls=%fused_computation.101 | loop fusion | flops 811008 | bytes 1179656 | tf_op jit(solution)/shard_map/jit(_where)/select_n | solution.py:156
  11.8 0.3 reshape.228
  12.1 4.5 %collective-permute-start.1 = (f32[38,128]{1,0:T(8,128)S(1)}, f32[38,128]{1,0:T(8,128)S(1)}, u32[]{:S(2)}, u32[]{:S(2)}) collective-permute-start(f32[38,128]{1,0:T(8,128)S(1)} %reshape.228), channel_id=1, source_target_pairs={{0,4},{4,8},{8,12},{1,5},{5,9},{9,13},{2,6},{6,10},{10,14},{3,7},{... | collective-permute-start | bytes 58376 | tf_op jit(solution)/shard_map/ppermute | solution.py:30
  16.6 0.3 reshape.230
  16.9 1.9 %collective-permute-start.2 = (f32[38,128]{1,0:T(8,128)S(1)}, f32[38,128]{1,0:T(8,128)S(1)}, u32[]{:S(2)}, u32[]{:S(2)}) collective-permute-start(f32[38,128]{1,0:T(8,128)S(1)} %reshape.230), channel_id=1, source_target_pairs={{4,0},{8,4},{12,8},{5,1},{9,5},{13,9},{6,2},{10,6},{14,10},{7,3},{... | collective-permute-start | bytes 58376 | tf_op jit(solution)/shard_map/ppermute | solution.py:30
  18.9 0.6 %fusion.74 = (s32[1]{0:T(128)}, s32[1]{0:T(128)}, s32[1]{0:T(128)}, s32[1]{0:T(128)}) fusion(s32[4]{0:T(128)S(1)} %copy-done), kind=kLoop, calls=%fused_computation.205 | loop fusion | bytes 32 | tf_op jit(solution)/shard_map/slice | solution.py:214
  27.2 0.6 %reshape.229 = f32[19,8,8,4]{3,2,1,0:T(8,128)S(1)} reshape(f32[38,128]{1,0:T(8,128)S(1)} %collective-permute-done.1) | data formatting | bytes 38912 | tf_op jit(solution)/shard_map/reshape | solution.py:51
  27.9 0.6 %reshape.231 = f32[19,8,8,4]{3,2,1,0:T(8,128)S(1)} reshape(f32[38,128]{1,0:T(8,128)S(1)} %collective-permute-done.2) | data formatting | bytes 38912 | tf_op jit(solution)/shard_map/reshape | solution.py:51
  28.5 0.6 pad_maximum_fusion.1
  29.1 0.3 fusion.72
  29.4 1.5 %reshape.232 = f32[646,128]{1,0:T(8,128)} reshape(f32[19,8,4,136]{3,2,1,0:T(4,128)S(1)} %get-tuple-element.52) | data formatting | bytes 661504 | tf_op jit(solution)/shard_map/reshape | solution.py:47
  30.9 3.2 %collective-permute-start.3 = (f32[646,128]{1,0:T(8,128)}, f32[646,128]{1,0:T(8,128)S(1)}, u32[]{:S(2)}, u32[]{:S(2)}) collective-permute-start(f32[646,128]{1,0:T(8,128)} %reshape.232), channel_id=1, source_target_pairs={{0,1},{1,2},{2,3},{4,5},{5,6},{6,7},{8,9},{9,10},{10,11},{12,13},{... | collective-permute-start | bytes 992264 | tf_op jit(solution)/shard_map/ppermute | solution.py:30
  34.1 0.7 %reshape.234 = f32[646,128]{1,0:T(8,128)S(1)} reshape(f32[19,8,4,136]{3,2,1,0:T(4,128)S(1)} %get-tuple-element.53) | data formatting | bytes 661504 | tf_op jit(solution)/shard_map/reshape | solution.py:47
  34.8 1.5 %collective-permute-start.4 = (f32[646,128]{1,0:T(8,128)S(1)}, f32[646,128]{1,0:T(8,128)}, u32[]{:S(2)}, u32[]{:S(2)}) collective-permute-start(f32[646,128]{1,0:T(8,128)S(1)} %reshape.234), channel_id=1, source_target_pairs={{1,0},{2,1},{3,2},{5,4},{6,5},{7,6},{9,8},{10,9},{11,10},{13,12},{... | collective-permute-start | bytes 992264 | tf_op jit(solution)/shard_map/ppermute | solution.py:30
  36.4 3.6 %collective-permute-done.3 = f32[646,128]{1,0:T(8,128)S(1)} collective-permute-done((f32[646,128]{1,0:T(8,128)}, f32[646,128]{1,0:T(8,128)S(1)}, u32[]{:S(2)}, u32[]{:S(2)}) %collective-permute-start.3) | collective-permute-done | bytes 330784 | tf_op jit(solution)/shard_map/ppermute | solution.py:30
  40.1 1.0 %reshape.233 = f32[19,8,4,136]{3,2,1,0:T(4,128)S(1)} reshape(f32[646,128]{1,0:T(8,128)S(1)} %collective-permute-done.3) | data formatting | bytes 661504 | tf_op jit(solution)/shard_map/reshape | solution.py:51
  41.0 3.7 %collective-permute-done.4 = f32[646,128]{1,0:T(8,128)} collective-permute-done((f32[646,128]{1,0:T(8,128)S(1)}, f32[646,128]{1,0:T(8,128)}, u32[]{:S(2)}, u32[]{:S(2)}) %collective-permute-start.4) | collective-permute-done | bytes 330784 | tf_op jit(solution)/shard_map/ppermute | solution.py:30
  44.7 1.9 %reshape.235 = f32[19,8,4,136]{3,2,1,0:T(4,128)S(1)} reshape(f32[646,128]{1,0:T(8,128)} %collective-permute-done.4) | data formatting | bytes 661504 | tf_op jit(solution)/shard_map/reshape | solution.py:51
  47.1 1.2 %pad_maximum_fusion = f32[19,8,16,136]{3,2,1,0:T(8,128)S(1)} fusion(f32[19,8,4,136]{3,2,1,0:T(4,128)S(1)} %reshape.235, f32[19,8,8,4]{3,2,1,0:T(8,128)S(1)} %reshape.231, f32[1,8,8,128]{3,2,1,0:T(8,128)S(1)} %broadcast_in_dim.103, f32[18,4,8,128]{3,2,1,0:T(8,128)S(1)} %get-tuple-element.57, f32[18,4,8,128]{3,2,1,0:T(8,128)S(1)} %get-tuple-element.56, ...), kind=kLoop, calls=%fused_computation | loop fusion | flops 1984512 | bytes 2646016 | tf_op jit(solution)/shard_map/concatenate | solution.py:40
  49.1 0.4 copy-done.1
  52.5 0.3 multiply_add_fusion.1
  53.9 0.3 multiply_add_fusion
  54.9 0.7 %dynamic-slice_multiply_fusion = f32[4,8,128]{2,1,0:T(8,128)} fusion(f32[8,16,136]{2,1,0:T(8,128)S(1)} %fusion.50, s32[]{:T(128)S(6)} %select_n.137, s32[]{:T(128)S(6)} %add.350), kind=kLoop, calls=%fused_computation.189 | loop fusion | flops 4096 | bytes 32776 | tf_op jit(solution)/shard_map/div | solution.py:229
  55.6 0.8 %pad_dynamic-slice_fusion.27 = (f32[3,4,8,128]{3,2,1,0:T(8,128)}, f32[3,4,8,128]{3,2,1,0:T(8,128)}) fusion(s32[]{:T(128)S(6)} %dynamic_slice.77, s32[]{:T(128)S(6)} %add.350, f32[3,8,16,136]{3,2,1,0:T(8,128)S(1)} %fusion.11, f32[3,8,16,136]{3,2,1,0:T(8,128)S(1)} %fusion.20), kind=kLoop, calls=%fused_computation.41 | loop fusion | bytes 516104 | tf_op jit(solution)/shard_map/slice | solution.py:223
  56.3 0.8 %pad_dynamic-slice_fusion = (f32[2,3,4,8,128]{4,3,2,1,0:T(8,128)}, f32[2,3,4,8,128]{4,3,2,1,0:T(8,128)}) fusion(s32[]{:T(128)S(6)} %dynamic_slice.77, s32[]{:T(128)S(6)} %add.350, f32[2,3,8,16,136]{4,3,2,1,0:T(8,128)S(1)} %get-tuple-element.14, f32[2,3,8,16,136]{4,3,2,1,0:T(8,128)S(1)} %get-tuple-element.13), kind=kLoop, calls=%fused_computation.2 | loop fusion | bytes 1032200 | tf_op jit(solution)/shard_map/slice | solution.py:223
  (83 shorter events, 5.9 us)
Async XLA Ops:
  1.6 8.8 %collective-permute-start = (f32[18,4,8,128]{3,2,1,0:T(8,128)S(1)}, f32[18,4,8,128]{3,2,1,0:T(8,128)S(1)}, u32[]{:S(2)}, u32[]{:S(2)}) collective-permute-start(f32[18,4,8,128]{3,2,1,0:T(8,128)S(1)} %pad_maximum_fusion.3), channel_id=1, source_target_pairs={{0,16},{16,0},{1,17},{17,1},{2,18},{18,2},{3,19},{19,3},{4,20},{20... | collective-permute-start | bytes 884744 | tf_op jit(solution)/shard_map/ppermute | solution.py:25
  11.5 7.4 %copy-start = (s32[4]{0:T(128)S(1)}, s32[4]{0:T(128)}, u32[]{:S(2)}) copy-start(s32[4]{0:T(128)} %param.16) | copy-start | bytes 52
  12.1 15.1 %collective-permute-start.1 = (f32[38,128]{1,0:T(8,128)S(1)}, f32[38,128]{1,0:T(8,128)S(1)}, u32[]{:S(2)}, u32[]{:S(2)}) collective-permute-start(f32[38,128]{1,0:T(8,128)S(1)} %reshape.228), channel_id=1, source_target_pairs={{0,4},{4,8},{8,12},{1,5},{5,9},{9,13},{2,6},{6,10},{10,14},{3,7},{... | collective-permute-start | bytes 58376 | tf_op jit(solution)/shard_map/ppermute | solution.py:30
  16.9 11.0 %collective-permute-start.2 = (f32[38,128]{1,0:T(8,128)S(1)}, f32[38,128]{1,0:T(8,128)S(1)}, u32[]{:S(2)}, u32[]{:S(2)}) collective-permute-start(f32[38,128]{1,0:T(8,128)S(1)} %reshape.230), channel_id=1, source_target_pairs={{4,0},{8,4},{12,8},{5,1},{9,5},{13,9},{6,2},{10,6},{14,10},{7,3},{... | collective-permute-start | bytes 58376 | tf_op jit(solution)/shard_map/ppermute | solution.py:30
  30.9 9.2 %collective-permute-start.3 = (f32[646,128]{1,0:T(8,128)}, f32[646,128]{1,0:T(8,128)S(1)}, u32[]{:S(2)}, u32[]{:S(2)}) collective-permute-start(f32[646,128]{1,0:T(8,128)} %reshape.232), channel_id=1, source_target_pairs={{0,1},{1,2},{2,3},{4,5},{5,6},{6,7},{8,9},{9,10},{10,11},{12,13},{... | collective-permute-start | bytes 992264 | tf_op jit(solution)/shard_map/ppermute | solution.py:30
  34.8 9.9 %collective-permute-start.4 = (f32[646,128]{1,0:T(8,128)S(1)}, f32[646,128]{1,0:T(8,128)}, u32[]{:S(2)}, u32[]{:S(2)}) collective-permute-start(f32[646,128]{1,0:T(8,128)S(1)} %reshape.234), channel_id=1, source_target_pairs={{1,0},{2,1},{3,2},{5,4},{6,5},{7,6},{9,8},{10,9},{11,10},{13,12},{... | collective-permute-start | bytes 992264 | tf_op jit(solution)/shard_map/ppermute | solution.py:30
  48.9 0.7 %copy-start.1 = (f32[8]{0:T(128)S(1)}, f32[8]{0:T(128)}, u32[]{:S(2)}) copy-start(f32[8]{0:T(128)} %param.17) | copy-start | bytes 100
  48.9 0.7 %copy-start.2 = (f32[8]{0:T(128)S(1)}, f32[8]{0:T(128)}, u32[]{:S(2)}) copy-start(f32[8]{0:T(128)} %param.18) | copy-start | bytes 100

commit v3 on v2

--- a/solution.py
+++ b/solution.py
@@ -28,6 +28,57 @@
                 got[j] = jnp.where(inside, received, jnp.zeros_like(received))
             continue
         got[k] = lax.ppermute(value, axis, pairs)
+    return got
+
+
+def from_neighbours(value_for, axes, offsets):
+    counts = [lax.axis_size(a) for a in axes]
+    mine = [lax.axis_index(a) for a in axes]
+    coords = [()]
+    for n in counts:
+        coords = [c + (i,) for c in coords for i in range(n)]
+
+    def linear(c):
+        index = 0
+        for i, n in zip(c, counts):
+            index = index * n + i
+        return index
+
+    def pairs_of(k):
+        out = []
+        for c in coords:
+            t = tuple(ci - ki for ci, ki in zip(c, k))
+            if all(0 <= ti < n for ti, n in zip(t, counts)):
+                out.append((linear(c), linear(t)))
+        return out
+
+    def exists(k):
+        ok = jnp.bool_(True)
+        for m, ki, n in zip(mine, k, counts):
+            ok = ok & (m + ki >= 0) & (m + ki < n)
+        return ok
+
+    got = {}
+    for k in offsets:
+        if k in got:
+            continue
+        back = tuple(-ki for ki in k)
+        pairs = pairs_of(k)
+        if not pairs:
+            got[k] = jnp.zeros_like(value_for(back))
+            continue
+        if back in offsets and back not in got:
+            both = pairs + pairs_of(back)
+            if len({a for a, _ in both}) == len(both) and len({b for _, b in both}) == len(both):
+                toward_back, toward_k = (value_for(back), value_for(k))
+                payload = toward_k
+                if toward_back is not toward_k:
+                    payload = jnp.where(exists(back), toward_back, toward_k)
+                received = lax.ppermute(payload, axes, both)
+                for j in (k, back):
+                    got[j] = jnp.where(exists(j), received, jnp.zeros_like(received))
+                continue
+        got[k] = lax.ppermute(value_for(back), axes, pairs)
     return got
 
 
@@ -145,31 +196,48 @@
     below = -(-STEPS // planes)
     above = -(-(STEPS + STEPS * WSHIFT) // planes)
     whole_column = (below + above + 1) * planes >= total_z
+    kinds = material.astype(jnp.float32)
+    with_kinds = jnp.concatenate([state, jnp.broadcast_to(kinds[None, None], (1,) + state.shape[1:])], axis=0)
     if whole_column:
-        offsets = [k for k in range(-(n_prop - 1), n_prop) if k != 0]
-        pieces = from_offsets(state, "prop", offsets)
-        pieces[0] = state
+        head = lax.slice_in_dim(with_kinds, 0, halo, axis=3)
+        tail = lax.slice_in_dim(with_kinds, columns - halo, columns, axis=3)
+
+        def value_for(d):
+            if d[1] == 0:
+                return state
+            return packed(tail if d[1] > 0 else head)
+
+        offsets = [
+            (kz, kx) for kz in range(-(n_prop - 1), n_prop) for kx in (-1, 0, 1) if (kz, kx) != (0, 0)
+        ]
+        pieces = from_neighbours(value_for, ("prop", "tx"), offsets)
+        pieces[(0, 0)] = state
         blocks = []
         for j in range(n_prop):
-            block = jnp.zeros_like(state)
-            for k, piece in pieces.items():
-                block = jnp.where(at_z + k == j, piece, block)
-            blocks.append(block)
+            parts = []
+            for kx in (-1, 0, 1):
+                part = None
+                for kz in range(-(n_prop - 1), n_prop):
+                    piece = pieces[(kz, kx)]
+                    part = piece if part is None else jnp.where(at_z + kz == j, piece, part)
+                if kx == 0:
+                    part = jnp.concatenate([part, with_kinds[-1:]], axis=0)
+                else:
+                    part = unpacked(part, head.shape)
+                parts.append(part)
+            blocks.append(jnp.concatenate(parts, axis=3))
         state = jnp.concatenate(blocks, axis=1)
         base_z = jnp.int32(0)
         own_z = at_z * planes
     else:
         offsets = [k for k in range(-below, above + 1) if k != 0]
-        pieces = from_offsets(state, "prop", offsets)
-        pieces[0] = state
+        pieces = from_offsets(with_kinds, "prop", offsets)
+        pieces[0] = with_kinds
         state = jnp.concatenate([pieces[k] for k in range(-below, above + 1)], axis=1)
         base_z = (at_z - below) * planes
         own_z = below * planes
+        state = with_halo(state, "tx", 3, halo)
     depth = state.shape[1]
-
-    kinds = material.astype(jnp.float32)
-    state = jnp.concatenate([state, jnp.broadcast_to(kinds[None, None], (1, depth, rows, columns))], axis=0)
-    state = with_halo(state, "tx", 3, halo)
     state = with_halo(state, "ty", 2, halo)
     kinds = state[-1, 0].astype(jnp.int32)
     electric_b, magnetic_b = (state[0:3], state[3:6])

time: 57.7 us -> 63.9 us (1.11)
  the two profiles are of different devices: /device:TPU:1 before, /device:TPU:0 now
where the time goes in v3:
time: 63.9 us; the launch traced here: 63.4 us
  starting transfers between devices  18.5 us (29%)
  local copies, waits for them, and re-layouts  15.3 us (24%)
  other arithmetic  11.2 us (18%)
  between operations  9.33 us (15%)
  waiting for transfers between devices  8.98 us (14%)
    ppermute x3, starting transfers between devices, from_neighbours(): received = lax.ppermute(payload, axes, both)  9.95 us
    ppermute x2, waiting for transfers between devices, from_offsets(): got[k] = lax.ppermute(value, axis, pairs)  8.96 us
    ppermute x2, starting transfers between devices, from_offsets(): got[k] = lax.ppermute(value, axis, pairs)  4.96 us
    reshape x6, local copies, waits for them, and re-layouts, unpacked(): return values.reshape(shape)  4.46 us
    unnamed x24, local copies, waits for them, and re-layouts  4 us
    concatenate x1, other arithmetic, with_halo(): return jnp.concatenate([below, cells, above], axis=dim)  3.96 us
    ppermute x2, starting transfers between devices, from_neighbours(): got[k] = lax.ppermute(value_for(back), axes, pairs)  3.64 us
    reshape x2, local copies, waits for them, and re-layouts, packed(): return values.reshape(-1, lanes)  2.22 us
  transfers between devices with their start and end apart: 7, of which 2 were waited for; matrix products, arithmetic and copies ran while one was open for 7% of the time, Pallas kernels for 0%

profile of v3, /device:TPU:0, one launch (start us, length us, event | category | flops | bytes accessed | tf_op | source)
XLA Modules:
  0.0 63.4 jit_solution(2429193115362099555)
XLA Ops:
  0.7 0.9 %constant_dynamic-update-slice_fusion.4 = f32[19,4,8,128]{3,2,1,0:T(8,128)S(1)} fusion(f32[3,4,8,128]{3,2,1,0:T(8,128)} %param.11), kind=kLoop, calls=%fused_computation.201 | loop fusion | bytes 98304
  1.6 0.7 %convert_element_type.20 = f32[8,128]{1,0:T(8,128)S(1)} convert(s32[8,128]{1,0:T(8,128)} %param.15) | non-fusion elementwise | flops 1024 | bytes 8192 | tf_op jit(solution)/shard_map/convert_element_type | solution.py:199
  2.3 0.8 %constant_dynamic-update-slice_fusion.3 = f32[19,4,8,128]{3,2,1,0:T(8,128)S(1)} fusion(f32[19,4,8,128]{3,2,1,0:T(8,128)S(1)} %constant_dynamic-update-slice_fusion.4, f32[3,4,8,128]{3,2,1,0:T(8,128)} %param.12), kind=kLoop, calls=%fused_computation.200 | loop fusion | bytes 98304
  3.1 0.9 %constant_dynamic-update-slice_fusion.2 = f32[19,4,8,128]{3,2,1,0:T(8,128)S(1)} fusion(f32[19,4,8,128]{3,2,1,0:T(8,128)S(1)} %constant_dynamic-update-slice_fusion.3, f32[6,4,8,128]{3,2,1,0:T(8,128)} %bitcast.322), kind=kLoop, calls=%fused_computation.199 | loop fusion | bytes 196608
  4.0 0.9 %constant_dynamic-update-slice_fusion.1 = f32[19,4,8,128]{3,2,1,0:T(8,128)S(1)} fusion(f32[19,4,8,128]{3,2,1,0:T(8,128)S(1)} %constant_dynamic-update-slice_fusion.2, f32[6,4,8,128]{3,2,1,0:T(8,128)} %bitcast.325), kind=kLoop, calls=%fused_computation.198 | loop fusion | bytes 196608
  5.1 0.3 copy.23
  5.4 2.4 %collective-permute-start.1 = (f32[19,128]{0,1:T(8,128)S(1)}, f32[19,128]{0,1:T(8,128)S(1)}, u32[]{:S(2)}, u32[]{:S(2)}) collective-permute-start(f32[19,128]{0,1:T(8,128)S(1)} %bitcast.336), channel_id=1, source_target_pairs={{0,4},{4,8},{8,12},{16,20},{20,24},{24,28},{1,5},{5,9},{9,13},{17,... | collective-permute-start | bytes 29192 | tf_op jit(solution)/shard_map/ppermute | solution.py:81
  8.1 1.3 %collective-permute-start.4 = (f32[19,128]{0,1:T(8,128)S(1)}, f32[19,128]{0,1:T(8,128)S(1)}, u32[]{:S(2)}, u32[]{:S(2)}) collective-permute-start(f32[19,128]{0,1:T(8,128)S(1)} %bitcast.338), channel_id=1, source_target_pairs={{4,0},{8,4},{12,8},{20,16},{24,20},{28,24},{5,1},{9,5},{13,9},{21,... | collective-permute-start | bytes 29192 | tf_op jit(solution)/shard_map/ppermute | solution.py:81
  9.4 0.7 %collective-permute-start = (f32[19,128]{0,1:T(8,128)S(1)}, f32[19,128]{0,1:T(8,128)S(1)}, u32[]{:S(2)}, u32[]{:S(2)}) collective-permute-start(f32[19,128]{0,1:T(8,128)S(1)} %get-tuple-element.105), channel_id=1, source_target_pairs={{4,16},{8,20},{12,24},{16,4},{20,8},{24,12},{5,17},{9,21},{13,25},... | collective-permute-start | bytes 29192 | tf_op jit(solution)/shard_map/ppermute | solution.py:77
  10.1 9.2 %collective-permute-start.2 = (f32[19,128]{0,1:T(8,128)S(1)}, f32[19,128]{0,1:T(8,128)S(1)}, u32[]{:S(2)}, u32[]{:S(2)}) collective-permute-start(f32[19,128]{0,1:T(8,128)S(1)} %get-tuple-element.104), channel_id=1, source_target_pairs={{0,20},{4,24},{8,28},{20,0},{24,4},{28,8},{1,21},{5,25},{9,29},{21... | collective-permute-start | bytes 29192 | tf_op jit(solution)/shard_map/ppermute | solution.py:77
  19.7 0.6 fusion.74
  28.1 0.4 copy.24
  28.5 0.4 copy.25
  28.9 0.4 copy.26
  29.3 0.4 copy.27
  29.9 0.5 maximum_maximum_fusion
  30.7 1.5 %reshape.244 = f32[646,128]{1,0:T(8,128)} reshape(f32[19,8,4,136]{3,2,1,0:T(4,128)S(1)} %get-tuple-element.48) | data formatting | bytes 661504 | tf_op jit(solution)/shard_map/reshape | solution.py:98
  32.2 3.5 %collective-permute-start.5 = (f32[646,128]{1,0:T(8,128)}, f32[646,128]{1,0:T(8,128)S(1)}, u32[]{:S(2)}, u32[]{:S(2)}) collective-permute-start(f32[646,128]{1,0:T(8,128)} %reshape.244), channel_id=1, source_target_pairs={{0,1},{1,2},{2,3},{4,5},{5,6},{6,7},{8,9},{9,10},{10,11},{12,13},{... | collective-permute-start | bytes 992264 | tf_op jit(solution)/shard_map/ppermute | solution.py:30
  35.7 0.7 %reshape.246 = f32[646,128]{1,0:T(8,128)S(1)} reshape(f32[19,8,4,136]{3,2,1,0:T(4,128)S(1)} %get-tuple-element.49) | data formatting | bytes 661504 | tf_op jit(solution)/shard_map/reshape | solution.py:98
  36.5 1.5 %collective-permute-start.6 = (f32[646,128]{1,0:T(8,128)S(1)}, f32[646,128]{1,0:T(8,128)}, u32[]{:S(2)}, u32[]{:S(2)}) collective-permute-start(f32[646,128]{1,0:T(8,128)S(1)} %reshape.246), channel_id=1, source_target_pairs={{1,0},{2,1},{3,2},{5,4},{6,5},{7,6},{9,8},{10,9},{11,10},{13,12},{... | collective-permute-start | bytes 992264 | tf_op jit(solution)/shard_map/ppermute | solution.py:30
  38.0 5.3 %collective-permute-done.5 = f32[646,128]{1,0:T(8,128)S(1)} collective-permute-done((f32[646,128]{1,0:T(8,128)}, f32[646,128]{1,0:T(8,128)S(1)}, u32[]{:S(2)}, u32[]{:S(2)}) %collective-permute-start.5) | collective-permute-done | bytes 330784 | tf_op jit(solution)/shard_map/ppermute | solution.py:30
  43.3 1.0 %reshape.245 = f32[19,8,4,136]{3,2,1,0:T(4,128)S(1)} reshape(f32[646,128]{1,0:T(8,128)S(1)} %collective-permute-done.5) | data formatting | bytes 661504 | tf_op jit(solution)/shard_map/reshape | solution.py:102
  44.3 3.7 %collective-permute-done.6 = f32[646,128]{1,0:T(8,128)} collective-permute-done((f32[646,128]{1,0:T(8,128)S(1)}, f32[646,128]{1,0:T(8,128)}, u32[]{:S(2)}, u32[]{:S(2)}) %collective-permute-start.6) | collective-permute-done | bytes 330784 | tf_op jit(solution)/shard_map/ppermute | solution.py:30
  48.0 1.9 %reshape.247 = f32[19,8,4,136]{3,2,1,0:T(4,128)S(1)} reshape(f32[646,128]{1,0:T(8,128)} %collective-permute-done.6) | data formatting | bytes 661504 | tf_op jit(solution)/shard_map/reshape | solution.py:102
  50.4 4.0 %pad_maximum_fusion = f32[19,8,16,136]{3,2,1,0:T(8,128)S(1)} fusion(f32[19,8,4,136]{3,2,1,0:T(4,128)S(1)} %reshape.247, f32[19,4,8,4]{3,2,1,0:T(8,128)S(1)} %copy.27, f32[1,4,8,128]{3,2,1,0:T(8,128)S(1)} %broadcast_in_dim.103, f32[18,4,8,128]{3,2,1,0:T(8,128)S(1)} %get-tuple-element.51, f32[19,4,8,4]{3,2,1,0:T(8,128)S(1)} %copy.26, ...), kind=kLoop, calls=%fused_computation | loop fusion | flops 2976768 | bytes 2629632 | tf_op jit(solution)/shard_map/concatenate | solution.py:91
  55.2 0.4 copy-done.8
  57.3 0.3 multiply_add_fusion.2
  58.7 0.3 multiply_add_fusion.1
  60.2 0.3 multiply_add_fusion
  61.1 0.7 %dynamic-slice_multiply_fusion = f32[4,8,128]{2,1,0:T(8,128)} fusion(f32[8,16,136]{2,1,0:T(8,128)S(1)} %fusion.50, s32[]{:T(128)S(6)} %select_n.217, s32[]{:T(128)S(6)} %add.382), kind=kLoop, calls=%fused_computation.194 | loop fusion | flops 4096 | bytes 32776 | tf_op jit(solution)/shard_map/div | solution.py:297
  61.8 0.8 %pad_dynamic-slice_fusion.27 = (f32[3,4,8,128]{3,2,1,0:T(8,128)}, f32[3,4,8,128]{3,2,1,0:T(8,128)}) fusion(s32[]{:T(128)S(6)} %dynamic_slice.77, s32[]{:T(128)S(6)} %add.382, f32[3,8,16,136]{3,2,1,0:T(8,128)S(1)} %fusion.11, f32[3,8,16,136]{3,2,1,0:T(8,128)S(1)} %fusion.20), kind=kLoop, calls=%fused_computation.40 | loop fusion | bytes 516104 | tf_op jit(solution)/shard_map/slice | solution.py:291
  62.5 0.8 %pad_dynamic-slice_fusion = (f32[2,3,4,8,128]{4,3,2,1,0:T(8,128)}, f32[2,3,4,8,128]{4,3,2,1,0:T(8,128)}) fusion(s32[]{:T(128)S(6)} %dynamic_slice.77, s32[]{:T(128)S(6)} %add.382, f32[2,3,8,16,136]{4,3,2,1,0:T(8,128)S(1)} %get-tuple-element.14, f32[2,3,8,16,136]{4,3,2,1,0:T(8,128)S(1)} %get-tuple-element.13), kind=kLoop, calls=%fused_computation.2 | loop fusion | bytes 1032200 | tf_op jit(solution)/shard_map/slice | solution.py:291
  (111 shorter events, 6.6 us)
Async XLA Ops:
  0.6 18.7 %copy-start.2 = (f32[3,4,8,128]{3,2,1,0:T(8,128)S(1)}, f32[3,4,8,128]{3,2,1,0:T(8,128)}, u32[]{:S(2)}) copy-start(f32[3,4,8,128]{3,2,1,0:T(8,128)} %param.11) | copy-start | bytes 147460
  0.6 18.7 %copy-start.3 = (f32[3,4,8,128]{3,2,1,0:T(8,128)S(1)}, f32[3,4,8,128]{3,2,1,0:T(8,128)}, u32[]{:S(2)}) copy-start(f32[3,4,8,128]{3,2,1,0:T(8,128)} %param.12) | copy-start | bytes 147460
  0.7 18.7 %copy-start = (f32[2,3,4,8,128]{4,3,2,1,0:T(8,128)S(1)}, f32[2,3,4,8,128]{4,3,2,1,0:T(8,128)}, u32[]{:S(2)}) copy-start(f32[2,3,4,8,128]{4,3,2,1,0:T(8,128)} %param.13) | copy-start | bytes 294916
  0.7 18.7 %copy-start.1 = (f32[2,3,4,8,128]{4,3,2,1,0:T(8,128)S(1)}, f32[2,3,4,8,128]{4,3,2,1,0:T(8,128)}, u32[]{:S(2)}) copy-start(f32[2,3,4,8,128]{4,3,2,1,0:T(8,128)} %param.14) | copy-start | bytes 294916
  0.7 18.8 %copy-start.5 = (f32[2,8]{1,0:T(2,128)S(1)}, f32[2,8]{1,0:T(2,128)}, u32[]{:S(2)}) copy-start(f32[2,8]{1,0:T(2,128)} %param.21) | copy-start | bytes 196
  0.7 18.8 %copy-start.6 = (f32[2,8]{1,0:T(2,128)S(1)}, f32[2,8]{1,0:T(2,128)}, u32[]{:S(2)}) copy-start(f32[2,8]{1,0:T(2,128)} %param.20) | copy-start | bytes 196
  0.7 18.8 %copy-start.7 = (f32[2,8]{1,0:T(2,128)S(1)}, f32[2,8]{1,0:T(2,128)}, u32[]{:S(2)}) copy-start(f32[2,8]{1,0:T(2,128)} %param.19) | copy-start | bytes 196
  0.7 18.9 %copy-start.4 = (s32[4]{0:T(128)S(1)}, s32[4]{0:T(128)}, u32[]{:S(2)}) copy-start(s32[4]{0:T(128)} %param.16) | copy-start | bytes 52
  5.4 22.6 %collective-permute-start.1 = (f32[19,128]{0,1:T(8,128)S(1)}, f32[19,128]{0,1:T(8,128)S(1)}, u32[]{:S(2)}, u32[]{:S(2)}) collective-permute-start(f32[19,128]{0,1:T(8,128)S(1)} %bitcast.336), channel_id=1, source_target_pairs={{0,4},{4,8},{8,12},{16,20},{20,24},{24,28},{1,5},{5,9},{9,13},{17,... | collective-permute-start | bytes 29192 | tf_op jit(solution)/shard_map/ppermute | solution.py:81
  8.1 20.0 %collective-permute-start.4 = (f32[19,128]{0,1:T(8,128)S(1)}, f32[19,128]{0,1:T(8,128)S(1)}, u32[]{:S(2)}, u32[]{:S(2)}) collective-permute-start(f32[19,128]{0,1:T(8,128)S(1)} %bitcast.338), channel_id=1, source_target_pairs={{4,0},{8,4},{12,8},{20,16},{24,20},{28,24},{5,1},{9,5},{13,9},{21,... | collective-permute-start | bytes 29192 | tf_op jit(solution)/shard_map/ppermute | solution.py:81
  9.4 18.6 %collective-permute-start = (f32[19,128]{0,1:T(8,128)S(1)}, f32[19,128]{0,1:T(8,128)S(1)}, u32[]{:S(2)}, u32[]{:S(2)}) collective-permute-start(f32[19,128]{0,1:T(8,128)S(1)} %get-tuple-element.105), channel_id=1, source_target_pairs={{4,16},{8,20},{12,24},{16,4},{20,8},{24,12},{5,17},{9,21},{13,25},... | collective-permute-start | bytes 29192 | tf_op jit(solution)/shard_map/ppermute | solution.py:77
  10.1 17.9 %collective-permute-start.2 = (f32[19,128]{0,1:T(8,128)S(1)}, f32[19,128]{0,1:T(8,128)S(1)}, u32[]{:S(2)}, u32[]{:S(2)}) collective-permute-start(f32[19,128]{0,1:T(8,128)S(1)} %get-tuple-element.104), channel_id=1, source_target_pairs={{0,20},{4,24},{8,28},{20,0},{24,4},{28,8},{1,21},{5,25},{9,29},{21... | collective-permute-start | bytes 29192 | tf_op jit(solution)/shard_map/ppermute | solution.py:77
  19.4 10.4 %collective-permute-start.3 = (f32[18,4,8,128]{3,2,1,0:T(8,128)S(1)}, f32[18,4,8,128]{3,2,1,0:T(8,128)S(1)}, u32[]{:S(2)}, u32[]{:S(2)}) collective-permute-start(f32[18,4,8,128]{3,2,1,0:T(8,128)S(1)} %pad_maximum_fusion.1), channel_id=1, source_target_pairs={{0,16},{4,20},{8,24},{12,28},{16,0},{20,4},{24,8},{28,12},{1,17},{... | collective-permute-start | bytes 884744 | tf_op jit(solution)/shard_map/ppermute | solution.py:77
  32.2 11.1 %collective-permute-start.5 = (f32[646,128]{1,0:T(8,128)}, f32[646,128]{1,0:T(8,128)S(1)}, u32[]{:S(2)}, u32[]{:S(2)}) collective-permute-start(f32[646,128]{1,0:T(8,128)} %reshape.244), channel_id=1, source_target_pairs={{0,1},{1,2},{2,3},{4,5},{5,6},{6,7},{8,9},{9,10},{10,11},{12,13},{... | collective-permute-start | bytes 992264 | tf_op jit(solution)/shard_map/ppermute | solution.py:30
  36.5 11.5 %collective-permute-start.6 = (f32[646,128]{1,0:T(8,128)S(1)}, f32[646,128]{1,0:T(8,128)}, u32[]{:S(2)}, u32[]{:S(2)}) collective-permute-start(f32[646,128]{1,0:T(8,128)S(1)} %reshape.246), channel_id=1, source_target_pairs={{1,0},{2,1},{3,2},{5,4},{6,5},{7,6},{9,8},{10,9},{11,10},{13,12},{... | collective-permute-start | bytes 992264 | tf_op jit(solution)/shard_map/ppermute | solution.py:30
  55.0 0.7 %copy-start.8 = (f32[8]{0:T(128)S(1)}, f32[8]{0:T(128)}, u32[]{:S(2)}) copy-start(f32[8]{0:T(128)} %param.17) | copy-start | bytes 100
  55.0 0.7 %copy-start.9 = (f32[8]{0:T(128)S(1)}, f32[8]{0:T(128)}, u32[]{:S(2)}) copy-start(f32[8]{0:T(128)} %param.18) | copy-start | bytes 100

commit v4 on v2

--- a/solution.py
+++ b/solution.py
@@ -169,8 +169,8 @@
 
     kinds = material.astype(jnp.float32)
     state = jnp.concatenate([state, jnp.broadcast_to(kinds[None, None], (1, depth, rows, columns))], axis=0)
+    state = with_halo(state, "ty", 2, halo)
     state = with_halo(state, "tx", 3, halo)
-    state = with_halo(state, "ty", 2, halo)
     kinds = state[-1, 0].astype(jnp.int32)
     electric_b, magnetic_b = (state[0:3], state[3:6])
     polarization_b = state[6:12].reshape((2, 3) + state.shape[1:])

time: 57.7 us -> 60 us (1.040)
  waiting for transfers between devices: 11 us -> 9.56 us
  starting transfers between devices: 13.2 us -> 14.5 us
  other arithmetic: 10.1 us -> 11.3 us
  local copies, waits for them, and re-layouts: 13.7 us -> 14.9 us
    broadcast_in_dim x3, local copies, waits for them, and re-layouts: 2.27 us -> 3.91 us  [cell_lookup(): jnp.where(selector, table[:, None, None], jnp.float32(0.0))]
    ppermute x1, waiting for transfers between devices: 3.68 us -> 2.04 us  [from_offsets(): received = lax.ppermute(value, axis, pairs)]
    ppermute x4, starting transfers between devices: 11.1 us -> 12.4 us  [from_offsets(): got[k] = lax.ppermute(value, axis, pairs)]
    unnamed x6 -> x22, local copies, waits for them, and re-layouts: 0.47 us -> 1.38 us
    reshape x4 -> x2, local copies, waits for them, and re-layouts: 4.1 us -> 3.32 us  [unpacked(): return values.reshape(shape)]
    convert_element_type x1, other arithmetic: 0.08 us -> 0.81 us  [body(): kinds = state[-1, 0].astype(jnp.int32)]
    reshape x4 -> x2, local copies, waits for them, and re-layouts: 2.85 us -> 2.23 us  [packed(): return values.reshape(-1, lanes)]
  transfers between devices with their start and end apart: 5 -> 5, of which waited for: 3 -> 3; matrix products, arithmetic and copies ran while one was open for 11% -> 13% of each run, Pallas kernels for 0% -> 0%
where the time goes in v4:
time: 60 us; the launch traced here: 59.4 us
  local copies, waits for them, and re-layouts  14.9 us (25%)
  starting transfers between devices  14.5 us (24%)
  other arithmetic  11.3 us (19%)
  waiting for transfers between devices  9.56 us (16%)
  between operations  9.13 us (15%)
    ppermute x4, starting transfers between devices, from_offsets(): got[k] = lax.ppermute(value, axis, pairs)  12.4 us
    ppermute x4, waiting for transfers between devices, from_offsets(): got[k] = lax.ppermute(value, axis, pairs)  7.52 us
    broadcast_in_dim x3, local copies, waits for them, and re-layouts, cell_lookup(): jnp.where(selector, table[:, None, None], jnp.float32(0.0))  3.91 us
    reshape x2, local copies, waits for them, and re-layouts, unpacked(): return values.reshape(shape)  3.32 us
    reshape x2, local copies, waits for them, and re-layouts, packed(): return values.reshape(-1, lanes)  2.23 us
    ppermute x1, starting transfers between devices, from_offsets(): received = lax.ppermute(value, axis, pairs)  2.11 us
    ppermute x1, waiting for transfers between devices, from_offsets(): received = lax.ppermute(value, axis, pairs)  2.04 us
    concatenate x2, other arithmetic, with_halo(): return jnp.concatenate([below, cells, above], axis=dim)  1.99 us
  transfers between devices with their start and end apart: 5, of which 3 were waited for; matrix products, arithmetic and copies ran while one was open for 13% of the time, Pallas kernels for 0%

profile of v4, /device:TPU:1, one launch (start us, length us, event | category | flops | bytes accessed | tf_op | source)
XLA Modules:
  0.0 59.4 jit_solution(3721784382470595602)
XLA Ops:
  0.6 1.0 %pad_maximum_fusion.3 = f32[18,4,8,128]{3,2,1,0:T(8,128)S(1)} fusion(f32[6,4,8,128]{3,2,1,0:T(8,128)} %bitcast.344, f32[6,4,8,128]{3,2,1,0:T(8,128)} %bitcast.346, f32[3,4,8,128]{3,2,1,0:T(8,128)} %param.12, f32[3,4,8,128]{3,2,1,0:T(8,128)} %param.11), kind=kLoop, calls=%fused_computation.99 | loop fusion | flops 221184 | bytes 589824 | tf_op jit(solution)/shard_map/concatenate | solution.py:135
  1.6 2.1 %collective-permute-start = (f32[18,4,8,128]{3,2,1,0:T(8,128)S(1)}, f32[18,4,8,128]{3,2,1,0:T(8,128)S(1)}, u32[]{:S(2)}, u32[]{:S(2)}) collective-permute-start(f32[18,4,8,128]{3,2,1,0:T(8,128)S(1)} %pad_maximum_fusion.3), channel_id=1, source_target_pairs={{0,16},{16,0},{1,17},{17,1},{2,18},{18,2},{3,19},{19,3},{4,20},{20... | collective-permute-start | bytes 884744 | tf_op jit(solution)/shard_map/ppermute | solution.py:25
  3.7 0.7 %convert_element_type.20 = f32[8,128]{1,0:T(8,128)S(1)} convert(s32[8,128]{1,0:T(8,128)} %param.15) | non-fusion elementwise | flops 1024 | bytes 8192 | tf_op jit(solution)/shard_map/convert_element_type | solution.py:170
  4.4 1.3 %slice_bitcast_fusion.33 = (f32[8]{0:T(128)}, f32[8]{0:T(128)}) fusion(f32[2,8]{1,0:T(2,128)} %param.21), kind=kLoop, calls=%fused_computation.200 | loop fusion | bytes 128 | tf_op jit(solution)/shard_map/jit(_where)/broadcast_in_dim | solution.py:96
  5.7 1.3 %slice_bitcast_fusion.31 = (f32[8]{0:T(128)}, f32[8]{0:T(128)}) fusion(f32[2,8]{1,0:T(2,128)} %param.20), kind=kLoop, calls=%fused_computation.198 | loop fusion | bytes 128 | tf_op jit(solution)/shard_map/jit(_where)/broadcast_in_dim | solution.py:96
  7.0 1.3 %slice_bitcast_fusion.29 = (f32[8]{0:T(128)}, f32[8]{0:T(128)}) fusion(f32[2,8]{1,0:T(2,128)} %param.19), kind=kLoop, calls=%fused_computation.196 | loop fusion | bytes 128 | tf_op jit(solution)/shard_map/jit(_where)/broadcast_in_dim | solution.py:96
  8.4 2.0 %collective-permute-done = f32[18,4,8,128]{3,2,1,0:T(8,128)S(1)} collective-permute-done((f32[18,4,8,128]{3,2,1,0:T(8,128)S(1)}, f32[18,4,8,128]{3,2,1,0:T(8,128)S(1)}, u32[]{:S(2)}, u32[]{:S(2)}) %collective-permute-start) | collective-permute-done | bytes 294944 | tf_op jit(solution)/shard_map/ppermute | solution.py:25
  10.4 1.0 %select_select_fusion.1 = (f32[18,4,8,128]{3,2,1,0:T(8,128)S(1)}, f32[18,4,8,128]{3,2,1,0:T(8,128)S(1)}) fusion(f32[18,4,8,128]{3,2,1,0:T(8,128)S(1)} %collective-permute-done, pred[]{:T(512)S(6)} %and.62, pred[]{:T(512)S(6)} %eq.28, pred[]{:T(512)S(6)} %and.61, pred[]{:T(512)S(6)} %eq.27, pred[]{:T(512)S(6)} %eq.26, f32[6,4,8,128]{3,2,1,0:T(8,128)} %bitcast.345, ...), kind=kLoop, calls=%fused_computation.101 | loop fusion | flops 811008 | bytes 1179656 | tf_op jit(solution)/shard_map/jit(_where)/select_n | solution.py:156
  11.7 3.1 %collective-permute-start.1 = (f32[608,128]{1,0:T(8,128)S(1)}, f32[608,128]{1,0:T(8,128)S(1)}, u32[]{:S(2)}, u32[]{:S(2)}) collective-permute-start(f32[608,128]{1,0:T(8,128)S(1)} %bitcast.349), channel_id=1, source_target_pairs={{0,1},{1,2},{2,3},{4,5},{5,6},{6,7},{8,9},{9,10},{10,11},{12,13},{... | collective-permute-start | bytes 933896 | tf_op jit(solution)/shard_map/ppermute | solution.py:30
  14.8 1.3 %collective-permute-start.2 = (f32[608,128]{1,0:T(8,128)S(1)}, f32[608,128]{1,0:T(8,128)S(1)}, u32[]{:S(2)}, u32[]{:S(2)}) collective-permute-start(f32[608,128]{1,0:T(8,128)S(1)} %bitcast.348), channel_id=1, source_target_pairs={{1,0},{2,1},{3,2},{5,4},{6,5},{7,6},{9,8},{10,9},{11,10},{13,12},{... | collective-permute-start | bytes 933896 | tf_op jit(solution)/shard_map/ppermute | solution.py:30
  16.2 3.7 %collective-permute-done.1 = f32[608,128]{1,0:T(8,128)S(1)} collective-permute-done((f32[608,128]{1,0:T(8,128)S(1)}, f32[608,128]{1,0:T(8,128)S(1)}, u32[]{:S(2)}, u32[]{:S(2)}) %collective-permute-start.1) | collective-permute-done | bytes 311328 | tf_op jit(solution)/shard_map/ppermute | solution.py:30
  19.9 3.9 %collective-permute-done.2 = f32[608,128]{1,0:T(8,128)S(1)} collective-permute-done((f32[608,128]{1,0:T(8,128)S(1)}, f32[608,128]{1,0:T(8,128)S(1)}, u32[]{:S(2)}, u32[]{:S(2)}) %collective-permute-start.2) | collective-permute-done | bytes 311328 | tf_op jit(solution)/shard_map/ppermute | solution.py:30
  23.8 0.7 %copy-done = f32[608,128]{1,0:T(8,128)} copy-done((f32[608,128]{1,0:T(8,128)}, f32[608,128]{1,0:T(8,128)S(1)}, u32[]{:S(2)}) %copy-start) | copy-done | bytes 311320
  24.7 0.4 fusion.72
  25.2 1.4 %reshape.232 = f32[76,128]{1,0:T(8,128)} reshape(f32[19,8,16,4]{3,2,1,0:T(8,128)S(1)} %get-tuple-element.52) | data formatting | bytes 77824 | tf_op jit(solution)/shard_map/reshape | solution.py:47
  26.6 5.9 %collective-permute-start.3 = (f32[76,128]{1,0:T(8,128)}, f32[76,128]{1,0:T(8,128)S(1)}, u32[]{:S(2)}, u32[]{:S(2)}) collective-permute-start(f32[76,128]{1,0:T(8,128)} %reshape.232), channel_id=1, source_target_pairs={{0,4},{4,8},{8,12},{1,5},{5,9},{9,13},{2,6},{6,10},{10,14},{3,7},{... | collective-permute-start | bytes 116744 | tf_op jit(solution)/shard_map/ppermute | solution.py:30
  32.5 0.8 %reshape.234 = f32[76,128]{1,0:T(8,128)S(1)} reshape(f32[19,8,16,4]{3,2,1,0:T(8,128)S(1)} %get-tuple-element.53) | data formatting | bytes 77824 | tf_op jit(solution)/shard_map/reshape | solution.py:47
  33.3 2.1 %collective-permute-start.4 = (f32[76,128]{1,0:T(8,128)S(1)}, f32[76,128]{1,0:T(8,128)}, u32[]{:S(2)}, u32[]{:S(2)}) collective-permute-start(f32[76,128]{1,0:T(8,128)S(1)} %reshape.234), channel_id=1, source_target_pairs={{4,0},{8,4},{12,8},{5,1},{9,5},{13,9},{6,2},{10,6},{14,10},{7,3},{... | collective-permute-start | bytes 116744 | tf_op jit(solution)/shard_map/ppermute | solution.py:30
  35.4 0.6 fusion.74
  43.8 1.3 %reshape.233 = f32[19,8,16,4]{3,2,1,0:T(8,128)S(1)} reshape(f32[76,128]{1,0:T(8,128)S(1)} %collective-permute-done.3) | data formatting | bytes 77824 | tf_op jit(solution)/shard_map/reshape | solution.py:51
  45.1 2.0 %reshape.235 = f32[19,8,16,4]{3,2,1,0:T(8,128)S(1)} reshape(f32[76,128]{1,0:T(8,128)} %collective-permute-done.4) | data formatting | bytes 77824 | tf_op jit(solution)/shard_map/reshape | solution.py:51
  47.1 0.8 %fusion.61 = s32[16,136]{1,0:T(8,128)S(1)} fusion(f32[19,8,16,4]{3,2,1,0:T(8,128)S(1)} %reshape.235, f32[19,8,16,4]{3,2,1,0:T(8,128)S(1)} %reshape.233, f32[19,8,4,128]{3,2,1,0:T(4,128)} %bitcast.321, f32[19,8,4,128]{3,2,1,0:T(4,128)S(1)} %bitcast.315, f32[1,8,8,128]{3,2,1,0:T(8,128)S(1)} %broadcast_in_dim.103, f32[18,4,8,128]{3,2,1,0:T(8,128)S(1)} %get-tuple-element.57, ...), kind=kLoop, calls=%fused_computation.191 | loop fusion | flops 15232 | bytes 1331712 | tf_op jit(solution)/shard_map/convert_element_type | solution.py:174
  48.6 1.8 %pad_maximum_fusion = f32[19,8,16,136]{3,2,1,0:T(8,128)S(1)} fusion(f32[19,8,16,4]{3,2,1,0:T(8,128)S(1)} %reshape.235, f32[19,8,4,128]{3,2,1,0:T(4,128)S(1)} %bitcast.324, f32[1,8,8,128]{3,2,1,0:T(8,128)S(1)} %broadcast_in_dim.103, f32[18,4,8,128]{3,2,1,0:T(8,128)S(1)} %get-tuple-element.57, f32[18,4,8,128]{3,2,1,0:T(8,128)S(1)} %get-tuple-element.56, ...), kind=kLoop, calls=%fused_computation | loop fusion | flops 1984512 | bytes 2646016 | tf_op jit(solution)/shard_map/concatenate | solution.py:40
  50.4 0.3 subtract_bitcast_fusion.23
  51.3 0.3 copy-done.3
  52.2 0.3 multiply_add_fusion.3
  53.3 0.3 multiply_add_fusion.2
  54.8 0.3 multiply_add_fusion.1
  56.2 0.3 multiply_add_fusion
  57.1 0.7 %dynamic-slice_multiply_fusion = f32[4,8,128]{2,1,0:T(8,128)} fusion(f32[8,16,136]{2,1,0:T(8,128)S(1)} %fusion.50, s32[]{:T(128)S(6)} %select_n.137, s32[]{:T(128)S(6)} %add.350), kind=kLoop, calls=%fused_computation.189 | loop fusion | flops 4096 | bytes 32776 | tf_op jit(solution)/shard_map/div | solution.py:229
  57.8 0.8 %pad_dynamic-slice_fusion.27 = (f32[3,4,8,128]{3,2,1,0:T(8,128)}, f32[3,4,8,128]{3,2,1,0:T(8,128)}) fusion(s32[]{:T(128)S(6)} %dynamic_slice.77, s32[]{:T(128)S(6)} %add.350, f32[3,8,16,136]{3,2,1,0:T(8,128)S(1)} %fusion.11, f32[3,8,16,136]{3,2,1,0:T(8,128)S(1)} %fusion.20), kind=kLoop, calls=%fused_computation.41 | loop fusion | bytes 516104 | tf_op jit(solution)/shard_map/slice | solution.py:223
  58.6 0.8 %pad_dynamic-slice_fusion = (f32[2,3,4,8,128]{4,3,2,1,0:T(8,128)}, f32[2,3,4,8,128]{4,3,2,1,0:T(8,128)}) fusion(s32[]{:T(128)S(6)} %dynamic_slice.77, s32[]{:T(128)S(6)} %add.350, f32[2,3,8,16,136]{4,3,2,1,0:T(8,128)S(1)} %get-tuple-element.14, f32[2,3,8,16,136]{4,3,2,1,0:T(8,128)S(1)} %get-tuple-element.13), kind=kLoop, calls=%fused_computation.2 | loop fusion | bytes 1032200 | tf_op jit(solution)/shard_map/slice | solution.py:223
  (95 shorter events, 5.6 us)
Async XLA Ops:
  1.6 8.8 %collective-permute-start = (f32[18,4,8,128]{3,2,1,0:T(8,128)S(1)}, f32[18,4,8,128]{3,2,1,0:T(8,128)S(1)}, u32[]{:S(2)}, u32[]{:S(2)}) collective-permute-start(f32[18,4,8,128]{3,2,1,0:T(8,128)S(1)} %pad_maximum_fusion.3), channel_id=1, source_target_pairs={{0,16},{16,0},{1,17},{17,1},{2,18},{18,2},{3,19},{19,3},{4,20},{20... | collective-permute-start | bytes 884744 | tf_op jit(solution)/shard_map/ppermute | solution.py:25
  11.7 8.2 %collective-permute-start.1 = (f32[608,128]{1,0:T(8,128)S(1)}, f32[608,128]{1,0:T(8,128)S(1)}, u32[]{:S(2)}, u32[]{:S(2)}) collective-permute-start(f32[608,128]{1,0:T(8,128)S(1)} %bitcast.349), channel_id=1, source_target_pairs={{0,1},{1,2},{2,3},{4,5},{5,6},{6,7},{8,9},{9,10},{10,11},{12,13},{... | collective-permute-start | bytes 933896 | tf_op jit(solution)/shard_map/ppermute | solution.py:30
  14.8 8.9 %collective-permute-start.2 = (f32[608,128]{1,0:T(8,128)S(1)}, f32[608,128]{1,0:T(8,128)S(1)}, u32[]{:S(2)}, u32[]{:S(2)}) collective-permute-start(f32[608,128]{1,0:T(8,128)S(1)} %bitcast.348), channel_id=1, source_target_pairs={{1,0},{2,1},{3,2},{5,4},{6,5},{7,6},{9,8},{10,9},{11,10},{13,12},{... | collective-permute-start | bytes 933896 | tf_op jit(solution)/shard_map/ppermute | solution.py:30
  23.8 0.7 %copy-start = (f32[608,128]{1,0:T(8,128)}, f32[608,128]{1,0:T(8,128)S(1)}, u32[]{:S(2)}) copy-start(f32[608,128]{1,0:T(8,128)S(1)} %collective-permute-done.2) | copy-start | bytes 933892
  26.6 8.8 %copy-start.2 = (s32[4]{0:T(128)S(1)}, s32[4]{0:T(128)}, u32[]{:S(2)}) copy-start(s32[4]{0:T(128)} %param.16) | copy-start | bytes 52
  26.6 17.2 %collective-permute-start.3 = (f32[76,128]{1,0:T(8,128)}, f32[76,128]{1,0:T(8,128)S(1)}, u32[]{:S(2)}, u32[]{:S(2)}) collective-permute-start(f32[76,128]{1,0:T(8,128)} %reshape.232), channel_id=1, source_target_pairs={{0,4},{4,8},{8,12},{1,5},{5,9},{9,13},{2,6},{6,10},{10,14},{3,7},{... | collective-permute-start | bytes 116744 | tf_op jit(solution)/shard_map/ppermute | solution.py:30
  33.3 11.8 %collective-permute-start.4 = (f32[76,128]{1,0:T(8,128)S(1)}, f32[76,128]{1,0:T(8,128)}, u32[]{:S(2)}, u32[]{:S(2)}) collective-permute-start(f32[76,128]{1,0:T(8,128)S(1)} %reshape.234), channel_id=1, source_target_pairs={{4,0},{8,4},{12,8},{5,1},{9,5},{13,9},{6,2},{10,6},{14,10},{7,3},{... | collective-permute-start | bytes 116744 | tf_op jit(solution)/shard_map/ppermute | solution.py:30
  47.1 1.0 %copy-start.1 = (f32[608,128]{1,0:T(8,128)S(1)}, f32[608,128]{1,0:T(8,128)}, u32[]{:S(2)}) copy-start(f32[608,128]{1,0:T(8,128)} %copy-done) | copy-start | bytes 933892
  51.0 0.6 %copy-start.3 = (f32[8]{0:T(128)S(1)}, f32[8]{0:T(128)}, u32[]{:S(2)}) copy-start(f32[8]{0:T(128)} %get-tuple-element.104) | copy-start | bytes 100
  51.0 0.6 %copy-start.4 = (f32[8]{0:T(128)S(1)}, f32[8]{0:T(128)}, u32[]{:S(2)}) copy-start(f32[8]{0:T(128)} %get-tuple-element.105) | copy-start | bytes 100
  51.0 0.7 %copy-start.5 = (f32[8]{0:T(128)S(1)}, f32[8]{0:T(128)}, u32[]{:S(2)}) copy-start(f32[8]{0:T(128)} %get-tuple-element.106) | copy-start | bytes 100
  51.0 0.7 %copy-start.6 = (f32[8]{0:T(128)S(1)}, f32[8]{0:T(128)}, u32[]{:S(2)}) copy-start(f32[8]{0:T(128)} %get-tuple-element.107) | copy-start | bytes 100
  51.0 0.7 %copy-start.7 = (f32[8]{0:T(128)S(1)}, f32[8]{0:T(128)}, u32[]{:S(2)}) copy-start(f32[8]{0:T(128)} %get-tuple-element.108) | copy-start | bytes 100
  51.1 0.6 %copy-start.8 = (f32[8]{0:T(128)S(1)}, f32[8]{0:T(128)}, u32[]{:S(2)}) copy-start(f32[8]{0:T(128)} %get-tuple-element.109) | copy-start | bytes 100
  51.1 0.7 %copy-start.9 = (f32[8]{0:T(128)S(1)}, f32[8]{0:T(128)}, u32[]{:S(2)}) copy-start(f32[8]{0:T(128)} %param.17) | copy-start | bytes 100
  51.1 0.7 %copy-start.10 = (f32[8]{0:T(128)S(1)}, f32[8]{0:T(128)}, u32[]{:S(2)}) copy-start(f32[8]{0:T(128)} %param.18) | copy-start | bytes 100

commit v5 on v4

--- a/solution.py
+++ b/solution.py
@@ -35,8 +35,16 @@
     length = cells.shape[dim]
     head = lax.slice_in_dim(cells, 0, width, axis=dim)
     tail = lax.slice_in_dim(cells, length - width, length, axis=dim)
-    below = unpacked(from_offsets(packed(tail), axis, (-1,))[-1], tail.shape)
-    above = unpacked(from_offsets(packed(head), axis, (1,))[1], head.shape)
+    if dim == cells.ndim - 1:
+        def pack(values):
+            return values.reshape(-1, width).T
+
+        def unpack(values, shape):
+            return values.T.reshape(shape)
+    else:
+        pack, unpack = (packed, unpacked)
+    below = unpack(from_offsets(pack(tail), axis, (-1,))[-1], tail.shape)
+    above = unpack(from_offsets(pack(head), axis, (1,))[1], head.shape)
     return jnp.concatenate([below, cells, above], axis=dim)
 
 

time: 60 us -> 57.3 us (0.955)
  local copies, waits for them, and re-layouts: 14.9 us -> 12.4 us
    reshape x4, local copies, waits for them, and re-layouts: 5.55 us -> 3.01 us  [the longest x2 1.61 us: unpack(): return values.T.reshape(shape)]
  transfers between devices with their start and end apart: 5 -> 5, of which waited for: 3 -> 3; matrix products, arithmetic and copies ran while one was open for 13% -> 11% of each run, Pallas kernels for 0% -> 0%
where the time goes in v5:
time: 57.3 us; the launch traced here: 56.7 us
  starting transfers between devices  14.4 us (25%)
  local copies, waits for them, and re-layouts  12.4 us (22%)
  other arithmetic  11.3 us (20%)
  waiting for transfers between devices  9.56 us (17%)
  between operations  9.13 us (16%)
    ppermute x4, starting transfers between devices, from_offsets(): got[k] = lax.ppermute(value, axis, pairs)  12.3 us
    ppermute x4, waiting for transfers between devices, from_offsets(): got[k] = lax.ppermute(value, axis, pairs)  7.52 us
    broadcast_in_dim x3, local copies, waits for them, and re-layouts, cell_lookup(): jnp.where(selector, table[:, None, None], jnp.float32(0.0))  3.91 us
    ppermute x1, starting transfers between devices, from_offsets(): received = lax.ppermute(value, axis, pairs)  2.11 us
    ppermute x1, waiting for transfers between devices, from_offsets(): received = lax.ppermute(value, axis, pairs)  2.04 us
    concatenate x2, other arithmetic, with_halo(): return jnp.concatenate([below, cells, above], axis=dim)  1.99 us
    reshape x2, local copies, waits for them, and re-layouts, unpack(): return values.T.reshape(shape)  1.61 us
    slice x2, local copies, waits for them, and re-layouts, own(): return lax.slice_in_dim(values, halo, halo + columns, axis=dim + 2)  1.58 us
  transfers between devices with their start and end apart: 5, of which 3 were waited for; matrix products, arithmetic and copies ran while one was open for 11% of the time, Pallas kernels for 0%

profile of v5, /device:TPU:1, one launch (start us, length us, event | category | flops | bytes accessed | tf_op | source)
XLA Modules:
  0.0 56.7 jit_solution(7742447986748954066)
XLA Ops:
  0.6 1.0 %pad_maximum_fusion.3 = f32[18,4,8,128]{3,2,1,0:T(8,128)S(1)} fusion(f32[6,4,8,128]{3,2,1,0:T(8,128)} %bitcast.360, f32[6,4,8,128]{3,2,1,0:T(8,128)} %bitcast.362, f32[3,4,8,128]{3,2,1,0:T(8,128)} %param.12, f32[3,4,8,128]{3,2,1,0:T(8,128)} %param.11), kind=kLoop, calls=%fused_computation.99 | loop fusion | flops 221184 | bytes 589824 | tf_op jit(solution)/shard_map/concatenate | solution.py:143
  1.6 2.1 %collective-permute-start = (f32[18,4,8,128]{3,2,1,0:T(8,128)S(1)}, f32[18,4,8,128]{3,2,1,0:T(8,128)S(1)}, u32[]{:S(2)}, u32[]{:S(2)}) collective-permute-start(f32[18,4,8,128]{3,2,1,0:T(8,128)S(1)} %pad_maximum_fusion.3), channel_id=1, source_target_pairs={{0,16},{16,0},{1,17},{17,1},{2,18},{18,2},{3,19},{19,3},{4,20},{20... | collective-permute-start | bytes 884744 | tf_op jit(solution)/shard_map/ppermute | solution.py:25
  3.7 0.7 %convert_element_type.20 = f32[8,128]{1,0:T(8,128)S(1)} convert(s32[8,128]{1,0:T(8,128)} %param.15) | non-fusion elementwise | flops 1024 | bytes 8192 | tf_op jit(solution)/shard_map/convert_element_type | solution.py:178
  4.4 1.3 %slice_bitcast_fusion.33 = (f32[8]{0:T(128)}, f32[8]{0:T(128)}) fusion(f32[2,8]{1,0:T(2,128)} %param.21), kind=kLoop, calls=%fused_computation.200 | loop fusion | bytes 128 | tf_op jit(solution)/shard_map/jit(_where)/broadcast_in_dim | solution.py:104
  5.7 1.3 %slice_bitcast_fusion.31 = (f32[8]{0:T(128)}, f32[8]{0:T(128)}) fusion(f32[2,8]{1,0:T(2,128)} %param.20), kind=kLoop, calls=%fused_computation.198 | loop fusion | bytes 128 | tf_op jit(solution)/shard_map/jit(_where)/broadcast_in_dim | solution.py:104
  7.0 1.3 %slice_bitcast_fusion.29 = (f32[8]{0:T(128)}, f32[8]{0:T(128)}) fusion(f32[2,8]{1,0:T(2,128)} %param.19), kind=kLoop, calls=%fused_computation.196 | loop fusion | bytes 128 | tf_op jit(solution)/shard_map/jit(_where)/broadcast_in_dim | solution.py:104
  8.4 2.0 %collective-permute-done = f32[18,4,8,128]{3,2,1,0:T(8,128)S(1)} collective-permute-done((f32[18,4,8,128]{3,2,1,0:T(8,128)S(1)}, f32[18,4,8,128]{3,2,1,0:T(8,128)S(1)}, u32[]{:S(2)}, u32[]{:S(2)}) %collective-permute-start) | collective-permute-done | bytes 294944 | tf_op jit(solution)/shard_map/ppermute | solution.py:25
  10.4 1.0 %select_select_fusion.1 = (f32[18,4,8,128]{3,2,1,0:T(8,128)S(1)}, f32[18,4,8,128]{3,2,1,0:T(8,128)S(1)}) fusion(f32[18,4,8,128]{3,2,1,0:T(8,128)S(1)} %collective-permute-done, pred[]{:T(512)S(6)} %and.62, pred[]{:T(512)S(6)} %eq.28, pred[]{:T(512)S(6)} %and.61, pred[]{:T(512)S(6)} %eq.27, pred[]{:T(512)S(6)} %eq.26, f32[6,4,8,128]{3,2,1,0:T(8,128)} %bitcast.361, ...), kind=kLoop, calls=%fused_computation.101 | loop fusion | flops 811008 | bytes 1179656 | tf_op jit(solution)/shard_map/jit(_where)/select_n | solution.py:164
  11.7 3.1 %collective-permute-start.1 = (f32[608,128]{1,0:T(8,128)S(1)}, f32[608,128]{1,0:T(8,128)S(1)}, u32[]{:S(2)}, u32[]{:S(2)}) collective-permute-start(f32[608,128]{1,0:T(8,128)S(1)} %bitcast.365), channel_id=1, source_target_pairs={{0,1},{1,2},{2,3},{4,5},{5,6},{6,7},{8,9},{9,10},{10,11},{12,13},{... | collective-permute-start | bytes 933896 | tf_op jit(solution)/shard_map/ppermute | solution.py:30
  14.8 1.3 %collective-permute-start.2 = (f32[608,128]{1,0:T(8,128)S(1)}, f32[608,128]{1,0:T(8,128)S(1)}, u32[]{:S(2)}, u32[]{:S(2)}) collective-permute-start(f32[608,128]{1,0:T(8,128)S(1)} %bitcast.364), channel_id=1, source_target_pairs={{1,0},{2,1},{3,2},{5,4},{6,5},{7,6},{9,8},{10,9},{11,10},{13,12},{... | collective-permute-start | bytes 933896 | tf_op jit(solution)/shard_map/ppermute | solution.py:30
  16.2 3.7 %collective-permute-done.1 = f32[608,128]{1,0:T(8,128)S(1)} collective-permute-done((f32[608,128]{1,0:T(8,128)S(1)}, f32[608,128]{1,0:T(8,128)S(1)}, u32[]{:S(2)}, u32[]{:S(2)}) %collective-permute-start.1) | collective-permute-done | bytes 311328 | tf_op jit(solution)/shard_map/ppermute | solution.py:30
  19.9 3.9 %collective-permute-done.2 = f32[608,128]{1,0:T(8,128)S(1)} collective-permute-done((f32[608,128]{1,0:T(8,128)S(1)}, f32[608,128]{1,0:T(8,128)S(1)}, u32[]{:S(2)}, u32[]{:S(2)}) %collective-permute-start.2) | collective-permute-done | bytes 311328 | tf_op jit(solution)/shard_map/ppermute | solution.py:30
  23.8 0.7 %copy-done = f32[608,128]{1,0:T(8,128)} copy-done((f32[608,128]{1,0:T(8,128)}, f32[608,128]{1,0:T(8,128)S(1)}, u32[]{:S(2)}) %copy-start) | copy-done | bytes 311320
  24.7 0.4 fusion.72
  25.2 1.0 %copy.30 = f32[2432,4]{0,1:T(4,128)} copy(f32[2432,4]{1,0:T(8,128)S(1)} %bitcast.341) | data formatting | bytes 77824 | tf_op jit(solution)/shard_map/reshape | solution.py:40
  26.2 4.8 %collective-permute-start.4 = (f32[4,2432]{1,0:T(4,128)}, f32[4,2432]{1,0:T(4,128)S(1)}, u32[]{:S(2)}, u32[]{:S(2)}) collective-permute-start(f32[4,2432]{1,0:T(4,128)} %bitcast.372), channel_id=1, source_target_pairs={{4,0},{8,4},{12,8},{5,1},{9,5},{13,9},{6,2},{10,6},{14,10},{7,3},{... | collective-permute-start | bytes 116744 | tf_op jit(solution)/shard_map/ppermute | solution.py:30
  31.0 0.4 copy.28
  31.3 3.1 %collective-permute-start.3 = (f32[4,2432]{1,0:T(4,128)S(1)}, f32[4,2432]{1,0:T(4,128)}, u32[]{:S(2)}, u32[]{:S(2)}) collective-permute-start(f32[4,2432]{1,0:T(4,128)S(1)} %bitcast.374), channel_id=1, source_target_pairs={{0,4},{4,8},{8,12},{1,5},{5,9},{9,13},{2,6},{6,10},{10,14},{3,7},{... | collective-permute-start | bytes 116744 | tf_op jit(solution)/shard_map/ppermute | solution.py:30
  34.4 0.6 %fusion.74 = (s32[1]{0:T(128)}, s32[1]{0:T(128)}, s32[1]{0:T(128)}, s32[1]{0:T(128)}) fusion(s32[4]{0:T(128)S(1)} %copy-done.2), kind=kLoop, calls=%fused_computation.205 | loop fusion | bytes 32 | tf_op jit(solution)/shard_map/slice | solution.py:222
  42.8 0.4 copy.31
  43.2 1.2 %copy.29 = f32[2432,4]{1,0:T(8,128)S(1)} copy(f32[2432,4]{0,1:T(4,128)} %bitcast.8) | data formatting | bytes 77824 | tf_op jit(solution)/shard_map/reshape | solution.py:43
  44.5 0.8 %fusion.61 = s32[16,136]{1,0:T(8,128)S(1)} fusion(f32[19,8,16,4]{3,2,1,0:T(8,128)S(1)} %bitcast.318, f32[19,8,16,4]{3,2,1,0:T(8,128)S(1)} %bitcast.323, f32[19,8,4,128]{3,2,1,0:T(4,128)} %bitcast.335, f32[19,8,4,128]{3,2,1,0:T(4,128)S(1)} %bitcast.329, f32[1,8,8,128]{3,2,1,0:T(8,128)S(1)} %broadcast_in_dim.103, f32[18,4,8,128]{3,2,1,0:T(8,128)S(1)} %get-tuple-element.57, ...), kind=kLoop, calls=%fused_computation.191 | loop fusion | flops 15232 | bytes 1331712 | tf_op jit(solution)/shard_map/convert_element_type | solution.py:182
  45.9 1.8 %pad_maximum_fusion = f32[19,8,16,136]{3,2,1,0:T(8,128)S(1)} fusion(f32[19,8,16,4]{3,2,1,0:T(8,128)S(1)} %bitcast.321, f32[19,8,4,128]{3,2,1,0:T(4,128)S(1)} %bitcast.338, f32[1,8,8,128]{3,2,1,0:T(8,128)S(1)} %broadcast_in_dim.103, f32[18,4,8,128]{3,2,1,0:T(8,128)S(1)} %get-tuple-element.57, f32[18,4,8,128]{3,2,1,0:T(8,128)S(1)} %get-tuple-element.56, ...), kind=kLoop, calls=%fused_computation | loop fusion | flops 1984512 | bytes 2646016 | tf_op jit(solution)/shard_map/concatenate | solution.py:48
  47.7 0.3 subtract_bitcast_fusion.23
  48.6 0.3 copy-done.3
  49.5 0.3 multiply_add_fusion.3
  50.7 0.3 multiply_add_fusion.2
  52.1 0.3 multiply_add_fusion.1
  53.5 0.3 multiply_add_fusion
  54.5 0.7 %dynamic-slice_multiply_fusion = f32[4,8,128]{2,1,0:T(8,128)} fusion(f32[8,16,136]{2,1,0:T(8,128)S(1)} %fusion.50, s32[]{:T(128)S(6)} %select_n.137, s32[]{:T(128)S(6)} %add.350), kind=kLoop, calls=%fused_computation.189 | loop fusion | flops 4096 | bytes 32776 | tf_op jit(solution)/shard_map/div | solution.py:237
  55.1 0.8 %pad_dynamic-slice_fusion.27 = (f32[3,4,8,128]{3,2,1,0:T(8,128)}, f32[3,4,8,128]{3,2,1,0:T(8,128)}) fusion(s32[]{:T(128)S(6)} %dynamic_slice.77, s32[]{:T(128)S(6)} %add.350, f32[3,8,16,136]{3,2,1,0:T(8,128)S(1)} %fusion.11, f32[3,8,16,136]{3,2,1,0:T(8,128)S(1)} %fusion.20), kind=kLoop, calls=%fused_computation.41 | loop fusion | bytes 516104 | tf_op jit(solution)/shard_map/slice | solution.py:231
  55.9 0.8 %pad_dynamic-slice_fusion = (f32[2,3,4,8,128]{4,3,2,1,0:T(8,128)}, f32[2,3,4,8,128]{4,3,2,1,0:T(8,128)}) fusion(s32[]{:T(128)S(6)} %dynamic_slice.77, s32[]{:T(128)S(6)} %add.350, f32[2,3,8,16,136]{4,3,2,1,0:T(8,128)S(1)} %get-tuple-element.14, f32[2,3,8,16,136]{4,3,2,1,0:T(8,128)S(1)} %get-tuple-element.13), kind=kLoop, calls=%fused_computation.2 | loop fusion | bytes 1032200 | tf_op jit(solution)/shard_map/slice | solution.py:231
  (95 shorter events, 5.6 us)
Async XLA Ops:
  1.6 8.8 %collective-permute-start = (f32[18,4,8,128]{3,2,1,0:T(8,128)S(1)}, f32[18,4,8,128]{3,2,1,0:T(8,128)S(1)}, u32[]{:S(2)}, u32[]{:S(2)}) collective-permute-start(f32[18,4,8,128]{3,2,1,0:T(8,128)S(1)} %pad_maximum_fusion.3), channel_id=1, source_target_pairs={{0,16},{16,0},{1,17},{17,1},{2,18},{18,2},{3,19},{19,3},{4,20},{20... | collective-permute-start | bytes 884744 | tf_op jit(solution)/shard_map/ppermute | solution.py:25
  11.7 8.2 %collective-permute-start.1 = (f32[608,128]{1,0:T(8,128)S(1)}, f32[608,128]{1,0:T(8,128)S(1)}, u32[]{:S(2)}, u32[]{:S(2)}) collective-permute-start(f32[608,128]{1,0:T(8,128)S(1)} %bitcast.365), channel_id=1, source_target_pairs={{0,1},{1,2},{2,3},{4,5},{5,6},{6,7},{8,9},{9,10},{10,11},{12,13},{... | collective-permute-start | bytes 933896 | tf_op jit(solution)/shard_map/ppermute | solution.py:30
  14.8 8.9 %collective-permute-start.2 = (f32[608,128]{1,0:T(8,128)S(1)}, f32[608,128]{1,0:T(8,128)S(1)}, u32[]{:S(2)}, u32[]{:S(2)}) collective-permute-start(f32[608,128]{1,0:T(8,128)S(1)} %bitcast.364), channel_id=1, source_target_pairs={{1,0},{2,1},{3,2},{5,4},{6,5},{7,6},{9,8},{10,9},{11,10},{13,12},{... | collective-permute-start | bytes 933896 | tf_op jit(solution)/shard_map/ppermute | solution.py:30
  23.8 0.7 %copy-start = (f32[608,128]{1,0:T(8,128)}, f32[608,128]{1,0:T(8,128)S(1)}, u32[]{:S(2)}) copy-start(f32[608,128]{1,0:T(8,128)S(1)} %collective-permute-done.2) | copy-start | bytes 933892
  26.2 8.2 %copy-start.2 = (s32[4]{0:T(128)S(1)}, s32[4]{0:T(128)}, u32[]{:S(2)}) copy-start(s32[4]{0:T(128)} %param.16) | copy-start | bytes 52
  26.2 16.6 %collective-permute-start.4 = (f32[4,2432]{1,0:T(4,128)}, f32[4,2432]{1,0:T(4,128)S(1)}, u32[]{:S(2)}, u32[]{:S(2)}) collective-permute-start(f32[4,2432]{1,0:T(4,128)} %bitcast.372), channel_id=1, source_target_pairs={{4,0},{8,4},{12,8},{5,1},{9,5},{13,9},{6,2},{10,6},{14,10},{7,3},{... | collective-permute-start | bytes 116744 | tf_op jit(solution)/shard_map/ppermute | solution.py:30
  31.3 11.9 %collective-permute-start.3 = (f32[4,2432]{1,0:T(4,128)S(1)}, f32[4,2432]{1,0:T(4,128)}, u32[]{:S(2)}, u32[]{:S(2)}) collective-permute-start(f32[4,2432]{1,0:T(4,128)S(1)} %bitcast.374), channel_id=1, source_target_pairs={{0,4},{4,8},{8,12},{1,5},{5,9},{9,13},{2,6},{6,10},{10,14},{3,7},{... | collective-permute-start | bytes 116744 | tf_op jit(solution)/shard_map/ppermute | solution.py:30
  44.4 1.0 %copy-start.1 = (f32[608,128]{1,0:T(8,128)S(1)}, f32[608,128]{1,0:T(8,128)}, u32[]{:S(2)}) copy-start(f32[608,128]{1,0:T(8,128)} %copy-done) | copy-start | bytes 933892
  48.3 0.6 %copy-start.3 = (f32[8]{0:T(128)S(1)}, f32[8]{0:T(128)}, u32[]{:S(2)}) copy-start(f32[8]{0:T(128)} %get-tuple-element.104) | copy-start | bytes 100
  48.3 0.6 %copy-start.4 = (f32[8]{0:T(128)S(1)}, f32[8]{0:T(128)}, u32[]{:S(2)}) copy-start(f32[8]{0:T(128)} %get-tuple-element.105) | copy-start | bytes 100
  48.3 0.7 %copy-start.5 = (f32[8]{0:T(128)S(1)}, f32[8]{0:T(128)}, u32[]{:S(2)}) copy-start(f32[8]{0:T(128)} %get-tuple-element.106) | copy-start | bytes 100
  48.3 0.7 %copy-start.6 = (f32[8]{0:T(128)S(1)}, f32[8]{0:T(128)}, u32[]{:S(2)}) copy-start(f32[8]{0:T(128)} %get-tuple-element.107) | copy-start | bytes 100
  48.4 0.7 %copy-start.7 = (f32[8]{0:T(128)S(1)}, f32[8]{0:T(128)}, u32[]{:S(2)}) copy-start(f32[8]{0:T(128)} %get-tuple-element.108) | copy-start | bytes 100
  48.4 0.6 %copy-start.8 = (f32[8]{0:T(128)S(1)}, f32[8]{0:T(128)}, u32[]{:S(2)}) copy-start(f32[8]{0:T(128)} %get-tuple-element.109) | copy-start | bytes 100
  48.4 0.7 %copy-start.9 = (f32[8]{0:T(128)S(1)}, f32[8]{0:T(128)}, u32[]{:S(2)}) copy-start(f32[8]{0:T(128)} %param.17) | copy-start | bytes 100
  48.4 0.7 %copy-start.10 = (f32[8]{0:T(128)S(1)}, f32[8]{0:T(128)}, u32[]{:S(2)}) copy-start(f32[8]{0:T(128)} %param.18) | copy-start | bytes 100

commit v6 on v5

--- a/solution.py
+++ b/solution.py
@@ -1,6 +1,10 @@
+import functools
+
 import jax
 import jax.numpy as jnp
 from jax import lax
+from jax.experimental import pallas as pl
+from jax.experimental.pallas import tpu as pltpu
 from jax.sharding import PartitionSpec as P
 
 STEPS = 4
@@ -31,7 +35,7 @@
     return got
 
 
-def with_halo(cells, axis, dim, width):
+def with_ring(cells, axis, dim, width, total):
     length = cells.shape[dim]
     head = lax.slice_in_dim(cells, 0, width, axis=dim)
     tail = lax.slice_in_dim(cells, length - width, length, axis=dim)
@@ -45,7 +49,23 @@
         pack, unpack = (packed, unpacked)
     below = unpack(from_offsets(pack(tail), axis, (-1,))[-1], tail.shape)
     above = unpack(from_offsets(pack(head), axis, (1,))[1], head.shape)
-    return jnp.concatenate([below, cells, above], axis=dim)
+    parts = [cells, above]
+    gap = total - length - 2 * width
+    if gap:
+        gap_shape = list(cells.shape)
+        gap_shape[dim] = gap
+        parts.append(jnp.zeros(gap_shape, cells.dtype))
+    parts.append(below)
+    return jnp.concatenate(parts, axis=dim)
+
+
+def ring_coordinates(start, length, width, total):
+    marks = lax.broadcasted_iota(jnp.int32, (total,), 0)
+    return jnp.where(
+        marks < length + width,
+        start + marks,
+        jnp.where(marks >= total - width, start - (total - marks), -1),
+    )
 
 
 def packed(values):
@@ -177,69 +197,147 @@
 
     kinds = material.astype(jnp.float32)
     state = jnp.concatenate([state, jnp.broadcast_to(kinds[None, None], (1, depth, rows, columns))], axis=0)
-    state = with_halo(state, "ty", 2, halo)
-    state = with_halo(state, "tx", 3, halo)
+    ring_rows = -(-(rows + 2 * halo) // 8) * 8
+    ring_columns = -(-(columns + 2 * halo) // 128) * 128
+    state = with_ring(state, "ty", 2, halo, ring_rows)
+    state = with_ring(state, "tx", 3, halo, ring_columns)
     kinds = state[-1, 0].astype(jnp.int32)
-    electric_b, magnetic_b = (state[0:3], state[3:6])
-    polarization_b = state[6:12].reshape((2, 3) + state.shape[1:])
-    current_b = state[12:18].reshape((2, 3) + state.shape[1:])
-
-    ext_rows, ext_columns = (rows + 2 * halo, columns + 2 * halo)
+
+    place_z = base_z + lax.broadcasted_iota(jnp.int32, (depth,), 0)
+    place_y = ring_coordinates(at_y * rows, rows, halo, ring_rows)
+    place_x = ring_coordinates(at_x * columns, columns, halo, ring_columns)
     keep_mask = (
-        inside_range(base_z, depth, total_z, 0, 3)
-        & inside_range(at_y * rows - halo, ext_rows, total_y, 1, 3)
-        & inside_range(at_x * columns - halo, ext_columns, total_x, 2, 3)
+        ((place_z >= 0) & (place_z < total_z))[:, None, None]
+        & ((place_y >= 0) & (place_y < total_y))[None, :, None]
+        & ((place_x >= 0) & (place_x < total_x))[None, None, :]
     ).astype(jnp.float32)
 
     materials_count = permittivity.shape[0]
     selector = kinds[None] == lax.broadcasted_iota(
-        jnp.int32, (materials_count, ext_rows, ext_columns), 0
+        jnp.int32, (materials_count, ring_rows, ring_columns), 0
     )
     eps_cell = cell_lookup(selector, permittivity)
     kerr_cell = cell_lookup(selector, nonlinear)
-    strength = jnp.stack(
-        [cell_lookup(selector, pole_strength[0]), cell_lookup(selector, pole_strength[1])]
-    )[:, None, None]
-    frequency = jnp.stack(
-        [cell_lookup(selector, pole_frequency[0]), cell_lookup(selector, pole_frequency[1])]
-    )
-    damping = jnp.stack(
-        [cell_lookup(selector, pole_damping[0]), cell_lookup(selector, pole_damping[1])]
-    )
-    half_damp = 0.5 * time_step * damping
-    keep_rate = ((1.0 - half_damp) / (1.0 + half_damp))[:, None, None]
-    drive_rate = (time_step * frequency * frequency / (1.0 + half_damp))[:, None, None]
-
-    for moment in range(STEPS):
-        magnetic_b = (magnetic_b - time_step * curl_forward(electric_b)) * keep_mask[None]
-        squared = jnp.sum(electric_b * electric_b, axis=0)
-        current_b = keep_rate * current_b + drive_rate * (strength * electric_b[None] - polarization_b)
-        polarization_b = polarization_b + time_step * current_b
-        electric_b = electric_b + time_step * (
-            curl_backward(magnetic_b) - current_b[0] - current_b[1]
-        ) / (eps_cell + kerr_cell * squared)
-        electric_b = electric_b * keep_mask[None]
-        amount = advance[moment]
-        electric_b = advance_planes(electric_b, amount, 1)
-        magnetic_b = advance_planes(magnetic_b, amount, 1)
-        polarization_b = advance_planes(polarization_b, amount, 2)
-        current_b = advance_planes(current_b, amount, 2)
-
-    def own(values, dim):
-        values = lax.dynamic_slice_in_dim(values, own_z, planes, axis=dim)
-        values = lax.slice_in_dim(values, halo, halo + rows, axis=dim + 1)
-        return lax.slice_in_dim(values, halo, halo + columns, axis=dim + 2)
-
-    density = eps_cell * jnp.sum(electric_b * electric_b, axis=0) + jnp.sum(
-        magnetic_b * magnetic_b, axis=0
-    )
+    strength = [cell_lookup(selector, pole_strength[p]) for p in range(2)]
+    frequency = [cell_lookup(selector, pole_frequency[p]) for p in range(2)]
+    half_damp = [0.5 * time_step * cell_lookup(selector, pole_damping[p]) for p in range(2)]
+    keep_rate = [(1.0 - h) / (1.0 + h) for h in half_damp]
+    drive_rate = [time_step * f * f / (1.0 + h) for f, h in zip(frequency, half_damp)]
+    coefficients = jnp.stack([eps_cell, kerr_cell] + strength + keep_rate + drive_rate)
+
+    own_at = jnp.reshape(jnp.asarray(own_z, jnp.int32), (1,))
+    fields = state.shape[0] - 1
+    final, density = pl.pallas_call(
+        functools.partial(steps_kernel, planes=planes, rows=rows, columns=columns),
+        out_shape=(
+            jax.ShapeDtypeStruct((fields, planes, rows, columns), jnp.float32),
+            jax.ShapeDtypeStruct((depth, rows, columns), jnp.float32),
+        ),
+        in_specs=[
+            pl.BlockSpec(memory_space=pltpu.SMEM),
+            pl.BlockSpec(memory_space=pltpu.SMEM),
+            pl.BlockSpec(memory_space=pltpu.VMEM),
+            pl.BlockSpec(memory_space=pltpu.VMEM),
+            pl.BlockSpec(memory_space=pltpu.VMEM),
+        ],
+        out_specs=(
+            pl.BlockSpec(memory_space=pltpu.VMEM),
+            pl.BlockSpec(memory_space=pltpu.VMEM),
+        ),
+        scratch_shapes=[pltpu.VMEM((fields, depth + WSHIFT, ring_rows, ring_columns), jnp.float32)],
+    )(advance, own_at, state, coefficients, keep_mask)
+
     if whole_column:
-        column_energy = own(jnp.cumsum(density, axis=0), 0) / jnp.float32(total_z)
+        column_energy = lax.dynamic_slice_in_dim(jnp.cumsum(density, axis=0), own_z, planes, axis=0)
+        column_energy = column_energy / jnp.float32(total_z)
     else:
-        density = own(density, 0)
+        density = lax.slice_in_dim(density, own_z, own_z + planes, axis=0)
         prefix = entering(jnp.sum(density, axis=0), "prop")
         column_energy = (prefix[None] + jnp.cumsum(density, axis=0)) / jnp.float32(total_z)
-    return (own(electric_b, 1), own(magnetic_b, 1), own(polarization_b, 2), own(current_b, 2), column_energy)
+    pole_shape = (2, 3) + final.shape[1:]
+    return (
+        final[0:3],
+        final[3:6],
+        final[6:12].reshape(pole_shape),
+        final[12:18].reshape(pole_shape),
+        column_energy,
+    )
+
+
+def steps_kernel(advance_ref, own_ref, state_ref, coef_ref, mask_ref, out_ref, density_ref, work_ref, *, planes, rows, columns):
+    fields, depth = (work_ref.shape[0], work_ref.shape[1] - WSHIFT)
+    work_ref[:, depth:] = jnp.zeros((fields, WSHIFT) + work_ref.shape[2:], jnp.float32)
+    eps_cell, kerr_cell = (coef_ref[0], coef_ref[1])
+    strength, keep_rate, drive_rate = (
+        (coef_ref[2], coef_ref[3]),
+        (coef_ref[4], coef_ref[5]),
+        (coef_ref[6], coef_ref[7]),
+    )
+    keep_mask = mask_ref[...]
+    zero_plane = jnp.zeros((1,) + keep_mask.shape[1:], jnp.float32)
+    ring_rows, ring_columns = keep_mask.shape[1:]
+
+    def up_z(f):
+        return jnp.concatenate([f[1:], zero_plane], axis=0)
+
+    def down_z(f):
+        return jnp.concatenate([zero_plane, f[:-1]], axis=0)
+
+    def up_y(f):
+        return pltpu.roll(f, ring_rows - 1, 1)
+
+    def down_y(f):
+        return pltpu.roll(f, 1, 1)
+
+    def up_x(f):
+        return pltpu.roll(f, ring_columns - 1, 2)
+
+    def down_x(f):
+        return pltpu.roll(f, 1, 2)
+
+    amount = None
+    for moment in range(STEPS):
+        if amount is None:
+            values = [state_ref[c] for c in range(fields)]
+        else:
+            values = [work_ref[c, pl.ds(amount, depth)] for c in range(fields)]
+        e_x, e_y, e_z = values[0:3]
+        h_x, h_y, h_z = values[3:6]
+        pol = [values[6:9], values[9:12]]
+        cur = [values[12:15], values[15:18]]
+        h_x = (h_x - time_step * ((up_y(e_z) - e_z) - (up_z(e_y) - e_y))) * keep_mask
+        h_y = (h_y - time_step * ((up_z(e_x) - e_x) - (up_x(e_z) - e_z))) * keep_mask
+        h_z = (h_z - time_step * ((up_x(e_y) - e_y) - (up_y(e_x) - e_x))) * keep_mask
+        squared = e_x * e_x + e_y * e_y + e_z * e_z
+        electric = (e_x, e_y, e_z)
+        for p in range(2):
+            for c in range(3):
+                cur[p][c] = keep_rate[p] * cur[p][c] + drive_rate[p] * (strength[p] * electric[c] - pol[p][c])
+                pol[p][c] = pol[p][c] + time_step * cur[p][c]
+        curl_x = (h_z - down_y(h_z)) - (h_y - down_z(h_y))
+        curl_y = (h_x - down_z(h_x)) - (h_z - down_x(h_z))
+        curl_z = (h_y - down_x(h_y)) - (h_x - down_y(h_x))
+        denominator = eps_cell + kerr_cell * squared
+        new_e = [
+            (field + time_step * (curl - cur[0][c] - cur[1][c]) / denominator) * keep_mask
+            for c, (field, curl) in enumerate(zip(electric, (curl_x, curl_y, curl_z)))
+        ]
+        results = new_e + [h_x, h_y, h_z] + pol[0] + pol[1] + cur[0] + cur[1]
+        for c in range(fields):
+            work_ref[c, 0:depth] = results[c]
+        amount = advance_ref[moment]
+
+    start = amount + own_ref[0]
+    for c in range(fields):
+        out_ref[c] = work_ref[c, pl.ds(start, planes), 0:rows, 0:columns]
+    squared_e = None
+    squared_h = None
+    for c in range(3):
+        e = work_ref[c, pl.ds(amount, depth), 0:rows, 0:columns]
+        h = work_ref[3 + c, pl.ds(amount, depth), 0:rows, 0:columns]
+        squared_e = e * e if squared_e is None else squared_e + e * e
+        squared_h = h * h if squared_h is None else squared_h + h * h
+    density_ref[...] = eps_cell[0:rows, 0:columns][None] * squared_e + squared_h
 
 
 def solution(mesh):

time: 57.3 us -> 48.7 us (0.85)
  the two profiles are of different devices: /device:TPU:1 before, /device:TPU:28 now
where the time goes in v6:
time: 48.7 us; the launch traced here: 48.2 us
  waiting for transfers between devices  14.8 us (30%)
  local copies, waits for them, and re-layouts  10.2 us (21%)
  starting transfers between devices  9.58 us (20%)
  other arithmetic  7.55 us (16%)
  Pallas kernels  5.18 us (11%)
  between operations  0.88 us (2%)
    ppermute x4, waiting for transfers between devices, from_offsets(): got[k] = lax.ppermute(value, axis, pairs)  9.08 us
    ppermute x4, starting transfers between devices, from_offsets(): got[k] = lax.ppermute(value, axis, pairs)  8.02 us
    ppermute x1, waiting for transfers between devices, from_offsets(): received = lax.ppermute(value, axis, pairs)  5.71 us
    pallas_call x1, Pallas kernels, body(): pl.pallas_call(functools.partial(steps_kernel, planes=planes, rows=rows,...  5.18 us
    transpose x2, local copies, waits for them, and re-layouts, unpack(): return values.T.reshape(shape)  2.96 us
    concatenate x2, other arithmetic, with_ring(): return jnp.concatenate(parts, axis=dim)  2.44 us
    unnamed x16, local copies, waits for them, and re-layouts  1.94 us
    slice x1, local copies, waits for them, and re-layouts, body(): final[12:18].reshape(pole_shape)  1.63 us
  transfers between devices with their start and end apart: 5, of which 4 were waited for; matrix products, arithmetic and copies ran while one was open for 9% of the time, Pallas kernels for 0%

profile of v6, /device:TPU:28, one launch (start us, length us, event | category | flops | bytes accessed | tf_op | source)
XLA Modules:
  0.0 48.2 jit_solution(6957363766404747048)
XLA Ops:
  0.6 1.0 %pad_maximum_fusion.3 = f32[18,4,8,128]{3,2,1,0:T(8,128)S(1)} fusion(f32[6,4,8,128]{3,2,1,0:T(8,128)} %bitcast.66, f32[6,4,8,128]{3,2,1,0:T(8,128)} %bitcast.68, f32[3,4,8,128]{3,2,1,0:T(8,128)} %param.12, f32[3,4,8,128]{3,2,1,0:T(8,128)} %param.11), kind=kLoop, calls=%fused_computation.3 | loop fusion | flops 221184 | bytes 589824 | tf_op jit(solution)/shard_map/concatenate | solution.py:163
  1.6 1.6 %collective-permute-start = (f32[18,4,8,128]{3,2,1,0:T(8,128)S(1)}, f32[18,4,8,128]{3,2,1,0:T(8,128)S(1)}, u32[]{:S(2)}, u32[]{:S(2)}) collective-permute-start(f32[18,4,8,128]{3,2,1,0:T(8,128)S(1)} %pad_maximum_fusion.3), channel_id=1, source_target_pairs={{0,16},{16,0},{1,17},{17,1},{2,18},{18,2},{3,19},{19,3},{4,20},{20... | collective-permute-start | bytes 884744 | tf_op jit(solution)/shard_map/ppermute | solution.py:29
  3.2 0.1 broadcast_and_fusion
  3.2 0.7 %convert_element_type.16 = f32[8,128]{1,0:T(8,128)S(1)} convert(s32[8,128]{1,0:T(8,128)} %param.15) | non-fusion elementwise | flops 1024 | bytes 8192 | tf_op jit(solution)/shard_map/convert_element_type | solution.py:198
  3.9 0.8 %slice_bitcast_fusion.1 = (f32[8]{0:T(128)S(1)}, f32[8]{0:T(128)S(1)}, f32[8]{0:T(128)S(1)}, f32[8]{0:T(128)S(1)}) fusion(f32[2,8]{1,0:T(2,128)} %param.20, f32[2,8]{1,0:T(2,128)} %param.21), kind=kLoop, calls=%fused_computation.42 | loop fusion | bytes 256 | tf_op jit(solution)/shard_map/jit(_where)/broadcast_in_dim | solution.py:124
  4.7 5.7 %collective-permute-done = f32[18,4,8,128]{3,2,1,0:T(8,128)S(1)} collective-permute-done((f32[18,4,8,128]{3,2,1,0:T(8,128)S(1)}, f32[18,4,8,128]{3,2,1,0:T(8,128)S(1)}, u32[]{:S(2)}, u32[]{:S(2)}) %collective-permute-start) | collective-permute-done | bytes 294944 | tf_op jit(solution)/shard_map/ppermute | solution.py:29
  10.4 1.0 %select_select_fusion.1 = (f32[18,4,8,128]{3,2,1,0:T(8,128)S(1)}, f32[18,4,8,128]{3,2,1,0:T(8,128)S(1)}) fusion(f32[18,4,8,128]{3,2,1,0:T(8,128)S(1)} %collective-permute-done, pred[]{:T(512)S(6)} %and.56, pred[]{:T(512)S(6)} %eq.28, pred[]{:T(512)S(6)} %and.55, pred[]{:T(512)S(6)} %eq.27, pred[]{:T(512)S(6)} %eq.26, f32[6,4,8,128]{3,2,1,0:T(8,128)} %bitcast.67, ...), kind=kLoop, calls=%fused_computation.5 | loop fusion | flops 811008 | bytes 1179656 | tf_op jit(solution)/shard_map/jit(_where)/select_n | solution.py:184
  11.5 0.1 fusion.4
  11.7 2.4 %collective-permute-start.1 = (f32[608,128]{1,0:T(8,128)S(1)}, f32[608,128]{1,0:T(8,128)S(1)}, u32[]{:S(2)}, u32[]{:S(2)}) collective-permute-start(f32[608,128]{1,0:T(8,128)S(1)} %bitcast.71), channel_id=1, source_target_pairs={{1,0},{2,1},{3,2},{5,4},{6,5},{7,6},{9,8},{10,9},{11,10},{13,12},{... | collective-permute-start | bytes 933896 | tf_op jit(solution)/shard_map/ppermute | solution.py:34
  14.0 1.3 %collective-permute-start.2 = (f32[608,128]{1,0:T(8,128)S(1)}, f32[608,128]{1,0:T(8,128)S(1)}, u32[]{:S(2)}, u32[]{:S(2)}) collective-permute-start(f32[608,128]{1,0:T(8,128)S(1)} %bitcast.70), channel_id=1, source_target_pairs={{0,1},{1,2},{2,3},{4,5},{5,6},{6,7},{8,9},{9,10},{10,11},{12,13},{... | collective-permute-start | bytes 933896 | tf_op jit(solution)/shard_map/ppermute | solution.py:34
  15.4 0.7 %and_convert_fusion.mask_ref = f32[8,16,256]{2,1,0:T(8,128)} fusion(pred[256]{0:T(512)(128)(4,1)S(1)} %compare_and_fusion, pred[8,16]{1,0:T(8,128)(4,1)S(1)} %broadcast_and_fusion), kind=kLoop, calls=%fused_computation.15 | loop fusion | flops 65536 | bytes 131456 | tf_op jit(solution)/shard_map/convert_element_type | solution.py:213
  16.1 3.7 %collective-permute-done.1 = f32[608,128]{1,0:T(8,128)S(1)} collective-permute-done((f32[608,128]{1,0:T(8,128)S(1)}, f32[608,128]{1,0:T(8,128)S(1)}, u32[]{:S(2)}, u32[]{:S(2)}) %collective-permute-start.1) | collective-permute-done | bytes 311328 | tf_op jit(solution)/shard_map/ppermute | solution.py:34
  19.7 4.1 %collective-permute-done.2 = f32[608,128]{1,0:T(8,128)S(1)} collective-permute-done((f32[608,128]{1,0:T(8,128)S(1)}, f32[608,128]{1,0:T(8,128)S(1)}, u32[]{:S(2)}, u32[]{:S(2)}) %collective-permute-start.2) | collective-permute-done | bytes 311328 | tf_op jit(solution)/shard_map/ppermute | solution.py:34
  23.9 0.7 %copy-done.1 = f32[608,128]{1,0:T(8,128)} copy-done((f32[608,128]{1,0:T(8,128)}, f32[608,128]{1,0:T(8,128)S(1)}, u32[]{:S(2)}) %copy-start.1) | copy-done | bytes 311320
  24.6 0.2 pad_maximum_fusion.1
  24.8 0.4 fusion.3
  25.2 0.4 copy.20
  25.6 1.9 %collective-permute-start.3 = (f32[4,2432]{1,0:T(4,128)S(1)}, f32[4,2432]{1,0:T(4,128)S(1)}, u32[]{:S(2)}, u32[]{:S(2)}) collective-permute-start(f32[4,2432]{1,0:T(4,128)S(1)} %bitcast.74), channel_id=1, source_target_pairs={{4,0},{8,4},{12,8},{5,1},{9,5},{13,9},{6,2},{10,6},{14,10},{7,3},{... | collective-permute-start | bytes 116744 | tf_op jit(solution)/shard_map/ppermute | solution.py:34
  27.5 0.4 copy.22
  27.9 2.4 %collective-permute-start.4 = (f32[4,2432]{1,0:T(4,128)S(1)}, f32[4,2432]{1,0:T(4,128)S(1)}, u32[]{:S(2)}, u32[]{:S(2)}) collective-permute-start(f32[4,2432]{1,0:T(4,128)S(1)} %bitcast.76), channel_id=1, source_target_pairs={{0,4},{4,8},{8,12},{1,5},{5,9},{9,13},{2,6},{6,10},{10,14},{3,7},{... | collective-permute-start | bytes 116744 | tf_op jit(solution)/shard_map/ppermute | solution.py:34
  30.4 0.1 pad.6.clone
  30.5 1.5 %copy.21 = f32[2432,4]{1,0:T(8,128)} copy(f32[2432,4]{0,1:T(4,128)S(1)} %bitcast.75) | data formatting | bytes 77824 | tf_op jit(solution)/shard_map/transpose | solution.py:47
  32.0 1.3 %collective-permute-done.4 = f32[4,2432]{1,0:T(4,128)S(1)} collective-permute-done((f32[4,2432]{1,0:T(4,128)S(1)}, f32[4,2432]{1,0:T(4,128)S(1)}, u32[]{:S(2)}, u32[]{:S(2)}) %collective-permute-start.4) | collective-permute-done | bytes 38944 | tf_op jit(solution)/shard_map/ppermute | solution.py:34
  33.2 1.5 %copy.23 = f32[2432,4]{1,0:T(8,128)} copy(f32[2432,4]{0,1:T(4,128)S(1)} %bitcast.77) | data formatting | bytes 77824 | tf_op jit(solution)/shard_map/transpose | solution.py:47
  34.7 2.3 %pad_maximum_fusion.state_ref = f32[19,8,16,256]{3,2,1,0:T(8,128)S(1)} fusion(f32[19,8,16,4]{3,2,1,0:T(8,128)} %bitcast.59, f32[19,8,16,4]{3,2,1,0:T(8,128)} %bitcast.58, f32[19,8,4,128]{3,2,1,0:T(4,128)} %bitcast.65, f32[19,8,4,128]{3,2,1,0:T(4,128)S(1)} %bitcast.63, f32[1,8,8,128]{3,2,1,0:T(8,128)S(1)} %broadcast_in_dim.89, ...), kind=kLoop, calls=%fused_computation | loop fusion | flops 4358144 | bytes 3814400 | tf_op jit(solution)/shard_map/concatenate | solution.py:59
  37.0 0.1 select_reduce_fusion
  37.3 1.1 %copy-done = f32[19,8,16,256]{3,2,1,0:T(8,128)} copy-done((f32[19,8,16,256]{3,2,1,0:T(8,128)}, f32[19,8,16,256]{3,2,1,0:T(8,128)S(1)}, u32[]{:S(2)}) %copy-start) | copy-done | bytes 2490392
  38.5 5.2 %shard_map.146 = (f32[18,4,8,128]{3,2,1,0:T(8,128)}, f32[8,8,128]{2,1,0:T(8,128)}) custom-call(s32[4]{0:T(128)} %advance_ref.1, s32[1]{0:T(128)} %bitcast.own_ref, f32[19,8,16,256]{3,2,1,0:T(8,128)} %copy-done, f32[8,16,256]{2,1,0:T(8,128)} %copy-done.2, f32[8,16,256]{2,1,0:T(8,128)} %and_convert_fusion.mask_ref), custom_call_target="tpu_custom_call" | custom-call | tf_op jit(solution)/shard_map/pallas_call | solution.py:230
  43.7 1.6 %fusion.5 = (f32[6,4,8,128]{3,2,1,0:T(8,128)}, f32[6,4,8,128]{3,2,1,0:T(8,128)}) fusion(f32[18,4,8,128]{3,2,1,0:T(8,128)} %get-tuple-element.7), kind=kLoop, calls=%fused_computation.49 | loop fusion | bytes 393216 | tf_op jit(solution)/shard_map/slice | solution.py:262
  45.3 1.5 %fusion.6 = (f32[3,4,8,128]{3,2,1,0:T(8,128)}, f32[3,4,8,128]{3,2,1,0:T(8,128)}) fusion(f32[18,4,8,128]{3,2,1,0:T(8,128)} %get-tuple-element.7), kind=kLoop, calls=%fused_computation.50 | loop fusion | bytes 196608 | tf_op jit(solution)/shard_map/slice | solution.py:260
  46.8 0.8 %fusion.7 = f32[8,8,128]{2,1,0:T(8,128)S(1)} fusion(f32[8,8,128]{2,1,0:T(8,128)} %get-tuple-element.8), kind=kOutput, calls=%fused_computation.51 | output fusion | flops 57344 | bytes 65536 | tf_op jit(solution)/shard_map/jit(cumsum)/reduce_window_sum | solution.py:251
  47.5 0.6 %dynamic-slice_multiply_fusion = f32[4,8,128]{2,1,0:T(8,128)} fusion(f32[8,8,128]{2,1,0:T(8,128)S(1)} %fusion.7, s32[]{:T(128)S(6)} %select_n.138), kind=kLoop, calls=%fused_computation.32 | loop fusion | flops 4096 | bytes 32772 | tf_op jit(solution)/shard_map/div | solution.py:252
  (27 shorter events, 0.2 us)
Async XLA Ops:
  1.6 8.8 %collective-permute-start = (f32[18,4,8,128]{3,2,1,0:T(8,128)S(1)}, f32[18,4,8,128]{3,2,1,0:T(8,128)S(1)}, u32[]{:S(2)}, u32[]{:S(2)}) collective-permute-start(f32[18,4,8,128]{3,2,1,0:T(8,128)S(1)} %pad_maximum_fusion.3), channel_id=1, source_target_pairs={{0,16},{16,0},{1,17},{17,1},{2,18},{18,2},{3,19},{19,3},{4,20},{20... | collective-permute-start | bytes 884744 | tf_op jit(solution)/shard_map/ppermute | solution.py:29
  11.7 8.1 %collective-permute-start.1 = (f32[608,128]{1,0:T(8,128)S(1)}, f32[608,128]{1,0:T(8,128)S(1)}, u32[]{:S(2)}, u32[]{:S(2)}) collective-permute-start(f32[608,128]{1,0:T(8,128)S(1)} %bitcast.71), channel_id=1, source_target_pairs={{1,0},{2,1},{3,2},{5,4},{6,5},{7,6},{9,8},{10,9},{11,10},{13,12},{... | collective-permute-start | bytes 933896 | tf_op jit(solution)/shard_map/ppermute | solution.py:34
  14.0 9.8 %collective-permute-start.2 = (f32[608,128]{1,0:T(8,128)S(1)}, f32[608,128]{1,0:T(8,128)S(1)}, u32[]{:S(2)}, u32[]{:S(2)}) collective-permute-start(f32[608,128]{1,0:T(8,128)S(1)} %bitcast.70), channel_id=1, source_target_pairs={{0,1},{1,2},{2,3},{4,5},{5,6},{6,7},{8,9},{9,10},{10,11},{12,13},{... | collective-permute-start | bytes 933896 | tf_op jit(solution)/shard_map/ppermute | solution.py:34
  23.9 0.7 %copy-start.1 = (f32[608,128]{1,0:T(8,128)}, f32[608,128]{1,0:T(8,128)S(1)}, u32[]{:S(2)}) copy-start(f32[608,128]{1,0:T(8,128)S(1)} %collective-permute-done.2) | copy-start | bytes 933892
  25.2 5.1 %copy-start.3 = (f32[2,8]{1,0:T(2,128)S(1)}, f32[2,8]{1,0:T(2,128)}, u32[]{:S(2)}) copy-start(f32[2,8]{1,0:T(2,128)} %param.19) | copy-start | bytes 196
  25.6 4.9 %collective-permute-start.3 = (f32[4,2432]{1,0:T(4,128)S(1)}, f32[4,2432]{1,0:T(4,128)S(1)}, u32[]{:S(2)}, u32[]{:S(2)}) collective-permute-start(f32[4,2432]{1,0:T(4,128)S(1)} %bitcast.74), channel_id=1, source_target_pairs={{4,0},{8,4},{12,8},{5,1},{9,5},{13,9},{6,2},{10,6},{14,10},{7,3},{... | collective-permute-start | bytes 116744 | tf_op jit(solution)/shard_map/ppermute | solution.py:34
  27.9 5.3 %collective-permute-start.4 = (f32[4,2432]{1,0:T(4,128)S(1)}, f32[4,2432]{1,0:T(4,128)S(1)}, u32[]{:S(2)}, u32[]{:S(2)}) collective-permute-start(f32[4,2432]{1,0:T(4,128)S(1)} %bitcast.76), channel_id=1, source_target_pairs={{0,4},{4,8},{8,12},{1,5},{5,9},{9,13},{2,6},{6,10},{10,14},{3,7},{... | collective-permute-start | bytes 116744 | tf_op jit(solution)/shard_map/ppermute | solution.py:34
  34.7 2.3 %copy-start.4 = (f32[8]{0:T(128)S(1)}, f32[8]{0:T(128)}, u32[]{:S(2)}) copy-start(f32[8]{0:T(128)} %param.18) | copy-start | bytes 100
  34.7 2.3 %copy-start.5 = (f32[8]{0:T(128)S(1)}, f32[8]{0:T(128)}, u32[]{:S(2)}) copy-start(f32[8]{0:T(128)} %param.17) | copy-start | bytes 100
  37.0 1.5 %copy-start = (f32[19,8,16,256]{3,2,1,0:T(8,128)}, f32[19,8,16,256]{3,2,1,0:T(8,128)S(1)}, u32[]{:S(2)}) copy-start(f32[19,8,16,256]{3,2,1,0:T(8,128)S(1)} %pad_maximum_fusion.state_ref) | copy-start | bytes 7471108
  37.3 1.2 %copy-start.2 = (f32[8,16,256]{2,1,0:T(8,128)}, f32[8,16,256]{2,1,0:T(8,128)S(1)}, u32[]{:S(2)}) copy-start(f32[8,16,256]{2,1,0:T(8,128)S(1)} %constant_dynamic-update-slice_fusion.coef_ref) | copy-start | bytes 393220

commit v7 on v6

--- a/solution.py
+++ b/solution.py
@@ -227,11 +227,17 @@
 
     own_at = jnp.reshape(jnp.asarray(own_z, jnp.int32), (1,))
     fields = state.shape[0] - 1
-    final, density = pl.pallas_call(
-        functools.partial(steps_kernel, planes=planes, rows=rows, columns=columns),
+    block = (planes, rows, columns)
+    outs = pl.pallas_call(
+        functools.partial(
+            steps_kernel, planes=planes, rows=rows, columns=columns, whole=whole_column, total=total_z
+        ),
         out_shape=(
-            jax.ShapeDtypeStruct((fields, planes, rows, columns), jnp.float32),
-            jax.ShapeDtypeStruct((depth, rows, columns), jnp.float32),
+            jax.ShapeDtypeStruct((3,) + block, jnp.float32),
+            jax.ShapeDtypeStruct((3,) + block, jnp.float32),
+            jax.ShapeDtypeStruct((2, 3) + block, jnp.float32),
+            jax.ShapeDtypeStruct((2, 3) + block, jnp.float32),
+            jax.ShapeDtypeStruct(block, jnp.float32),
         ),
         in_specs=[
             pl.BlockSpec(memory_space=pltpu.SMEM),
@@ -240,31 +246,24 @@
             pl.BlockSpec(memory_space=pltpu.VMEM),
             pl.BlockSpec(memory_space=pltpu.VMEM),
         ],
-        out_specs=(
-            pl.BlockSpec(memory_space=pltpu.VMEM),
-            pl.BlockSpec(memory_space=pltpu.VMEM),
-        ),
-        scratch_shapes=[pltpu.VMEM((fields, depth + WSHIFT, ring_rows, ring_columns), jnp.float32)],
+        out_specs=tuple(pl.BlockSpec(memory_space=pltpu.VMEM) for _ in range(5)),
+        scratch_shapes=[
+            pltpu.VMEM((fields, depth + WSHIFT, ring_rows, ring_columns), jnp.float32),
+            pltpu.VMEM((depth, rows, columns), jnp.float32),
+        ],
     )(advance, own_at, state, coefficients, keep_mask)
-
-    if whole_column:
-        column_energy = lax.dynamic_slice_in_dim(jnp.cumsum(density, axis=0), own_z, planes, axis=0)
-        column_energy = column_energy / jnp.float32(total_z)
-    else:
-        density = lax.slice_in_dim(density, own_z, own_z + planes, axis=0)
-        prefix = entering(jnp.sum(density, axis=0), "prop")
-        column_energy = (prefix[None] + jnp.cumsum(density, axis=0)) / jnp.float32(total_z)
-    pole_shape = (2, 3) + final.shape[1:]
-    return (
-        final[0:3],
-        final[3:6],
-        final[6:12].reshape(pole_shape),
-        final[12:18].reshape(pole_shape),
-        column_energy,
-    )
-
-
-def steps_kernel(advance_ref, own_ref, state_ref, coef_ref, mask_ref, out_ref, density_ref, work_ref, *, planes, rows, columns):
+    electric_o, magnetic_o, polarization_o, current_o, column_energy = outs
+    if not whole_column:
+        prefix = entering(jnp.sum(column_energy, axis=0), "prop")
+        column_energy = (prefix[None] + jnp.cumsum(column_energy, axis=0)) / jnp.float32(total_z)
+    return (electric_o, magnetic_o, polarization_o, current_o, column_energy)
+
+
+def steps_kernel(
+    advance_ref, own_ref, state_ref, coef_ref, mask_ref,
+    electric_ref, magnetic_ref, polarization_ref, current_ref, energy_ref,
+    work_ref, running_ref, *, planes, rows, columns, whole, total,
+):
     fields, depth = (work_ref.shape[0], work_ref.shape[1] - WSHIFT)
     work_ref[:, depth:] = jnp.zeros((fields, WSHIFT) + work_ref.shape[2:], jnp.float32)
     eps_cell, kerr_cell = (coef_ref[0], coef_ref[1])
@@ -328,16 +327,32 @@
         amount = advance_ref[moment]
 
     start = amount + own_ref[0]
-    for c in range(fields):
-        out_ref[c] = work_ref[c, pl.ds(start, planes), 0:rows, 0:columns]
+    for c in range(3):
+        electric_ref[c] = work_ref[c, pl.ds(start, planes), 0:rows, 0:columns]
+        magnetic_ref[c] = work_ref[3 + c, pl.ds(start, planes), 0:rows, 0:columns]
+        for p in range(2):
+            polarization_ref[p, c] = work_ref[6 + 3 * p + c, pl.ds(start, planes), 0:rows, 0:columns]
+            current_ref[p, c] = work_ref[12 + 3 * p + c, pl.ds(start, planes), 0:rows, 0:columns]
+    eps_own = eps_cell[0:rows, 0:columns]
+    reach = depth if whole else planes
+    first = amount if whole else start
     squared_e = None
     squared_h = None
     for c in range(3):
-        e = work_ref[c, pl.ds(amount, depth), 0:rows, 0:columns]
-        h = work_ref[3 + c, pl.ds(amount, depth), 0:rows, 0:columns]
+        e = work_ref[c, pl.ds(first, reach), 0:rows, 0:columns]
+        h = work_ref[3 + c, pl.ds(first, reach), 0:rows, 0:columns]
         squared_e = e * e if squared_e is None else squared_e + e * e
         squared_h = h * h if squared_h is None else squared_h + h * h
-    density_ref[...] = eps_cell[0:rows, 0:columns][None] * squared_e + squared_h
+    density = eps_own[None] * squared_e + squared_h
+    if whole:
+        total_so_far = density[0]
+        running_ref[0] = total_so_far
+        for z in range(1, depth):
+            total_so_far = total_so_far + density[z]
+            running_ref[z] = total_so_far
+        energy_ref[...] = running_ref[pl.ds(own_ref[0], planes)] / jnp.float32(total)
+    else:
+        energy_ref[...] = density
 
 
 def solution(mesh):

time: 48.7 us -> 44 us (0.903)
  local copies, waits for them, and re-layouts: 10.2 us -> 7.08 us
  other arithmetic: 7.55 us -> 6.19 us
    slice x2 -> x0, local copies, waits for them, and re-layouts: 3.09 us -> none  [the longest x1 1.63 us: body(): final[12:18].reshape(pole_shape)]
    another operation x1 -> x0, other arithmetic: 0.77 us -> none  [body(): jnp.cumsum(density, axis=0)]
    div x1 -> x0, other arithmetic: 0.61 us -> none  [body(): column_energy = column_energy / jnp.float32(total_z)]
  transfers between devices with their start and end apart: 5 -> 5, of which waited for: 4 -> 4; matrix products, arithmetic and copies ran while one was open for 9% -> 10% of each run, Pallas kernels for 0% -> 0%
where the time goes in v7:
time: 44 us; the launch traced here: 43.6 us
  waiting for transfers between devices  14.8 us (34%)
  starting transfers between devices  9.58 us (22%)
  local copies, waits for them, and re-layouts  7.08 us (16%)
  other arithmetic  6.19 us (14%)
  Pallas kernels  5.12 us (12%)
  between operations  0.88 us (2%)
    ppermute x4, waiting for transfers between devices, from_offsets(): got[k] = lax.ppermute(value, axis, pairs)  9.07 us
    ppermute x4, starting transfers between devices, from_offsets(): got[k] = lax.ppermute(value, axis, pairs)  8.02 us
    ppermute x1, waiting for transfers between devices, from_offsets(): received = lax.ppermute(value, axis, pairs)  5.71 us
    pallas_call x1, Pallas kernels, body(): pl.pallas_call(functools.partial(steps_kernel, planes=planes, rows=rows,...  5.12 us
    transpose x2, local copies, waits for them, and re-layouts, unpack(): return values.T.reshape(shape)  2.96 us
    concatenate x2, other arithmetic, with_ring(): return jnp.concatenate(parts, axis=dim)  2.44 us
    unnamed x16, local copies, waits for them, and re-layouts  1.94 us
    ppermute x1, starting transfers between devices, from_offsets(): received = lax.ppermute(value, axis, pairs)  1.56 us
  transfers between devices with their start and end apart: 5, of which 4 were waited for; matrix products, arithmetic and copies ran while one was open for 10% of the time, Pallas kernels for 0%

profile of v7, /device:TPU:28, one launch (start us, length us, event | category | flops | bytes accessed | tf_op | source)
XLA Modules:
  0.0 43.6 jit_solution(10346954249824308834)
XLA Ops:
  0.6 1.0 %pad_maximum_fusion.3 = f32[18,4,8,128]{3,2,1,0:T(8,128)S(1)} fusion(f32[6,4,8,128]{3,2,1,0:T(8,128)} %bitcast.63, f32[6,4,8,128]{3,2,1,0:T(8,128)} %bitcast.65, f32[3,4,8,128]{3,2,1,0:T(8,128)} %param.12, f32[3,4,8,128]{3,2,1,0:T(8,128)} %param.11), kind=kLoop, calls=%fused_computation.3 | loop fusion | flops 221184 | bytes 589824 | tf_op jit(solution)/shard_map/concatenate | solution.py:163
  1.6 1.6 %collective-permute-start = (f32[18,4,8,128]{3,2,1,0:T(8,128)S(1)}, f32[18,4,8,128]{3,2,1,0:T(8,128)S(1)}, u32[]{:S(2)}, u32[]{:S(2)}) collective-permute-start(f32[18,4,8,128]{3,2,1,0:T(8,128)S(1)} %pad_maximum_fusion.3), channel_id=1, source_target_pairs={{0,16},{16,0},{1,17},{17,1},{2,18},{18,2},{3,19},{19,3},{4,20},{20... | collective-permute-start | bytes 884744 | tf_op jit(solution)/shard_map/ppermute | solution.py:29
  3.2 0.1 broadcast_and_fusion
  3.2 0.7 %convert_element_type.16 = f32[8,128]{1,0:T(8,128)S(1)} convert(s32[8,128]{1,0:T(8,128)} %param.15) | non-fusion elementwise | flops 1024 | bytes 8192 | tf_op jit(solution)/shard_map/convert_element_type | solution.py:198
  3.9 0.8 %slice_bitcast_fusion.1 = (f32[8]{0:T(128)S(1)}, f32[8]{0:T(128)S(1)}, f32[8]{0:T(128)S(1)}, f32[8]{0:T(128)S(1)}) fusion(f32[2,8]{1,0:T(2,128)} %param.20, f32[2,8]{1,0:T(2,128)} %param.21), kind=kLoop, calls=%fused_computation.41 | loop fusion | bytes 256 | tf_op jit(solution)/shard_map/jit(_where)/broadcast_in_dim | solution.py:124
  4.7 5.7 %collective-permute-done = f32[18,4,8,128]{3,2,1,0:T(8,128)S(1)} collective-permute-done((f32[18,4,8,128]{3,2,1,0:T(8,128)S(1)}, f32[18,4,8,128]{3,2,1,0:T(8,128)S(1)}, u32[]{:S(2)}, u32[]{:S(2)}) %collective-permute-start) | collective-permute-done | bytes 294944 | tf_op jit(solution)/shard_map/ppermute | solution.py:29
  10.4 1.0 %select_select_fusion.1 = (f32[18,4,8,128]{3,2,1,0:T(8,128)S(1)}, f32[18,4,8,128]{3,2,1,0:T(8,128)S(1)}) fusion(f32[18,4,8,128]{3,2,1,0:T(8,128)S(1)} %collective-permute-done, pred[]{:T(512)S(6)} %and.56, pred[]{:T(512)S(6)} %eq.28, pred[]{:T(512)S(6)} %and.55, pred[]{:T(512)S(6)} %eq.27, pred[]{:T(512)S(6)} %eq.26, f32[6,4,8,128]{3,2,1,0:T(8,128)} %bitcast.64, ...), kind=kLoop, calls=%fused_computation.5 | loop fusion | flops 811008 | bytes 1179656 | tf_op jit(solution)/shard_map/jit(_where)/select_n | solution.py:184
  11.5 0.1 fusion.4
  11.7 2.4 %collective-permute-start.1 = (f32[608,128]{1,0:T(8,128)S(1)}, f32[608,128]{1,0:T(8,128)S(1)}, u32[]{:S(2)}, u32[]{:S(2)}) collective-permute-start(f32[608,128]{1,0:T(8,128)S(1)} %bitcast.68), channel_id=1, source_target_pairs={{1,0},{2,1},{3,2},{5,4},{6,5},{7,6},{9,8},{10,9},{11,10},{13,12},{... | collective-permute-start | bytes 933896 | tf_op jit(solution)/shard_map/ppermute | solution.py:34
  14.0 1.3 %collective-permute-start.2 = (f32[608,128]{1,0:T(8,128)S(1)}, f32[608,128]{1,0:T(8,128)S(1)}, u32[]{:S(2)}, u32[]{:S(2)}) collective-permute-start(f32[608,128]{1,0:T(8,128)S(1)} %bitcast.67), channel_id=1, source_target_pairs={{0,1},{1,2},{2,3},{4,5},{5,6},{6,7},{8,9},{9,10},{10,11},{12,13},{... | collective-permute-start | bytes 933896 | tf_op jit(solution)/shard_map/ppermute | solution.py:34
  15.4 0.7 %and_convert_fusion.mask_ref = f32[8,16,256]{2,1,0:T(8,128)} fusion(pred[256]{0:T(512)(128)(4,1)S(1)} %compare_and_fusion, pred[8,16]{1,0:T(8,128)(4,1)S(1)} %broadcast_and_fusion), kind=kLoop, calls=%fused_computation.15 | loop fusion | flops 65536 | bytes 131456 | tf_op jit(solution)/shard_map/convert_element_type | solution.py:213
  16.1 3.6 %collective-permute-done.1 = f32[608,128]{1,0:T(8,128)S(1)} collective-permute-done((f32[608,128]{1,0:T(8,128)S(1)}, f32[608,128]{1,0:T(8,128)S(1)}, u32[]{:S(2)}, u32[]{:S(2)}) %collective-permute-start.1) | collective-permute-done | bytes 311328 | tf_op jit(solution)/shard_map/ppermute | solution.py:34
  19.7 4.1 %collective-permute-done.2 = f32[608,128]{1,0:T(8,128)S(1)} collective-permute-done((f32[608,128]{1,0:T(8,128)S(1)}, f32[608,128]{1,0:T(8,128)S(1)}, u32[]{:S(2)}, u32[]{:S(2)}) %collective-permute-start.2) | collective-permute-done | bytes 311328 | tf_op jit(solution)/shard_map/ppermute | solution.py:34
  23.9 0.7 %copy-done.1 = f32[608,128]{1,0:T(8,128)} copy-done((f32[608,128]{1,0:T(8,128)}, f32[608,128]{1,0:T(8,128)S(1)}, u32[]{:S(2)}) %copy-start.1) | copy-done | bytes 311320
  24.6 0.2 pad_maximum_fusion.1
  24.8 0.4 fusion.3
  25.2 0.0 copy-start.3
  25.2 0.4 copy.20
  25.6 1.9 %collective-permute-start.3 = (f32[4,2432]{1,0:T(4,128)S(1)}, f32[4,2432]{1,0:T(4,128)S(1)}, u32[]{:S(2)}, u32[]{:S(2)}) collective-permute-start(f32[4,2432]{1,0:T(4,128)S(1)} %bitcast.69), channel_id=1, source_target_pairs={{4,0},{8,4},{12,8},{5,1},{9,5},{13,9},{6,2},{10,6},{14,10},{7,3},{... | collective-permute-start | bytes 116744 | tf_op jit(solution)/shard_map/ppermute | solution.py:34
  27.5 0.4 copy.22
  27.9 2.4 %collective-permute-start.4 = (f32[4,2432]{1,0:T(4,128)S(1)}, f32[4,2432]{1,0:T(4,128)S(1)}, u32[]{:S(2)}, u32[]{:S(2)}) collective-permute-start(f32[4,2432]{1,0:T(4,128)S(1)} %bitcast.71), channel_id=1, source_target_pairs={{0,4},{4,8},{8,12},{1,5},{5,9},{9,13},{2,6},{6,10},{10,14},{3,7},{... | collective-permute-start | bytes 116744 | tf_op jit(solution)/shard_map/ppermute | solution.py:34
  30.4 0.0 copy-done.3
  30.4 0.1 pad.6.clone
  30.5 0.0 collective-permute-done.3
  30.5 1.5 %copy.21 = f32[2432,4]{1,0:T(8,128)} copy(f32[2432,4]{0,1:T(4,128)S(1)} %bitcast.70) | data formatting | bytes 77824 | tf_op jit(solution)/shard_map/transpose | solution.py:47
  32.0 1.3 %collective-permute-done.4 = f32[4,2432]{1,0:T(4,128)S(1)} collective-permute-done((f32[4,2432]{1,0:T(4,128)S(1)}, f32[4,2432]{1,0:T(4,128)S(1)}, u32[]{:S(2)}, u32[]{:S(2)}) %collective-permute-start.4) | collective-permute-done | bytes 38944 | tf_op jit(solution)/shard_map/ppermute | solution.py:34
  33.2 1.5 %copy.23 = f32[2432,4]{1,0:T(8,128)} copy(f32[2432,4]{0,1:T(4,128)S(1)} %bitcast.72) | data formatting | bytes 77824 | tf_op jit(solution)/shard_map/transpose | solution.py:47
  34.7 2.3 %pad_maximum_fusion.state_ref = f32[19,8,16,256]{3,2,1,0:T(8,128)S(1)} fusion(f32[19,8,16,4]{3,2,1,0:T(8,128)} %bitcast.56, f32[19,8,16,4]{3,2,1,0:T(8,128)} %bitcast.55, f32[19,8,4,128]{3,2,1,0:T(4,128)} %bitcast.62, f32[19,8,4,128]{3,2,1,0:T(4,128)S(1)} %bitcast.60, f32[1,8,8,128]{3,2,1,0:T(8,128)S(1)} %broadcast_in_dim.89, ...), kind=kLoop, calls=%fused_computation | loop fusion | flops 4358144 | bytes 3814400 | tf_op jit(solution)/shard_map/concatenate | solution.py:59
  37.0 0.1 select_reduce_fusion
  37.3 1.1 %copy-done = f32[19,8,16,256]{3,2,1,0:T(8,128)} copy-done((f32[19,8,16,256]{3,2,1,0:T(8,128)}, f32[19,8,16,256]{3,2,1,0:T(8,128)S(1)}, u32[]{:S(2)}) %copy-start) | copy-done | bytes 2490392
  38.4 0.1 copy-done.2
  38.5 5.1 %shard_map.146 = (f32[3,4,8,128]{3,2,1,0:T(8,128)}, f32[3,4,8,128]{3,2,1,0:T(8,128)}, f32[2,3,4,8,128]{4,3,2,1,0:T(8,128)}, f32[2,3,4,8,128]{4,3,2,1,0:T(8,128)}, f32[4,8,128]{2,1,0:T(8,128)}) custom-call(s32[4]{0:T(128)} %advance_ref.1, s32[1]{0:T(128)} %bitcast.own_ref, f32[19,8,16,256]{3,2,1,0:T(8,128)} %copy-done, f32[8,16,256]{2,1,0:T(8,128)} %copy-done.2, ...), custom_call_target="tpu_custom_call" | custom-call | tf_op jit(solution)/shard_map/pallas_call | solution.py:231
  (23 shorter events, 0.2 us)
Async XLA Ops:
  1.6 8.8 %collective-permute-start = (f32[18,4,8,128]{3,2,1,0:T(8,128)S(1)}, f32[18,4,8,128]{3,2,1,0:T(8,128)S(1)}, u32[]{:S(2)}, u32[]{:S(2)}) collective-permute-start(f32[18,4,8,128]{3,2,1,0:T(8,128)S(1)} %pad_maximum_fusion.3), channel_id=1, source_target_pairs={{0,16},{16,0},{1,17},{17,1},{2,18},{18,2},{3,19},{19,3},{4,20},{20... | collective-permute-start | bytes 884744 | tf_op jit(solution)/shard_map/ppermute | solution.py:29
  11.7 8.1 %collective-permute-start.1 = (f32[608,128]{1,0:T(8,128)S(1)}, f32[608,128]{1,0:T(8,128)S(1)}, u32[]{:S(2)}, u32[]{:S(2)}) collective-permute-start(f32[608,128]{1,0:T(8,128)S(1)} %bitcast.68), channel_id=1, source_target_pairs={{1,0},{2,1},{3,2},{5,4},{6,5},{7,6},{9,8},{10,9},{11,10},{13,12},{... | collective-permute-start | bytes 933896 | tf_op jit(solution)/shard_map/ppermute | solution.py:34
  14.0 9.8 %collective-permute-start.2 = (f32[608,128]{1,0:T(8,128)S(1)}, f32[608,128]{1,0:T(8,128)S(1)}, u32[]{:S(2)}, u32[]{:S(2)}) collective-permute-start(f32[608,128]{1,0:T(8,128)S(1)} %bitcast.67), channel_id=1, source_target_pairs={{0,1},{1,2},{2,3},{4,5},{5,6},{6,7},{8,9},{9,10},{10,11},{12,13},{... | collective-permute-start | bytes 933896 | tf_op jit(solution)/shard_map/ppermute | solution.py:34
  23.9 0.7 %copy-start.1 = (f32[608,128]{1,0:T(8,128)}, f32[608,128]{1,0:T(8,128)S(1)}, u32[]{:S(2)}) copy-start(f32[608,128]{1,0:T(8,128)S(1)} %collective-permute-done.2) | copy-start | bytes 933892
  25.2 5.1 %copy-start.3 = (f32[2,8]{1,0:T(2,128)S(1)}, f32[2,8]{1,0:T(2,128)}, u32[]{:S(2)}) copy-start(f32[2,8]{1,0:T(2,128)} %param.19) | copy-start | bytes 196
  25.6 4.9 %collective-permute-start.3 = (f32[4,2432]{1,0:T(4,128)S(1)}, f32[4,2432]{1,0:T(4,128)S(1)}, u32[]{:S(2)}, u32[]{:S(2)}) collective-permute-start(f32[4,2432]{1,0:T(4,128)S(1)} %bitcast.69), channel_id=1, source_target_pairs={{4,0},{8,4},{12,8},{5,1},{9,5},{13,9},{6,2},{10,6},{14,10},{7,3},{... | collective-permute-start | bytes 116744 | tf_op jit(solution)/shard_map/ppermute | solution.py:34
  27.9 5.3 %collective-permute-start.4 = (f32[4,2432]{1,0:T(4,128)S(1)}, f32[4,2432]{1,0:T(4,128)S(1)}, u32[]{:S(2)}, u32[]{:S(2)}) collective-permute-start(f32[4,2432]{1,0:T(4,128)S(1)} %bitcast.71), channel_id=1, source_target_pairs={{0,4},{4,8},{8,12},{1,5},{5,9},{9,13},{2,6},{6,10},{10,14},{3,7},{... | collective-permute-start | bytes 116744 | tf_op jit(solution)/shard_map/ppermute | solution.py:34
  34.7 2.3 %copy-start.4 = (f32[8]{0:T(128)S(1)}, f32[8]{0:T(128)}, u32[]{:S(2)}) copy-start(f32[8]{0:T(128)} %param.18) | copy-start | bytes 100
  34.7 2.3 %copy-start.5 = (f32[8]{0:T(128)S(1)}, f32[8]{0:T(128)}, u32[]{:S(2)}) copy-start(f32[8]{0:T(128)} %param.17) | copy-start | bytes 100
  37.0 1.4 %copy-start = (f32[19,8,16,256]{3,2,1,0:T(8,128)}, f32[19,8,16,256]{3,2,1,0:T(8,128)S(1)}, u32[]{:S(2)}) copy-start(f32[19,8,16,256]{3,2,1,0:T(8,128)S(1)} %pad_maximum_fusion.state_ref) | copy-start | bytes 7471108
  37.3 1.2 %copy-start.2 = (f32[8,16,256]{2,1,0:T(8,128)}, f32[8,16,256]{2,1,0:T(8,128)S(1)}, u32[]{:S(2)}) copy-start(f32[8,16,256]{2,1,0:T(8,128)S(1)} %constant_dynamic-update-slice_fusion.coef_ref) | copy-start | bytes 393220

commit v8 on v7

--- a/solution.py
+++ b/solution.py
@@ -197,11 +197,28 @@
 
     kinds = material.astype(jnp.float32)
     state = jnp.concatenate([state, jnp.broadcast_to(kinds[None, None], (1, depth, rows, columns))], axis=0)
-    ring_rows = -(-(rows + 2 * halo) // 8) * 8
-    ring_columns = -(-(columns + 2 * halo) // 128) * 128
-    state = with_ring(state, "ty", 2, halo, ring_rows)
-    state = with_ring(state, "tx", 3, halo, ring_columns)
-    kinds = state[-1, 0].astype(jnp.int32)
+    ring_rows = rows + 2 * halo
+    tile = -(-2 * halo // 128) * 128
+    ring_columns = columns + tile
+    head = lax.slice_in_dim(state, 0, halo, axis=2)
+    tail = lax.slice_in_dim(state, rows - halo, rows, axis=2)
+    below = unpacked(from_offsets(packed(tail), "ty", (-1,))[-1], tail.shape)
+    above = unpacked(from_offsets(packed(head), "ty", (1,))[1], head.shape)
+    side = jnp.concatenate([above, below], axis=2)
+
+    def columns_of(low, high):
+        return jnp.concatenate(
+            [lax.slice_in_dim(state, low, high, axis=3), lax.slice_in_dim(side, low, high, axis=3)], axis=2
+        )
+
+    x_head, x_tail = (columns_of(0, halo), columns_of(columns - halo, columns))
+    from_right = from_offsets(x_head.reshape(-1, halo).T, "tx", (1,))[1]
+    from_left = from_offsets(x_tail.reshape(-1, halo).T, "tx", (-1,))[-1]
+    gap = jnp.zeros((tile - 2 * halo, from_right.shape[1]), jnp.float32)
+    halo_tile = jnp.concatenate([from_right, gap, from_left], axis=0).T.reshape(x_head.shape[:-1] + (tile,))
+    kinds = jnp.concatenate(
+        [jnp.concatenate([state[-1, 0], side[-1, 0]], axis=0), halo_tile[-1, 0]], axis=1
+    ).astype(jnp.int32)
 
     place_z = base_z + lax.broadcasted_iota(jnp.int32, (depth,), 0)
     place_y = ring_coordinates(at_y * rows, rows, halo, ring_rows)
@@ -242,16 +259,14 @@
         in_specs=[
             pl.BlockSpec(memory_space=pltpu.SMEM),
             pl.BlockSpec(memory_space=pltpu.SMEM),
-            pl.BlockSpec(memory_space=pltpu.VMEM),
-            pl.BlockSpec(memory_space=pltpu.VMEM),
-            pl.BlockSpec(memory_space=pltpu.VMEM),
-        ],
+        ]
+        + [pl.BlockSpec(memory_space=pltpu.VMEM) for _ in range(5)],
         out_specs=tuple(pl.BlockSpec(memory_space=pltpu.VMEM) for _ in range(5)),
         scratch_shapes=[
             pltpu.VMEM((fields, depth + WSHIFT, ring_rows, ring_columns), jnp.float32),
             pltpu.VMEM((depth, rows, columns), jnp.float32),
         ],
-    )(advance, own_at, state, coefficients, keep_mask)
+    )(advance, own_at, state, side, halo_tile, coefficients, keep_mask)
     electric_o, magnetic_o, polarization_o, current_o, column_energy = outs
     if not whole_column:
         prefix = entering(jnp.sum(column_energy, axis=0), "prop")
@@ -260,12 +275,16 @@
 
 
 def steps_kernel(
-    advance_ref, own_ref, state_ref, coef_ref, mask_ref,
+    advance_ref, own_ref, state_ref, side_ref, tile_ref, coef_ref, mask_ref,
     electric_ref, magnetic_ref, polarization_ref, current_ref, energy_ref,
     work_ref, running_ref, *, planes, rows, columns, whole, total,
 ):
     fields, depth = (work_ref.shape[0], work_ref.shape[1] - WSHIFT)
     work_ref[:, depth:] = jnp.zeros((fields, WSHIFT) + work_ref.shape[2:], jnp.float32)
+    for c in range(fields):
+        work_ref[c, 0:depth, 0:rows, 0:columns] = state_ref[c]
+        work_ref[c, 0:depth, rows:, 0:columns] = side_ref[c]
+        work_ref[c, 0:depth, :, columns:] = tile_ref[c]
     eps_cell, kerr_cell = (coef_ref[0], coef_ref[1])
     strength, keep_rate, drive_rate = (
         (coef_ref[2], coef_ref[3]),
@@ -294,12 +313,9 @@
     def down_x(f):
         return pltpu.roll(f, 1, 2)
 
-    amount = None
+    amount = 0
     for moment in range(STEPS):
-        if amount is None:
-            values = [state_ref[c] for c in range(fields)]
-        else:
-            values = [work_ref[c, pl.ds(amount, depth)] for c in range(fields)]
+        values = [work_ref[c, pl.ds(amount, depth)] for c in range(fields)]
         e_x, e_y, e_z = values[0:3]
         h_x, h_y, h_z = values[3:6]
         pol = [values[6:9], values[9:12]]

time: 44 us -> 43.3 us (0.984)
  local copies, waits for them, and re-layouts: 7.08 us -> 4.66 us
  other arithmetic: 6.19 us -> 7.13 us
  waiting for transfers between devices: 14.8 us -> 15.6 us
    transpose x2 -> x0, local copies, waits for them, and re-layouts: 2.96 us -> none  [unpack(): return values.T.reshape(shape)]
    ppermute x0 -> x2, local copies, waits for them, and re-layouts: none -> 1.89 us  [from_offsets(): got[k] = lax.ppermute(value, axis, pairs)]
    ppermute x4, waiting for transfers between devices: 9.07 us -> 10.6 us  [from_offsets(): got[k] = lax.ppermute(value, axis, pairs)]
    unnamed x16, local copies, waits for them, and re-layouts: 1.94 us -> 0.78 us
    concatenate x2 -> x4, other arithmetic: 2.44 us -> 3.37 us  [the longest x1 1.71 us: body(): jnp.concatenate([from_right, gap, from_left], axis=0)]
    ppermute x1, waiting for transfers between devices: 5.71 us -> 4.95 us  [from_offsets(): received = lax.ppermute(value, axis, pairs)]
  transfers between devices with their start and end apart: 5 -> 5, of which waited for: 4 -> 4; matrix products, arithmetic and copies ran while one was open for 10% -> 8% of each run, Pallas kernels for 0% -> 0%
where the time goes in v8:
time: 43.3 us; the launch traced here: 42.9 us
  waiting for transfers between devices  15.6 us (36%)
  starting transfers between devices  9.58 us (22%)
  other arithmetic  7.13 us (16%)
  Pallas kernels  5.05 us (12%)
  local copies, waits for them, and re-layouts  4.66 us (11%)
  between operations  0.92 us (2%)
    ppermute x4, waiting for transfers between devices, from_offsets(): got[k] = lax.ppermute(value, axis, pairs)  10.6 us
    ppermute x4, starting transfers between devices, from_offsets(): got[k] = lax.ppermute(value, axis, pairs)  8.02 us
    pallas_call x1, Pallas kernels, body(): pl.pallas_call(functools.partial(steps_kernel, planes=planes, rows=rows,...  5.05 us
    ppermute x1, waiting for transfers between devices, from_offsets(): received = lax.ppermute(value, axis, pairs)  4.95 us
    ppermute x2, local copies, waits for them, and re-layouts, from_offsets(): got[k] = lax.ppermute(value, axis, pairs)  1.89 us
    concatenate x1, other arithmetic, body(): jnp.concatenate([from_right, gap, from_left], axis=0)  1.71 us
    ppermute x1, starting transfers between devices, from_offsets(): received = lax.ppermute(value, axis, pairs)  1.56 us
    concatenate x2, other arithmetic, body(): side = jnp.concatenate([above, below], axis=2)  1.43 us
  transfers between devices with their start and end apart: 5, of which 4 were waited for; matrix products, arithmetic and copies ran while one was open for 8% of the time, Pallas kernels for 0%

profile of v8, /device:TPU:28, one launch (start us, length us, event | category | flops | bytes accessed | tf_op | source)
XLA Modules:
  0.0 42.9 jit_solution(8038862529364841331)
XLA Ops:
  0.6 1.0 %pad_maximum_fusion.5 = f32[18,4,8,128]{3,2,1,0:T(8,128)S(1)} fusion(f32[6,4,8,128]{3,2,1,0:T(8,128)} %bitcast.66, f32[6,4,8,128]{3,2,1,0:T(8,128)} %bitcast.68, f32[3,4,8,128]{3,2,1,0:T(8,128)} %param.12, f32[3,4,8,128]{3,2,1,0:T(8,128)} %param.11), kind=kLoop, calls=%fused_computation.13 | loop fusion | flops 221184 | bytes 589824 | tf_op jit(solution)/shard_map/concatenate | solution.py:163
  1.6 1.6 %collective-permute-start = (f32[18,4,8,128]{3,2,1,0:T(8,128)S(1)}, f32[18,4,8,128]{3,2,1,0:T(8,128)S(1)}, u32[]{:S(2)}, u32[]{:S(2)}) collective-permute-start(f32[18,4,8,128]{3,2,1,0:T(8,128)S(1)} %pad_maximum_fusion.5), channel_id=1, source_target_pairs={{0,16},{16,0},{1,17},{17,1},{2,18},{18,2},{3,19},{19,3},{4,20},{20... | collective-permute-start | bytes 884744 | tf_op jit(solution)/shard_map/ppermute | solution.py:29
  3.2 0.7 %convert_element_type.13 = f32[8,128]{1,0:T(8,128)S(1)} convert(s32[8,128]{1,0:T(8,128)} %param.15) | non-fusion elementwise | flops 1024 | bytes 8192 | tf_op jit(solution)/shard_map/convert_element_type | solution.py:198
  3.9 0.8 %slice_bitcast_fusion.2 = (f32[8]{0:T(128)S(1)}, f32[8]{0:T(128)S(1)}, f32[8]{0:T(128)S(1)}, f32[8]{0:T(128)S(1)}) fusion(f32[2,8]{1,0:T(2,128)} %param.20, f32[2,8]{1,0:T(2,128)} %param.21), kind=kLoop, calls=%fused_computation.53 | loop fusion | bytes 256 | tf_op jit(solution)/shard_map/jit(_where)/broadcast_in_dim | solution.py:124
  4.6 0.1 broadcast_and_fusion
  4.7 0.7 %and_convert_fusion.mask_ref = f32[8,16,256]{2,1,0:T(8,128)} fusion(pred[256]{0:T(512)(128)(4,1)S(1)} %compare_and_fusion, pred[8,16]{1,0:T(8,128)(4,1)S(1)} %broadcast_and_fusion), kind=kLoop, calls=%fused_computation.25 | loop fusion | flops 65536 | bytes 131456 | tf_op jit(solution)/shard_map/convert_element_type | solution.py:230
  5.5 4.9 %collective-permute-done = f32[18,4,8,128]{3,2,1,0:T(8,128)S(1)} collective-permute-done((f32[18,4,8,128]{3,2,1,0:T(8,128)S(1)}, f32[18,4,8,128]{3,2,1,0:T(8,128)S(1)}, u32[]{:S(2)}, u32[]{:S(2)}) %collective-permute-start) | collective-permute-done | bytes 294944 | tf_op jit(solution)/shard_map/ppermute | solution.py:29
  10.4 1.0 %select_select_fusion.1 = (f32[18,4,8,128]{3,2,1,0:T(8,128)S(1)}, f32[18,4,8,128]{3,2,1,0:T(8,128)S(1)}) fusion(f32[18,4,8,128]{3,2,1,0:T(8,128)S(1)} %collective-permute-done, pred[]{:T(512)S(6)} %and.56, pred[]{:T(512)S(6)} %eq.28, pred[]{:T(512)S(6)} %and.55, pred[]{:T(512)S(6)} %eq.27, pred[]{:T(512)S(6)} %eq.26, f32[6,4,8,128]{3,2,1,0:T(8,128)} %bitcast.67, ...), kind=kLoop, calls=%fused_computation.15 | loop fusion | flops 811008 | bytes 1179656 | tf_op jit(solution)/shard_map/jit(_where)/select_n | solution.py:184
  11.5 0.0 copy-start.3
  11.5 0.1 fusion.7
  11.7 2.4 %collective-permute-start.1 = (f32[608,128]{1,0:T(8,128)S(1)}, f32[608,128]{1,0:T(8,128)S(1)}, u32[]{:S(2)}, u32[]{:S(2)}) collective-permute-start(f32[608,128]{1,0:T(8,128)S(1)} %bitcast.71), channel_id=1, source_target_pairs={{1,0},{2,1},{3,2},{5,4},{6,5},{7,6},{9,8},{10,9},{11,10},{13,12},{... | collective-permute-start | bytes 933896 | tf_op jit(solution)/shard_map/ppermute | solution.py:34
  14.1 1.3 %collective-permute-start.2 = (f32[608,128]{1,0:T(8,128)S(1)}, f32[608,128]{1,0:T(8,128)S(1)}, u32[]{:S(2)}, u32[]{:S(2)}) collective-permute-start(f32[608,128]{1,0:T(8,128)S(1)} %bitcast.70), channel_id=1, source_target_pairs={{0,1},{1,2},{2,3},{4,5},{5,6},{6,7},{8,9},{9,10},{10,11},{12,13},{... | collective-permute-start | bytes 933896 | tf_op jit(solution)/shard_map/ppermute | solution.py:34
  15.4 0.1 pad.4.clone
  15.5 0.2 fusion.6
  15.7 4.1 %collective-permute-done.1 = f32[608,128]{1,0:T(8,128)S(1)} collective-permute-done((f32[608,128]{1,0:T(8,128)S(1)}, f32[608,128]{1,0:T(8,128)S(1)}, u32[]{:S(2)}, u32[]{:S(2)}) %collective-permute-start.1) | collective-permute-done | bytes 311328 | tf_op jit(solution)/shard_map/ppermute | solution.py:34
  19.8 4.1 %collective-permute-done.2 = f32[608,128]{1,0:T(8,128)S(1)} collective-permute-done((f32[608,128]{1,0:T(8,128)S(1)}, f32[608,128]{1,0:T(8,128)S(1)}, u32[]{:S(2)}, u32[]{:S(2)}) %collective-permute-start.2) | collective-permute-done | bytes 311328 | tf_op jit(solution)/shard_map/ppermute | solution.py:34
  23.9 0.4 %fusion = (f32[19,8,8,4]{3,2,1,0:T(8,128)S(1)}, f32[19,8,8,4]{3,2,1,0:T(8,128)S(1)}) fusion(f32[19,8,4,128]{3,2,1,0:T(4,128)S(1)} %bitcast.60, f32[19,8,4,128]{3,2,1,0:T(4,128)S(1)} %bitcast.63), kind=kLoop, calls=%fused_computation.10 | loop fusion | flops 9728 | bytes 661504 | tf_op jit(solution)/shard_map/concatenate | solution.py:207
  24.4 1.0 %pad_maximum_fusion.3.side_ref = f32[19,8,8,128]{3,2,1,0:T(8,128)} fusion(f32[19,8,4,128]{3,2,1,0:T(4,128)S(1)} %bitcast.64, f32[19,8,4,128]{3,2,1,0:T(4,128)S(1)} %bitcast.61), kind=kLoop, calls=%fused_computation.6 | loop fusion | flops 155648 | bytes 1245184 | tf_op jit(solution)/shard_map/concatenate | solution.py:207
  25.3 0.2 pad_maximum_fusion
  25.6 0.4 copy.36
  26.0 1.9 %collective-permute-start.3 = (f32[4,2432]{1,0:T(4,128)S(1)}, f32[4,2432]{1,0:T(4,128)S(1)}, u32[]{:S(2)}, u32[]{:S(2)}) collective-permute-start(f32[4,2432]{1,0:T(4,128)S(1)} %bitcast.72), channel_id=1, source_target_pairs={{4,0},{8,4},{12,8},{5,1},{9,5},{13,9},{6,2},{10,6},{14,10},{7,3},{... | collective-permute-start | bytes 116744 | tf_op jit(solution)/shard_map/ppermute | solution.py:34
  27.9 0.4 copy.37
  28.3 2.4 %collective-permute-start.4 = (f32[4,2432]{1,0:T(4,128)S(1)}, f32[4,2432]{1,0:T(4,128)S(1)}, u32[]{:S(2)}, u32[]{:S(2)}) collective-permute-start(f32[4,2432]{1,0:T(4,128)S(1)} %bitcast.73), channel_id=1, source_target_pairs={{0,4},{4,8},{8,12},{1,5},{5,9},{9,13},{2,6},{6,10},{10,14},{3,7},{... | collective-permute-start | bytes 116744 | tf_op jit(solution)/shard_map/ppermute | solution.py:34
  30.7 0.0 collective-permute-done.3
  30.7 0.4 copy.34
  31.2 2.4 %collective-permute-done.4 = f32[4,2432]{1,0:T(4,128)S(1)} collective-permute-done((f32[4,2432]{1,0:T(4,128)S(1)}, f32[4,2432]{1,0:T(4,128)S(1)}, u32[]{:S(2)}, u32[]{:S(2)}) %collective-permute-start.4) | collective-permute-done | bytes 38944 | tf_op jit(solution)/shard_map/ppermute | solution.py:34
  33.6 1.5 %copy.35 = f32[4,2432]{0,1:T(8,128)} copy(f32[4,2432]{1,0:T(4,128)S(1)} %collective-permute-done.4) | data formatting | bytes 77824 | tf_op jit(solution)/shard_map/ppermute | solution.py:34
  35.1 1.7 %pad_maximum_fusion.2 = f32[128,2432]{0,1:T(8,128)S(1)} fusion(f32[4,2432]{0,1:T(8,128)} %copy.35, f32[4,2432]{0,1:T(8,128)S(1)} %copy.34, f32[128]{0:T(128)S(1)} %pad.4.clone), kind=kLoop, calls=%fused_computation.2 | loop fusion | flops 622592 | bytes 1323520 | tf_op jit(solution)/shard_map/concatenate | solution.py:218
  36.8 0.1 select_reduce_fusion
  37.1 0.7 %copy-done.1 = f32[128,2432]{0,1:T(8,128)} copy-done((f32[128,2432]{0,1:T(8,128)}, f32[128,2432]{0,1:T(8,128)S(1)}, u32[]{:S(2)}) %copy-start.1) | copy-done | bytes 1245208
  37.8 0.0 copy-done.2
  37.9 5.0 %shard_map.146 = (f32[3,4,8,128]{3,2,1,0:T(8,128)}, f32[3,4,8,128]{3,2,1,0:T(8,128)}, f32[2,3,4,8,128]{4,3,2,1,0:T(8,128)}, f32[2,3,4,8,128]{4,3,2,1,0:T(8,128)}, f32[4,8,128]{2,1,0:T(8,128)}) custom-call(s32[4]{0:T(128)} %advance_ref.1, s32[1]{0:T(128)} %bitcast.own_ref, f32[19,8,8,128]{3,2,1,0:T(8,128)} %copy-done, ...), custom_call_target="tpu_custom_call" | custom-call | tf_op jit(solution)/shard_map/pallas_call | solution.py:248
  (27 shorter events, 0.2 us)
Async XLA Ops:
  1.6 8.8 %collective-permute-start = (f32[18,4,8,128]{3,2,1,0:T(8,128)S(1)}, f32[18,4,8,128]{3,2,1,0:T(8,128)S(1)}, u32[]{:S(2)}, u32[]{:S(2)}) collective-permute-start(f32[18,4,8,128]{3,2,1,0:T(8,128)S(1)} %pad_maximum_fusion.5), channel_id=1, source_target_pairs={{0,16},{16,0},{1,17},{17,1},{2,18},{18,2},{3,19},{19,3},{4,20},{20... | collective-permute-start | bytes 884744 | tf_op jit(solution)/shard_map/ppermute | solution.py:29
  11.5 3.9 %copy-start.3 = (f32[2,8]{1,0:T(2,128)S(1)}, f32[2,8]{1,0:T(2,128)}, u32[]{:S(2)}) copy-start(f32[2,8]{1,0:T(2,128)} %param.19) | copy-start | bytes 196
  11.5 4.2 %copy-start = (f32[19,8,8,128]{3,2,1,0:T(8,128)}, f32[19,8,8,128]{3,2,1,0:T(8,128)S(1)}, u32[]{:S(2)}) copy-start(f32[19,8,8,128]{3,2,1,0:T(8,128)S(1)} %pad_maximum_fusion.4.state_ref) | copy-start | bytes 1867780
  11.7 8.1 %collective-permute-start.1 = (f32[608,128]{1,0:T(8,128)S(1)}, f32[608,128]{1,0:T(8,128)S(1)}, u32[]{:S(2)}, u32[]{:S(2)}) collective-permute-start(f32[608,128]{1,0:T(8,128)S(1)} %bitcast.71), channel_id=1, source_target_pairs={{1,0},{2,1},{3,2},{5,4},{6,5},{7,6},{9,8},{10,9},{11,10},{13,12},{... | collective-permute-start | bytes 933896 | tf_op jit(solution)/shard_map/ppermute | solution.py:34
  14.1 9.8 %collective-permute-start.2 = (f32[608,128]{1,0:T(8,128)S(1)}, f32[608,128]{1,0:T(8,128)S(1)}, u32[]{:S(2)}, u32[]{:S(2)}) collective-permute-start(f32[608,128]{1,0:T(8,128)S(1)} %bitcast.70), channel_id=1, source_target_pairs={{0,1},{1,2},{2,3},{4,5},{5,6},{6,7},{8,9},{9,10},{10,11},{12,13},{... | collective-permute-start | bytes 933896 | tf_op jit(solution)/shard_map/ppermute | solution.py:34
  26.0 4.8 %collective-permute-start.3 = (f32[4,2432]{1,0:T(4,128)S(1)}, f32[4,2432]{1,0:T(4,128)S(1)}, u32[]{:S(2)}, u32[]{:S(2)}) collective-permute-start(f32[4,2432]{1,0:T(4,128)S(1)} %bitcast.72), channel_id=1, source_target_pairs={{4,0},{8,4},{12,8},{5,1},{9,5},{13,9},{6,2},{10,6},{14,10},{7,3},{... | collective-permute-start | bytes 116744 | tf_op jit(solution)/shard_map/ppermute | solution.py:34
  28.3 5.3 %collective-permute-start.4 = (f32[4,2432]{1,0:T(4,128)S(1)}, f32[4,2432]{1,0:T(4,128)S(1)}, u32[]{:S(2)}, u32[]{:S(2)}) collective-permute-start(f32[4,2432]{1,0:T(4,128)S(1)} %bitcast.73), channel_id=1, source_target_pairs={{0,4},{4,8},{8,12},{1,5},{5,9},{9,13},{2,6},{6,10},{10,14},{3,7},{... | collective-permute-start | bytes 116744 | tf_op jit(solution)/shard_map/ppermute | solution.py:34
  35.1 1.8 %copy-start.4 = (f32[8]{0:T(128)S(1)}, f32[8]{0:T(128)}, u32[]{:S(2)}) copy-start(f32[8]{0:T(128)} %param.18) | copy-start | bytes 100
  35.1 1.8 %copy-start.5 = (f32[8]{0:T(128)S(1)}, f32[8]{0:T(128)}, u32[]{:S(2)}) copy-start(f32[8]{0:T(128)} %param.17) | copy-start | bytes 100
  36.8 1.0 %copy-start.1 = (f32[128,2432]{0,1:T(8,128)}, f32[128,2432]{0,1:T(8,128)S(1)}, u32[]{:S(2)}) copy-start(f32[128,2432]{0,1:T(8,128)S(1)} %pad_maximum_fusion.2) | copy-start | bytes 3735556
  37.1 0.8 %copy-start.2 = (f32[8,16,256]{2,1,0:T(8,128)}, f32[8,16,256]{2,1,0:T(8,128)S(1)}, u32[]{:S(2)}) copy-start(f32[8,16,256]{2,1,0:T(8,128)S(1)} %constant_dynamic-update-slice_fusion.coef_ref) | copy-start | bytes 393220

commit v9 on v8

--- a/solution.py
+++ b/solution.py
@@ -212,13 +212,18 @@
         )
 
     x_head, x_tail = (columns_of(0, halo), columns_of(columns - halo, columns))
-    from_right = from_offsets(x_head.reshape(-1, halo).T, "tx", (1,))[1]
-    from_left = from_offsets(x_tail.reshape(-1, halo).T, "tx", (-1,))[-1]
-    gap = jnp.zeros((tile - 2 * halo, from_right.shape[1]), jnp.float32)
-    halo_tile = jnp.concatenate([from_right, gap, from_left], axis=0).T.reshape(x_head.shape[:-1] + (tile,))
-    kinds = jnp.concatenate(
-        [jnp.concatenate([state[-1, 0], side[-1, 0]], axis=0), halo_tile[-1, 0]], axis=1
-    ).astype(jnp.int32)
+    strip_rows = -(-halo // 8) * 8
+    strip_length = -(-x_head.size // halo // 128) * 128
+    assert 2 * strip_rows <= tile
+
+    def strip(values, at_top):
+        flat = values.reshape(-1, halo).T
+        room = strip_rows - halo
+        rows_pad = (0, room) if at_top else (room, 0)
+        return jnp.pad(flat, (rows_pad, (0, strip_length - flat.shape[1])))
+
+    from_right = from_offsets(strip(x_head, True), "tx", (1,))[1]
+    from_left = from_offsets(strip(x_tail, False), "tx", (-1,))[-1]
 
     place_z = base_z + lax.broadcasted_iota(jnp.int32, (depth,), 0)
     place_y = ring_coordinates(at_y * rows, rows, halo, ring_rows)
@@ -229,21 +234,20 @@
         & ((place_x >= 0) & (place_x < total_x))[None, None, :]
     ).astype(jnp.float32)
 
-    materials_count = permittivity.shape[0]
-    selector = kinds[None] == lax.broadcasted_iota(
-        jnp.int32, (materials_count, ring_rows, ring_columns), 0
+    half_damp = 0.5 * time_step * pole_damping
+    table = jnp.concatenate(
+        [
+            permittivity[None],
+            nonlinear[None],
+            pole_strength,
+            (1.0 - half_damp) / (1.0 + half_damp),
+            time_step * pole_frequency * pole_frequency / (1.0 + half_damp),
+        ],
+        axis=0,
     )
-    eps_cell = cell_lookup(selector, permittivity)
-    kerr_cell = cell_lookup(selector, nonlinear)
-    strength = [cell_lookup(selector, pole_strength[p]) for p in range(2)]
-    frequency = [cell_lookup(selector, pole_frequency[p]) for p in range(2)]
-    half_damp = [0.5 * time_step * cell_lookup(selector, pole_damping[p]) for p in range(2)]
-    keep_rate = [(1.0 - h) / (1.0 + h) for h in half_damp]
-    drive_rate = [time_step * f * f / (1.0 + h) for f, h in zip(frequency, half_damp)]
-    coefficients = jnp.stack([eps_cell, kerr_cell] + strength + keep_rate + drive_rate)
 
     own_at = jnp.reshape(jnp.asarray(own_z, jnp.int32), (1,))
-    fields = state.shape[0] - 1
+    fields = state.shape[0]
     block = (planes, rows, columns)
     outs = pl.pallas_call(
         functools.partial(
@@ -259,14 +263,17 @@
         in_specs=[
             pl.BlockSpec(memory_space=pltpu.SMEM),
             pl.BlockSpec(memory_space=pltpu.SMEM),
+            pl.BlockSpec(memory_space=pltpu.SMEM),
         ]
         + [pl.BlockSpec(memory_space=pltpu.VMEM) for _ in range(5)],
         out_specs=tuple(pl.BlockSpec(memory_space=pltpu.VMEM) for _ in range(5)),
         scratch_shapes=[
             pltpu.VMEM((fields, depth + WSHIFT, ring_rows, ring_columns), jnp.float32),
             pltpu.VMEM((depth, rows, columns), jnp.float32),
+            pltpu.VMEM((tile, strip_length), jnp.float32),
+            pltpu.VMEM((strip_length, tile), jnp.float32),
         ],
-    )(advance, own_at, state, side, halo_tile, coefficients, keep_mask)
+    )(advance, own_at, table, state, side, from_right, from_left, keep_mask)
     electric_o, magnetic_o, polarization_o, current_o, column_energy = outs
     if not whole_column:
         prefix = entering(jnp.sum(column_energy, axis=0), "prop")
@@ -275,22 +282,35 @@
 
 
 def steps_kernel(
-    advance_ref, own_ref, state_ref, side_ref, tile_ref, coef_ref, mask_ref,
+    advance_ref, own_ref, table_ref, state_ref, side_ref, right_ref, left_ref, mask_ref,
     electric_ref, magnetic_ref, polarization_ref, current_ref, energy_ref,
-    work_ref, running_ref, *, planes, rows, columns, whole, total,
+    work_ref, running_ref, strips_ref, turned_ref, *, planes, rows, columns, whole, total,
 ):
     fields, depth = (work_ref.shape[0], work_ref.shape[1] - WSHIFT)
+    ring_rows = work_ref.shape[2]
+    tile = strips_ref.shape[0]
+    strip_rows = right_ref.shape[0]
     work_ref[:, depth:] = jnp.zeros((fields, WSHIFT) + work_ref.shape[2:], jnp.float32)
+    strips_ref[...] = jnp.zeros(strips_ref.shape, jnp.float32)
+    strips_ref[0:strip_rows] = right_ref[...]
+    strips_ref[tile - strip_rows:tile] = left_ref[...]
+    turned_ref[...] = strips_ref[...].T
     for c in range(fields):
         work_ref[c, 0:depth, 0:rows, 0:columns] = state_ref[c]
         work_ref[c, 0:depth, rows:, 0:columns] = side_ref[c]
-        work_ref[c, 0:depth, :, columns:] = tile_ref[c]
-    eps_cell, kerr_cell = (coef_ref[0], coef_ref[1])
-    strength, keep_rate, drive_rate = (
-        (coef_ref[2], coef_ref[3]),
-        (coef_ref[4], coef_ref[5]),
-        (coef_ref[6], coef_ref[7]),
-    )
+        for z in range(depth):
+            first_row = (c * depth + z) * ring_rows
+            work_ref[c, z, :, columns:] = turned_ref[first_row:first_row + ring_rows]
+    kinds = work_ref[fields - 1, 0]
+
+    def lookup(row):
+        cell = jnp.zeros(kinds.shape, jnp.float32)
+        for m in range(table_ref.shape[1]):
+            cell = jnp.where(kinds == jnp.float32(m), table_ref[row, m], cell)
+        return cell
+
+    eps_cell, kerr_cell = (lookup(0), lookup(1))
+    strength, keep_rate, drive_rate = ((lookup(2), lookup(3)), (lookup(4), lookup(5)), (lookup(6), lookup(7)))
     keep_mask = mask_ref[...]
     zero_plane = jnp.zeros((1,) + keep_mask.shape[1:], jnp.float32)
     ring_rows, ring_columns = keep_mask.shape[1:]
@@ -315,7 +335,7 @@
 
     amount = 0
     for moment in range(STEPS):
-        values = [work_ref[c, pl.ds(amount, depth)] for c in range(fields)]
+        values = [work_ref[c, pl.ds(amount, depth)] for c in range(fields - 1)]
         e_x, e_y, e_z = values[0:3]
         h_x, h_y, h_z = values[3:6]
         pol = [values[6:9], values[9:12]]
@@ -338,7 +358,7 @@
             for c, (field, curl) in enumerate(zip(electric, (curl_x, curl_y, curl_z)))
         ]
         results = new_e + [h_x, h_y, h_z] + pol[0] + pol[1] + cur[0] + cur[1]
-        for c in range(fields):
+        for c in range(fields - 1):
             work_ref[c, 0:depth] = results[c]
         amount = advance_ref[moment]
 

time: 43.3 us -> 39.1 us (0.903)
  local copies, waits for them, and re-layouts: 4.66 us -> 2.48 us
  other arithmetic: 7.13 us -> 5.24 us
    ppermute x2 -> x0, local copies, waits for them, and re-layouts: 1.89 us -> none  [from_offsets(): got[k] = lax.ppermute(value, axis, pairs)]
    concatenate x1 -> x0, other arithmetic: 1.71 us -> none  [body(): jnp.concatenate([from_right, gap, from_left], axis=0)]
    broadcast_in_dim x3 -> x0, local copies, waits for them, and re-layouts: 0.77 us -> none  [the longest x2 0.77 us: cell_lookup(): jnp.where(selector, table[:, None, None], jnp.float32(0.0))]
    ppermute x1, waiting for transfers between devices: 4.95 us -> 5.71 us  [from_offsets(): received = lax.ppermute(value, axis, pairs)]
    ppermute x4, waiting for transfers between devices: 10.6 us -> 9.95 us  [from_offsets(): got[k] = lax.ppermute(value, axis, pairs)]
    concatenate x2 -> x1, local copies, waits for them, and re-layouts: 0.08 us -> 0.6 us  [body(): jnp.concatenate([permittivity[None], nonlinear[None], pole_strength, (1.0...]
  transfers between devices with their start and end apart: 5 -> 5, of which waited for: 4 -> 4; matrix products, arithmetic and copies ran while one was open for 8% -> 10% of each run, Pallas kernels for 0% -> 0%
where the time goes in v9:
time: 39.1 us; the launch traced here: 38.7 us
  waiting for transfers between devices  15.7 us (40%)
  starting transfers between devices  9.55 us (24%)
  other arithmetic  5.24 us (13%)
  Pallas kernels  4.97 us (13%)
  local copies, waits for them, and re-layouts  2.48 us (6%)
  between operations  0.85 us (2%)
    ppermute x4, waiting for transfers between devices, from_offsets(): got[k] = lax.ppermute(value, axis, pairs)  9.95 us
    ppermute x4, starting transfers between devices, from_offsets(): got[k] = lax.ppermute(value, axis, pairs)  7.99 us
    ppermute x1, waiting for transfers between devices, from_offsets(): received = lax.ppermute(value, axis, pairs)  5.71 us
    pallas_call x1, Pallas kernels, body(): pl.pallas_call(functools.partial(steps_kernel, planes=planes, rows=rows,...  4.97 us
    ppermute x1, starting transfers between devices, from_offsets(): received = lax.ppermute(value, axis, pairs)  1.56 us
    concatenate x2, other arithmetic, body(): side = jnp.concatenate([above, below], axis=2)  1.43 us
    select_n x1, other arithmetic, body(): block = jnp.where(at_z + k == j, piece, block)  1.02 us
    concatenate x1, other arithmetic, body(): jnp.concatenate([electric, magnetic, polarization.reshape((-1,) + electri...  0.97 us
  transfers between devices with their start and end apart: 5, of which 4 were waited for; matrix products, arithmetic and copies ran while one was open for 10% of the time, Pallas kernels for 0%

profile of v9, /device:TPU:28, one launch (start us, length us, event | category | flops | bytes accessed | tf_op | source)
XLA Modules:
  0.0 38.7 jit_solution(14774702371890388724)
XLA Ops:
  0.6 1.0 %pad_maximum_fusion.4 = f32[18,4,8,128]{3,2,1,0:T(8,128)S(1)} fusion(f32[6,4,8,128]{3,2,1,0:T(8,128)} %bitcast.19, f32[6,4,8,128]{3,2,1,0:T(8,128)} %bitcast.21, f32[3,4,8,128]{3,2,1,0:T(8,128)} %param.12, f32[3,4,8,128]{3,2,1,0:T(8,128)} %param.11), kind=kLoop, calls=%fused_computation.10 | loop fusion | flops 221184 | bytes 589824 | tf_op jit(solution)/shard_map/concatenate | solution.py:163
  1.6 1.6 %collective-permute-start = (f32[18,4,8,128]{3,2,1,0:T(8,128)S(1)}, f32[18,4,8,128]{3,2,1,0:T(8,128)S(1)}, u32[]{:S(2)}, u32[]{:S(2)}) collective-permute-start(f32[18,4,8,128]{3,2,1,0:T(8,128)S(1)} %pad_maximum_fusion.4), channel_id=1, source_target_pairs={{0,16},{16,0},{1,17},{17,1},{2,18},{18,2},{3,19},{19,3},{4,20},{20... | collective-permute-start | bytes 884744 | tf_op jit(solution)/shard_map/ppermute | solution.py:29
  3.2 0.7 %convert_element_type.10 = f32[8,128]{1,0:T(8,128)S(1)} convert(s32[8,128]{1,0:T(8,128)} %param.15) | non-fusion elementwise | flops 1024 | bytes 8192 | tf_op jit(solution)/shard_map/convert_element_type | solution.py:198
  3.9 0.1 broadcast_and_fusion
  4.0 0.7 %and_convert_fusion.mask_ref = f32[8,16,256]{2,1,0:T(8,128)} fusion(pred[256]{0:T(512)(128)(4,1)S(1)} %compare_and_fusion, pred[8,16]{1,0:T(8,128)(4,1)S(1)} %broadcast_and_fusion), kind=kLoop, calls=%fused_computation.13 | loop fusion | flops 65536 | bytes 131456 | tf_op jit(solution)/shard_map/convert_element_type | solution.py:235
  4.7 5.7 %collective-permute-done = f32[18,4,8,128]{3,2,1,0:T(8,128)S(1)} collective-permute-done((f32[18,4,8,128]{3,2,1,0:T(8,128)S(1)}, f32[18,4,8,128]{3,2,1,0:T(8,128)S(1)}, u32[]{:S(2)}, u32[]{:S(2)}) %collective-permute-start) | collective-permute-done | bytes 294944 | tf_op jit(solution)/shard_map/ppermute | solution.py:29
  10.4 1.0 %select_select_fusion.1 = (f32[18,4,8,128]{3,2,1,0:T(8,128)S(1)}, f32[18,4,8,128]{3,2,1,0:T(8,128)S(1)}) fusion(f32[18,4,8,128]{3,2,1,0:T(8,128)S(1)} %collective-permute-done, pred[]{:T(512)S(6)} %and.56, pred[]{:T(512)S(6)} %eq.20, pred[]{:T(512)S(6)} %and.55, pred[]{:T(512)S(6)} %eq.19, pred[]{:T(512)S(6)} %eq.18, f32[6,4,8,128]{3,2,1,0:T(8,128)} %bitcast.20, ...), kind=kLoop, calls=%fused_computation.12 | loop fusion | flops 811008 | bytes 1179656 | tf_op jit(solution)/shard_map/jit(_where)/select_n | solution.py:184
  11.5 0.0 copy-start.3
  11.5 0.0 copy-start.4
  11.5 0.0 copy-start.5
  11.5 0.0 copy-start.6
  11.5 0.0 copy-start.7
  11.6 0.1 fusion.4
  11.7 2.4 %collective-permute-start.1 = (f32[608,128]{1,0:T(8,128)S(1)}, f32[608,128]{1,0:T(8,128)S(1)}, u32[]{:S(2)}, u32[]{:S(2)}) collective-permute-start(f32[608,128]{1,0:T(8,128)S(1)} %bitcast.24), channel_id=1, source_target_pairs={{1,0},{2,1},{3,2},{5,4},{6,5},{7,6},{9,8},{10,9},{11,10},{13,12},{... | collective-permute-start | bytes 933896 | tf_op jit(solution)/shard_map/ppermute | solution.py:34
  14.1 1.3 %collective-permute-start.2 = (f32[608,128]{1,0:T(8,128)S(1)}, f32[608,128]{1,0:T(8,128)S(1)}, u32[]{:S(2)}, u32[]{:S(2)}) collective-permute-start(f32[608,128]{1,0:T(8,128)S(1)} %bitcast.23), channel_id=1, source_target_pairs={{0,1},{1,2},{2,3},{4,5},{5,6},{6,7},{8,9},{9,10},{10,11},{12,13},{... | collective-permute-start | bytes 933896 | tf_op jit(solution)/shard_map/ppermute | solution.py:34
  15.4 0.0 copy-done.5
  15.5 0.0 copy-done.6
  15.5 0.6 %concatenate.21.table_ref = f32[8,8]{1,0:T(8,128)} concatenate(f32[1,8]{1,0:T(1,128)S(1)} %bitcast.27, f32[1,8]{1,0:T(1,128)S(1)} %bitcast.28, f32[2,8]{1,0:T(2,128)S(1)} %copy-done.5, f32[2,8]{1,0:T(2,128)S(1)} %get-tuple-element.14, f32[2,8]{1,0:T(2,128)S(1)} %get-tuple-element.13), dimensions={0} | concatenate | bytes 512 | tf_op jit(solution)/shard_map/concatenate | solution.py:238
  16.1 0.2 fusion.3
  16.3 3.5 %collective-permute-done.1 = f32[608,128]{1,0:T(8,128)S(1)} collective-permute-done((f32[608,128]{1,0:T(8,128)S(1)}, f32[608,128]{1,0:T(8,128)S(1)}, u32[]{:S(2)}, u32[]{:S(2)}) %collective-permute-start.1) | collective-permute-done | bytes 311328 | tf_op jit(solution)/shard_map/ppermute | solution.py:34
  19.8 4.1 %collective-permute-done.2 = f32[608,128]{1,0:T(8,128)S(1)} collective-permute-done((f32[608,128]{1,0:T(8,128)S(1)}, f32[608,128]{1,0:T(8,128)S(1)}, u32[]{:S(2)}, u32[]{:S(2)}) %collective-permute-start.2) | collective-permute-done | bytes 311328 | tf_op jit(solution)/shard_map/ppermute | solution.py:34
  23.9 0.4 %fusion.1 = (f32[19,8,8,4]{3,2,1,0:T(8,128)S(1)}, f32[19,8,8,4]{3,2,1,0:T(8,128)S(1)}) fusion(f32[19,8,4,128]{3,2,1,0:T(4,128)S(1)} %bitcast.15, f32[19,8,4,128]{3,2,1,0:T(4,128)S(1)} %bitcast.17), kind=kLoop, calls=%fused_computation.8 | loop fusion | flops 9728 | bytes 661504 | tf_op jit(solution)/shard_map/concatenate | solution.py:207
  24.4 0.2 pad_maximum_fusion
  24.7 0.4 copy.28
  25.1 1.9 %collective-permute-start.3 = (f32[8,2432]{1,0:T(8,128)S(1)}, f32[8,2432]{1,0:T(8,128)S(1)}, u32[]{:S(2)}, u32[]{:S(2)}) collective-permute-start(f32[8,2432]{1,0:T(8,128)S(1)} %pad.8), channel_id=1, source_target_pairs={{4,0},{8,4},{12,8},{5,1},{9,5},{13,9},{6,2},{10,6},{14,10},{7,3},{... | collective-permute-start | bytes 233480 | tf_op jit(solution)/shard_map/ppermute | solution.py:34
  27.0 0.4 copy.29
  27.4 2.4 %collective-permute-start.4 = (f32[8,2432]{1,0:T(8,128)S(1)}, f32[8,2432]{1,0:T(8,128)S(1)}, u32[]{:S(2)}, u32[]{:S(2)}) collective-permute-start(f32[8,2432]{1,0:T(8,128)S(1)} %pad.9), channel_id=1, source_target_pairs={{0,4},{4,8},{8,12},{1,5},{5,9},{9,13},{2,6},{6,10},{10,14},{3,7},{... | collective-permute-start | bytes 233480 | tf_op jit(solution)/shard_map/ppermute | solution.py:34
  29.8 1.0 %pad_maximum_fusion.2.side_ref = f32[19,8,8,128]{3,2,1,0:T(8,128)} fusion(f32[19,8,4,128]{3,2,1,0:T(4,128)S(1)} %bitcast.18, f32[19,8,4,128]{3,2,1,0:T(4,128)S(1)} %bitcast.16), kind=kLoop, calls=%fused_computation.4 | loop fusion | flops 155648 | bytes 1245184 | tf_op jit(solution)/shard_map/concatenate | solution.py:207
  30.8 0.0 collective-permute-done.3.right_ref
  30.8 2.3 %collective-permute-done.4.left_ref = f32[8,2432]{1,0:T(8,128)S(1)} collective-permute-done((f32[8,2432]{1,0:T(8,128)S(1)}, f32[8,2432]{1,0:T(8,128)S(1)}, u32[]{:S(2)}, u32[]{:S(2)}) %collective-permute-start.4) | collective-permute-done | bytes 77856 | tf_op jit(solution)/shard_map/ppermute | solution.py:34
  33.1 0.6 %copy-done.2 = f32[8,2432]{1,0:T(8,128)} copy-done((f32[8,2432]{1,0:T(8,128)}, f32[8,2432]{1,0:T(8,128)S(1)}, u32[]{:S(2)}) %copy-start.2) | copy-done | bytes 77848
  33.8 5.0 %shard_map.146 = (f32[3,4,8,128]{3,2,1,0:T(8,128)}, f32[3,4,8,128]{3,2,1,0:T(8,128)}, f32[2,3,4,8,128]{4,3,2,1,0:T(8,128)}, f32[2,3,4,8,128]{4,3,2,1,0:T(8,128)}, f32[4,8,128]{2,1,0:T(8,128)}) custom-call(s32[4]{0:T(128)} %advance_ref.1, s32[1]{0:T(128)} %bitcast.own_ref, f32[8,8]{1,0:T(8,128)} %concatenate.21.table_ref, f32[19,8,8,128]{3,2,1,0:T(8,128)} %copy-done, ...), custom_call_target="tpu_custom_call" | custom-call | tf_op jit(solution)/shard_map/pallas_call | solution.py:252
  (16 shorter events, 0.2 us)
Async XLA Ops:
  1.6 8.8 %collective-permute-start = (f32[18,4,8,128]{3,2,1,0:T(8,128)S(1)}, f32[18,4,8,128]{3,2,1,0:T(8,128)S(1)}, u32[]{:S(2)}, u32[]{:S(2)}) collective-permute-start(f32[18,4,8,128]{3,2,1,0:T(8,128)S(1)} %pad_maximum_fusion.4), channel_id=1, source_target_pairs={{0,16},{16,0},{1,17},{17,1},{2,18},{18,2},{3,19},{19,3},{4,20},{20... | collective-permute-start | bytes 884744 | tf_op jit(solution)/shard_map/ppermute | solution.py:29
  11.5 4.0 %copy-start.3 = (f32[2,8]{1,0:T(2,128)S(1)}, f32[2,8]{1,0:T(2,128)}, u32[]{:S(2)}) copy-start(f32[2,8]{1,0:T(2,128)} %param.20) | copy-start | bytes 196
  11.5 4.0 %copy-start.4 = (f32[2,8]{1,0:T(2,128)S(1)}, f32[2,8]{1,0:T(2,128)}, u32[]{:S(2)}) copy-start(f32[2,8]{1,0:T(2,128)} %param.21) | copy-start | bytes 196
  11.5 4.0 %copy-start.5 = (f32[2,8]{1,0:T(2,128)S(1)}, f32[2,8]{1,0:T(2,128)}, u32[]{:S(2)}) copy-start(f32[2,8]{1,0:T(2,128)} %param.19) | copy-start | bytes 196
  11.5 4.0 %copy-start.6 = (f32[8]{0:T(128)S(1)}, f32[8]{0:T(128)}, u32[]{:S(2)}) copy-start(f32[8]{0:T(128)} %param.17) | copy-start | bytes 100
  11.5 4.0 %copy-start.7 = (f32[8]{0:T(128)S(1)}, f32[8]{0:T(128)}, u32[]{:S(2)}) copy-start(f32[8]{0:T(128)} %param.18) | copy-start | bytes 100
  11.6 4.7 %copy-start = (f32[19,8,8,128]{3,2,1,0:T(8,128)}, f32[19,8,8,128]{3,2,1,0:T(8,128)S(1)}, u32[]{:S(2)}) copy-start(f32[19,8,8,128]{3,2,1,0:T(8,128)S(1)} %pad_maximum_fusion.3.state_ref) | copy-start | bytes 1867780
  11.7 8.1 %collective-permute-start.1 = (f32[608,128]{1,0:T(8,128)S(1)}, f32[608,128]{1,0:T(8,128)S(1)}, u32[]{:S(2)}, u32[]{:S(2)}) collective-permute-start(f32[608,128]{1,0:T(8,128)S(1)} %bitcast.24), channel_id=1, source_target_pairs={{1,0},{2,1},{3,2},{5,4},{6,5},{7,6},{9,8},{10,9},{11,10},{13,12},{... | collective-permute-start | bytes 933896 | tf_op jit(solution)/shard_map/ppermute | solution.py:34
  14.1 9.8 %collective-permute-start.2 = (f32[608,128]{1,0:T(8,128)S(1)}, f32[608,128]{1,0:T(8,128)S(1)}, u32[]{:S(2)}, u32[]{:S(2)}) collective-permute-start(f32[608,128]{1,0:T(8,128)S(1)} %bitcast.23), channel_id=1, source_target_pairs={{0,1},{1,2},{2,3},{4,5},{5,6},{6,7},{8,9},{9,10},{10,11},{12,13},{... | collective-permute-start | bytes 933896 | tf_op jit(solution)/shard_map/ppermute | solution.py:34
  25.1 5.8 %collective-permute-start.3 = (f32[8,2432]{1,0:T(8,128)S(1)}, f32[8,2432]{1,0:T(8,128)S(1)}, u32[]{:S(2)}, u32[]{:S(2)}) collective-permute-start(f32[8,2432]{1,0:T(8,128)S(1)} %pad.8), channel_id=1, source_target_pairs={{4,0},{8,4},{12,8},{5,1},{9,5},{13,9},{6,2},{10,6},{14,10},{7,3},{... | collective-permute-start | bytes 233480 | tf_op jit(solution)/shard_map/ppermute | solution.py:34
  27.4 5.7 %collective-permute-start.4 = (f32[8,2432]{1,0:T(8,128)S(1)}, f32[8,2432]{1,0:T(8,128)S(1)}, u32[]{:S(2)}, u32[]{:S(2)}) collective-permute-start(f32[8,2432]{1,0:T(8,128)S(1)} %pad.9), channel_id=1, source_target_pairs={{0,4},{4,8},{8,12},{1,5},{5,9},{9,13},{2,6},{6,10},{10,14},{3,7},{... | collective-permute-start | bytes 233480 | tf_op jit(solution)/shard_map/ppermute | solution.py:34
  30.8 2.3 %copy-start.1 = (f32[8,2432]{1,0:T(8,128)}, f32[8,2432]{1,0:T(8,128)S(1)}, u32[]{:S(2)}) copy-start(f32[8,2432]{1,0:T(8,128)S(1)} %collective-permute-done.3.right_ref) | copy-start | bytes 233476
  33.1 0.6 %copy-start.2 = (f32[8,2432]{1,0:T(8,128)}, f32[8,2432]{1,0:T(8,128)S(1)}, u32[]{:S(2)}) copy-start(f32[8,2432]{1,0:T(8,128)S(1)} %collective-permute-done.4.left_ref) | copy-start | bytes 233476

commit v10 on v9

--- a/solution.py
+++ b/solution.py
@@ -352,9 +352,9 @@
         curl_x = (h_z - down_y(h_z)) - (h_y - down_z(h_y))
         curl_y = (h_x - down_z(h_x)) - (h_z - down_x(h_z))
         curl_z = (h_y - down_x(h_y)) - (h_x - down_y(h_x))
-        denominator = eps_cell + kerr_cell * squared
+        inverse = 1.0 / (eps_cell + kerr_cell * squared)
         new_e = [
-            (field + time_step * (curl - cur[0][c] - cur[1][c]) / denominator) * keep_mask
+            (field + time_step * (curl - cur[0][c] - cur[1][c]) * inverse) * keep_mask
             for c, (field, curl) in enumerate(zip(electric, (curl_x, curl_y, curl_z)))
         ]
         results = new_e + [h_x, h_y, h_z] + pol[0] + pol[1] + cur[0] + cur[1]

time: 39.1 us -> 39.1 us (level)
  no operation moved by 1% of the time
where the time goes in v10:
time: 39.1 us; the launch traced here: 38.7 us
  waiting for transfers between devices  15.7 us (40%)
  starting transfers between devices  9.55 us (24%)
  other arithmetic  5.24 us (13%)
  Pallas kernels  4.97 us (13%)
  local copies, waits for them, and re-layouts  2.48 us (6%)
  between operations  0.85 us (2%)
    ppermute x4, waiting for transfers between devices, from_offsets(): got[k] = lax.ppermute(value, axis, pairs)  9.95 us
    ppermute x4, starting transfers between devices, from_offsets(): got[k] = lax.ppermute(value, axis, pairs)  7.99 us
    ppermute x1, waiting for transfers between devices, from_offsets(): received = lax.ppermute(value, axis, pairs)  5.71 us
    pallas_call x1, Pallas kernels, body(): pl.pallas_call(functools.partial(steps_kernel, planes=planes, rows=rows,...  4.97 us
    ppermute x1, starting transfers between devices, from_offsets(): received = lax.ppermute(value, axis, pairs)  1.56 us
    concatenate x2, other arithmetic, body(): side = jnp.concatenate([above, below], axis=2)  1.43 us
    select_n x1, other arithmetic, body(): block = jnp.where(at_z + k == j, piece, block)  1.02 us
    concatenate x1, other arithmetic, body(): jnp.concatenate([electric, magnetic, polarization.reshape((-1,) + electri...  0.97 us
  transfers between devices with their start and end apart: 5, of which 4 were waited for; matrix products, arithmetic and copies ran while one was open for 10% of the time, Pallas kernels for 0%

profile of v10, /device:TPU:28, one launch (start us, length us, event | category | flops | bytes accessed | tf_op | source)
XLA Modules:
  0.0 38.7 jit_solution(9254168860124758399)
XLA Ops:
  0.6 1.0 %pad_maximum_fusion.4 = f32[18,4,8,128]{3,2,1,0:T(8,128)S(1)} fusion(f32[6,4,8,128]{3,2,1,0:T(8,128)} %bitcast.19, f32[6,4,8,128]{3,2,1,0:T(8,128)} %bitcast.21, f32[3,4,8,128]{3,2,1,0:T(8,128)} %param.12, f32[3,4,8,128]{3,2,1,0:T(8,128)} %param.11), kind=kLoop, calls=%fused_computation.10 | loop fusion | flops 221184 | bytes 589824 | tf_op jit(solution)/shard_map/concatenate | solution.py:163
  1.6 1.6 %collective-permute-start = (f32[18,4,8,128]{3,2,1,0:T(8,128)S(1)}, f32[18,4,8,128]{3,2,1,0:T(8,128)S(1)}, u32[]{:S(2)}, u32[]{:S(2)}) collective-permute-start(f32[18,4,8,128]{3,2,1,0:T(8,128)S(1)} %pad_maximum_fusion.4), channel_id=1, source_target_pairs={{0,16},{16,0},{1,17},{17,1},{2,18},{18,2},{3,19},{19,3},{4,20},{20... | collective-permute-start | bytes 884744 | tf_op jit(solution)/shard_map/ppermute | solution.py:29
  3.2 0.7 %convert_element_type.10 = f32[8,128]{1,0:T(8,128)S(1)} convert(s32[8,128]{1,0:T(8,128)} %param.15) | non-fusion elementwise | flops 1024 | bytes 8192 | tf_op jit(solution)/shard_map/convert_element_type | solution.py:198
  3.9 0.1 broadcast_and_fusion
  4.0 0.7 %and_convert_fusion.mask_ref = f32[8,16,256]{2,1,0:T(8,128)} fusion(pred[256]{0:T(512)(128)(4,1)S(1)} %compare_and_fusion, pred[8,16]{1,0:T(8,128)(4,1)S(1)} %broadcast_and_fusion), kind=kLoop, calls=%fused_computation.13 | loop fusion | flops 65536 | bytes 131456 | tf_op jit(solution)/shard_map/convert_element_type | solution.py:235
  4.7 5.7 %collective-permute-done = f32[18,4,8,128]{3,2,1,0:T(8,128)S(1)} collective-permute-done((f32[18,4,8,128]{3,2,1,0:T(8,128)S(1)}, f32[18,4,8,128]{3,2,1,0:T(8,128)S(1)}, u32[]{:S(2)}, u32[]{:S(2)}) %collective-permute-start) | collective-permute-done | bytes 294944 | tf_op jit(solution)/shard_map/ppermute | solution.py:29
  10.4 1.0 %select_select_fusion.1 = (f32[18,4,8,128]{3,2,1,0:T(8,128)S(1)}, f32[18,4,8,128]{3,2,1,0:T(8,128)S(1)}) fusion(f32[18,4,8,128]{3,2,1,0:T(8,128)S(1)} %collective-permute-done, pred[]{:T(512)S(6)} %and.56, pred[]{:T(512)S(6)} %eq.20, pred[]{:T(512)S(6)} %and.55, pred[]{:T(512)S(6)} %eq.19, pred[]{:T(512)S(6)} %eq.18, f32[6,4,8,128]{3,2,1,0:T(8,128)} %bitcast.20, ...), kind=kLoop, calls=%fused_computation.12 | loop fusion | flops 811008 | bytes 1179656 | tf_op jit(solution)/shard_map/jit(_where)/select_n | solution.py:184
  11.5 0.0 copy-start.3
  11.5 0.0 copy-start.4
  11.5 0.0 copy-start.5
  11.5 0.0 copy-start.6
  11.5 0.0 copy-start.7
  11.6 0.1 fusion.4
  11.7 2.4 %collective-permute-start.1 = (f32[608,128]{1,0:T(8,128)S(1)}, f32[608,128]{1,0:T(8,128)S(1)}, u32[]{:S(2)}, u32[]{:S(2)}) collective-permute-start(f32[608,128]{1,0:T(8,128)S(1)} %bitcast.24), channel_id=1, source_target_pairs={{1,0},{2,1},{3,2},{5,4},{6,5},{7,6},{9,8},{10,9},{11,10},{13,12},{... | collective-permute-start | bytes 933896 | tf_op jit(solution)/shard_map/ppermute | solution.py:34
  14.1 1.3 %collective-permute-start.2 = (f32[608,128]{1,0:T(8,128)S(1)}, f32[608,128]{1,0:T(8,128)S(1)}, u32[]{:S(2)}, u32[]{:S(2)}) collective-permute-start(f32[608,128]{1,0:T(8,128)S(1)} %bitcast.23), channel_id=1, source_target_pairs={{0,1},{1,2},{2,3},{4,5},{5,6},{6,7},{8,9},{9,10},{10,11},{12,13},{... | collective-permute-start | bytes 933896 | tf_op jit(solution)/shard_map/ppermute | solution.py:34
  15.4 0.0 copy-done.5
  15.5 0.0 copy-done.6
  15.5 0.6 %concatenate.21.table_ref = f32[8,8]{1,0:T(8,128)} concatenate(f32[1,8]{1,0:T(1,128)S(1)} %bitcast.27, f32[1,8]{1,0:T(1,128)S(1)} %bitcast.28, f32[2,8]{1,0:T(2,128)S(1)} %copy-done.5, f32[2,8]{1,0:T(2,128)S(1)} %get-tuple-element.14, f32[2,8]{1,0:T(2,128)S(1)} %get-tuple-element.13), dimensions={0} | concatenate | bytes 512 | tf_op jit(solution)/shard_map/concatenate | solution.py:238
  16.1 0.2 fusion.3
  16.3 3.5 %collective-permute-done.1 = f32[608,128]{1,0:T(8,128)S(1)} collective-permute-done((f32[608,128]{1,0:T(8,128)S(1)}, f32[608,128]{1,0:T(8,128)S(1)}, u32[]{:S(2)}, u32[]{:S(2)}) %collective-permute-start.1) | collective-permute-done | bytes 311328 | tf_op jit(solution)/shard_map/ppermute | solution.py:34
  19.8 4.1 %collective-permute-done.2 = f32[608,128]{1,0:T(8,128)S(1)} collective-permute-done((f32[608,128]{1,0:T(8,128)S(1)}, f32[608,128]{1,0:T(8,128)S(1)}, u32[]{:S(2)}, u32[]{:S(2)}) %collective-permute-start.2) | collective-permute-done | bytes 311328 | tf_op jit(solution)/shard_map/ppermute | solution.py:34
  23.9 0.4 %fusion.1 = (f32[19,8,8,4]{3,2,1,0:T(8,128)S(1)}, f32[19,8,8,4]{3,2,1,0:T(8,128)S(1)}) fusion(f32[19,8,4,128]{3,2,1,0:T(4,128)S(1)} %bitcast.15, f32[19,8,4,128]{3,2,1,0:T(4,128)S(1)} %bitcast.17), kind=kLoop, calls=%fused_computation.8 | loop fusion | flops 9728 | bytes 661504 | tf_op jit(solution)/shard_map/concatenate | solution.py:207
  24.4 0.2 pad_maximum_fusion
  24.7 0.4 copy.28
  25.1 1.9 %collective-permute-start.3 = (f32[8,2432]{1,0:T(8,128)S(1)}, f32[8,2432]{1,0:T(8,128)S(1)}, u32[]{:S(2)}, u32[]{:S(2)}) collective-permute-start(f32[8,2432]{1,0:T(8,128)S(1)} %pad.8), channel_id=1, source_target_pairs={{4,0},{8,4},{12,8},{5,1},{9,5},{13,9},{6,2},{10,6},{14,10},{7,3},{... | collective-permute-start | bytes 233480 | tf_op jit(solution)/shard_map/ppermute | solution.py:34
  27.0 0.4 copy.29
  27.4 2.4 %collective-permute-start.4 = (f32[8,2432]{1,0:T(8,128)S(1)}, f32[8,2432]{1,0:T(8,128)S(1)}, u32[]{:S(2)}, u32[]{:S(2)}) collective-permute-start(f32[8,2432]{1,0:T(8,128)S(1)} %pad.9), channel_id=1, source_target_pairs={{0,4},{4,8},{8,12},{1,5},{5,9},{9,13},{2,6},{6,10},{10,14},{3,7},{... | collective-permute-start | bytes 233480 | tf_op jit(solution)/shard_map/ppermute | solution.py:34
  29.8 1.0 %pad_maximum_fusion.2.side_ref = f32[19,8,8,128]{3,2,1,0:T(8,128)} fusion(f32[19,8,4,128]{3,2,1,0:T(4,128)S(1)} %bitcast.18, f32[19,8,4,128]{3,2,1,0:T(4,128)S(1)} %bitcast.16), kind=kLoop, calls=%fused_computation.4 | loop fusion | flops 155648 | bytes 1245184 | tf_op jit(solution)/shard_map/concatenate | solution.py:207
  30.8 0.0 collective-permute-done.3.right_ref
  30.8 2.3 %collective-permute-done.4.left_ref = f32[8,2432]{1,0:T(8,128)S(1)} collective-permute-done((f32[8,2432]{1,0:T(8,128)S(1)}, f32[8,2432]{1,0:T(8,128)S(1)}, u32[]{:S(2)}, u32[]{:S(2)}) %collective-permute-start.4) | collective-permute-done | bytes 77856 | tf_op jit(solution)/shard_map/ppermute | solution.py:34
  33.1 0.6 %copy-done.2 = f32[8,2432]{1,0:T(8,128)} copy-done((f32[8,2432]{1,0:T(8,128)}, f32[8,2432]{1,0:T(8,128)S(1)}, u32[]{:S(2)}) %copy-start.2) | copy-done | bytes 77848
  33.8 5.0 %shard_map.146 = (f32[3,4,8,128]{3,2,1,0:T(8,128)}, f32[3,4,8,128]{3,2,1,0:T(8,128)}, f32[2,3,4,8,128]{4,3,2,1,0:T(8,128)}, f32[2,3,4,8,128]{4,3,2,1,0:T(8,128)}, f32[4,8,128]{2,1,0:T(8,128)}) custom-call(s32[4]{0:T(128)} %advance_ref.1, s32[1]{0:T(128)} %bitcast.own_ref, f32[8,8]{1,0:T(8,128)} %concatenate.21.table_ref, f32[19,8,8,128]{3,2,1,0:T(8,128)} %copy-done, ...), custom_call_target="tpu_custom_call" | custom-call | tf_op jit(solution)/shard_map/pallas_call | solution.py:252
  (16 shorter events, 0.2 us)
Async XLA Ops:
  1.6 8.8 %collective-permute-start = (f32[18,4,8,128]{3,2,1,0:T(8,128)S(1)}, f32[18,4,8,128]{3,2,1,0:T(8,128)S(1)}, u32[]{:S(2)}, u32[]{:S(2)}) collective-permute-start(f32[18,4,8,128]{3,2,1,0:T(8,128)S(1)} %pad_maximum_fusion.4), channel_id=1, source_target_pairs={{0,16},{16,0},{1,17},{17,1},{2,18},{18,2},{3,19},{19,3},{4,20},{20... | collective-permute-start | bytes 884744 | tf_op jit(solution)/shard_map/ppermute | solution.py:29
  11.5 4.0 %copy-start.3 = (f32[2,8]{1,0:T(2,128)S(1)}, f32[2,8]{1,0:T(2,128)}, u32[]{:S(2)}) copy-start(f32[2,8]{1,0:T(2,128)} %param.20) | copy-start | bytes 196
  11.5 4.0 %copy-start.4 = (f32[2,8]{1,0:T(2,128)S(1)}, f32[2,8]{1,0:T(2,128)}, u32[]{:S(2)}) copy-start(f32[2,8]{1,0:T(2,128)} %param.21) | copy-start | bytes 196
  11.5 4.0 %copy-start.5 = (f32[2,8]{1,0:T(2,128)S(1)}, f32[2,8]{1,0:T(2,128)}, u32[]{:S(2)}) copy-start(f32[2,8]{1,0:T(2,128)} %param.19) | copy-start | bytes 196
  11.5 4.0 %copy-start.6 = (f32[8]{0:T(128)S(1)}, f32[8]{0:T(128)}, u32[]{:S(2)}) copy-start(f32[8]{0:T(128)} %param.17) | copy-start | bytes 100
  11.5 4.0 %copy-start.7 = (f32[8]{0:T(128)S(1)}, f32[8]{0:T(128)}, u32[]{:S(2)}) copy-start(f32[8]{0:T(128)} %param.18) | copy-start | bytes 100
  11.6 4.7 %copy-start = (f32[19,8,8,128]{3,2,1,0:T(8,128)}, f32[19,8,8,128]{3,2,1,0:T(8,128)S(1)}, u32[]{:S(2)}) copy-start(f32[19,8,8,128]{3,2,1,0:T(8,128)S(1)} %pad_maximum_fusion.3.state_ref) | copy-start | bytes 1867780
  11.7 8.1 %collective-permute-start.1 = (f32[608,128]{1,0:T(8,128)S(1)}, f32[608,128]{1,0:T(8,128)S(1)}, u32[]{:S(2)}, u32[]{:S(2)}) collective-permute-start(f32[608,128]{1,0:T(8,128)S(1)} %bitcast.24), channel_id=1, source_target_pairs={{1,0},{2,1},{3,2},{5,4},{6,5},{7,6},{9,8},{10,9},{11,10},{13,12},{... | collective-permute-start | bytes 933896 | tf_op jit(solution)/shard_map/ppermute | solution.py:34
  14.1 9.8 %collective-permute-start.2 = (f32[608,128]{1,0:T(8,128)S(1)}, f32[608,128]{1,0:T(8,128)S(1)}, u32[]{:S(2)}, u32[]{:S(2)}) collective-permute-start(f32[608,128]{1,0:T(8,128)S(1)} %bitcast.23), channel_id=1, source_target_pairs={{0,1},{1,2},{2,3},{4,5},{5,6},{6,7},{8,9},{9,10},{10,11},{12,13},{... | collective-permute-start | bytes 933896 | tf_op jit(solution)/shard_map/ppermute | solution.py:34
  25.1 5.8 %collective-permute-start.3 = (f32[8,2432]{1,0:T(8,128)S(1)}, f32[8,2432]{1,0:T(8,128)S(1)}, u32[]{:S(2)}, u32[]{:S(2)}) collective-permute-start(f32[8,2432]{1,0:T(8,128)S(1)} %pad.8), channel_id=1, source_target_pairs={{4,0},{8,4},{12,8},{5,1},{9,5},{13,9},{6,2},{10,6},{14,10},{7,3},{... | collective-permute-start | bytes 233480 | tf_op jit(solution)/shard_map/ppermute | solution.py:34
  27.4 5.7 %collective-permute-start.4 = (f32[8,2432]{1,0:T(8,128)S(1)}, f32[8,2432]{1,0:T(8,128)S(1)}, u32[]{:S(2)}, u32[]{:S(2)}) collective-permute-start(f32[8,2432]{1,0:T(8,128)S(1)} %pad.9), channel_id=1, source_target_pairs={{0,4},{4,8},{8,12},{1,5},{5,9},{9,13},{2,6},{6,10},{10,14},{3,7},{... | collective-permute-start | bytes 233480 | tf_op jit(solution)/shard_map/ppermute | solution.py:34
  30.8 2.3 %copy-start.1 = (f32[8,2432]{1,0:T(8,128)}, f32[8,2432]{1,0:T(8,128)S(1)}, u32[]{:S(2)}) copy-start(f32[8,2432]{1,0:T(8,128)S(1)} %collective-permute-done.3.right_ref) | copy-start | bytes 233476
  33.1 0.6 %copy-start.2 = (f32[8,2432]{1,0:T(8,128)}, f32[8,2432]{1,0:T(8,128)S(1)}, u32[]{:S(2)}) copy-start(f32[8,2432]{1,0:T(8,128)S(1)} %collective-permute-done.4.left_ref) | copy-start | bytes 233476

commit v11 on v10

--- a/solution.py
+++ b/solution.py
@@ -335,7 +335,16 @@
 
     amount = 0
     for moment in range(STEPS):
-        values = [work_ref[c, pl.ds(amount, depth)] for c in range(fields - 1)]
+        last = moment == STEPS - 1
+
+        def own(f):
+            return f[..., 0:rows, 0:columns] if last else f
+
+        values = [work_ref[c, pl.ds(amount, depth)] for c in range(6)]
+        if last:
+            values += [work_ref[c, pl.ds(amount, depth), 0:rows, 0:columns] for c in range(6, fields - 1)]
+        else:
+            values += [work_ref[c, pl.ds(amount, depth)] for c in range(6, fields - 1)]
         e_x, e_y, e_z = values[0:3]
         h_x, h_y, h_z = values[3:6]
         pol = [values[6:9], values[9:12]]
@@ -343,23 +352,32 @@
         h_x = (h_x - time_step * ((up_y(e_z) - e_z) - (up_z(e_y) - e_y))) * keep_mask
         h_y = (h_y - time_step * ((up_z(e_x) - e_x) - (up_x(e_z) - e_z))) * keep_mask
         h_z = (h_z - time_step * ((up_x(e_y) - e_y) - (up_y(e_x) - e_x))) * keep_mask
-        squared = e_x * e_x + e_y * e_y + e_z * e_z
-        electric = (e_x, e_y, e_z)
+        electric = (own(e_x), own(e_y), own(e_z))
+        squared = electric[0] * electric[0] + electric[1] * electric[1] + electric[2] * electric[2]
         for p in range(2):
             for c in range(3):
-                cur[p][c] = keep_rate[p] * cur[p][c] + drive_rate[p] * (strength[p] * electric[c] - pol[p][c])
+                cur[p][c] = own(keep_rate[p]) * cur[p][c] + own(drive_rate[p]) * (
+                    own(strength[p]) * electric[c] - pol[p][c]
+                )
                 pol[p][c] = pol[p][c] + time_step * cur[p][c]
-        curl_x = (h_z - down_y(h_z)) - (h_y - down_z(h_y))
-        curl_y = (h_x - down_z(h_x)) - (h_z - down_x(h_z))
-        curl_z = (h_y - down_x(h_y)) - (h_x - down_y(h_x))
-        inverse = 1.0 / (eps_cell + kerr_cell * squared)
+        curl_x = (own(h_z) - own(down_y(h_z))) - (own(h_y) - own(down_z(h_y)))
+        curl_y = (own(h_x) - own(down_z(h_x))) - (own(h_z) - own(down_x(h_z)))
+        curl_z = (own(h_y) - own(down_x(h_y))) - (own(h_x) - own(down_y(h_x)))
+        denominator = own(eps_cell) + own(kerr_cell) * squared
         new_e = [
-            (field + time_step * (curl - cur[0][c] - cur[1][c]) * inverse) * keep_mask
+            (field + time_step * (curl - cur[0][c] - cur[1][c]) / denominator) * own(keep_mask)
             for c, (field, curl) in enumerate(zip(electric, (curl_x, curl_y, curl_z)))
         ]
-        results = new_e + [h_x, h_y, h_z] + pol[0] + pol[1] + cur[0] + cur[1]
+        for c in range(3):
+            work_ref[3 + c, 0:depth] = (h_x, h_y, h_z)[c]
+        results = new_e + [None, None, None] + pol[0] + pol[1] + cur[0] + cur[1]
         for c in range(fields - 1):
-            work_ref[c, 0:depth] = results[c]
+            if c in (3, 4, 5):
+                continue
+            if last:
+                work_ref[c, 0:depth, 0:rows, 0:columns] = results[c]
+            else:
+                work_ref[c, 0:depth] = results[c]
         amount = advance_ref[moment]
 
     start = amount + own_ref[0]

time: 39.1 us -> 38.7 us (0.990)
  no operation moved by 1% of the time
where the time goes in v11:
time: 38.7 us; the launch traced here: 38.4 us
  waiting for transfers between devices  15.7 us (41%)
  starting transfers between devices  9.55 us (25%)
  other arithmetic  5.24 us (14%)
  Pallas kernels  4.61 us (12%)
  local copies, waits for them, and re-layouts  2.48 us (6%)
  between operations  0.85 us (2%)
    ppermute x4, waiting for transfers between devices, from_offsets(): got[k] = lax.ppermute(value, axis, pairs)  9.95 us
    ppermute x4, starting transfers between devices, from_offsets(): got[k] = lax.ppermute(value, axis, pairs)  7.99 us
    ppermute x1, waiting for transfers between devices, from_offsets(): received = lax.ppermute(value, axis, pairs)  5.71 us
    pallas_call x1, Pallas kernels, body(): pl.pallas_call(functools.partial(steps_kernel, planes=planes, rows=rows,...  4.61 us
    ppermute x1, starting transfers between devices, from_offsets(): received = lax.ppermute(value, axis, pairs)  1.56 us
    concatenate x2, other arithmetic, body(): side = jnp.concatenate([above, below], axis=2)  1.43 us
    select_n x1, other arithmetic, body(): block = jnp.where(at_z + k == j, piece, block)  1.02 us
    concatenate x1, other arithmetic, body(): jnp.concatenate([electric, magnetic, polarization.reshape((-1,) + electri...  0.97 us
  transfers between devices with their start and end apart: 5, of which 4 were waited for; matrix products, arithmetic and copies ran while one was open for 10% of the time, Pallas kernels for 0%

profile of v11, /device:TPU:28, one launch (start us, length us, event | category | flops | bytes accessed | tf_op | source)
XLA Modules:
  0.0 38.4 jit_solution(9702624233697271244)
XLA Ops:
  0.6 1.0 %pad_maximum_fusion.4 = f32[18,4,8,128]{3,2,1,0:T(8,128)S(1)} fusion(f32[6,4,8,128]{3,2,1,0:T(8,128)} %bitcast.19, f32[6,4,8,128]{3,2,1,0:T(8,128)} %bitcast.21, f32[3,4,8,128]{3,2,1,0:T(8,128)} %param.12, f32[3,4,8,128]{3,2,1,0:T(8,128)} %param.11), kind=kLoop, calls=%fused_computation.10 | loop fusion | flops 221184 | bytes 589824 | tf_op jit(solution)/shard_map/concatenate | solution.py:163
  1.6 1.6 %collective-permute-start = (f32[18,4,8,128]{3,2,1,0:T(8,128)S(1)}, f32[18,4,8,128]{3,2,1,0:T(8,128)S(1)}, u32[]{:S(2)}, u32[]{:S(2)}) collective-permute-start(f32[18,4,8,128]{3,2,1,0:T(8,128)S(1)} %pad_maximum_fusion.4), channel_id=1, source_target_pairs={{0,16},{16,0},{1,17},{17,1},{2,18},{18,2},{3,19},{19,3},{4,20},{20... | collective-permute-start | bytes 884744 | tf_op jit(solution)/shard_map/ppermute | solution.py:29
  3.2 0.7 %convert_element_type.10 = f32[8,128]{1,0:T(8,128)S(1)} convert(s32[8,128]{1,0:T(8,128)} %param.15) | non-fusion elementwise | flops 1024 | bytes 8192 | tf_op jit(solution)/shard_map/convert_element_type | solution.py:198
  3.9 0.1 broadcast_and_fusion
  4.0 0.7 %and_convert_fusion.mask_ref = f32[8,16,256]{2,1,0:T(8,128)} fusion(pred[256]{0:T(512)(128)(4,1)S(1)} %compare_and_fusion, pred[8,16]{1,0:T(8,128)(4,1)S(1)} %broadcast_and_fusion), kind=kLoop, calls=%fused_computation.13 | loop fusion | flops 65536 | bytes 131456 | tf_op jit(solution)/shard_map/convert_element_type | solution.py:235
  4.7 5.7 %collective-permute-done = f32[18,4,8,128]{3,2,1,0:T(8,128)S(1)} collective-permute-done((f32[18,4,8,128]{3,2,1,0:T(8,128)S(1)}, f32[18,4,8,128]{3,2,1,0:T(8,128)S(1)}, u32[]{:S(2)}, u32[]{:S(2)}) %collective-permute-start) | collective-permute-done | bytes 294944 | tf_op jit(solution)/shard_map/ppermute | solution.py:29
  10.4 1.0 %select_select_fusion.1 = (f32[18,4,8,128]{3,2,1,0:T(8,128)S(1)}, f32[18,4,8,128]{3,2,1,0:T(8,128)S(1)}) fusion(f32[18,4,8,128]{3,2,1,0:T(8,128)S(1)} %collective-permute-done, pred[]{:T(512)S(6)} %and.56, pred[]{:T(512)S(6)} %eq.20, pred[]{:T(512)S(6)} %and.55, pred[]{:T(512)S(6)} %eq.19, pred[]{:T(512)S(6)} %eq.18, f32[6,4,8,128]{3,2,1,0:T(8,128)} %bitcast.20, ...), kind=kLoop, calls=%fused_computation.12 | loop fusion | flops 811008 | bytes 1179656 | tf_op jit(solution)/shard_map/jit(_where)/select_n | solution.py:184
  11.5 0.0 copy-start.3
  11.5 0.0 copy-start.4
  11.5 0.0 copy-start.5
  11.5 0.0 copy-start.6
  11.5 0.0 copy-start.7
  11.6 0.1 fusion.4
  11.7 2.4 %collective-permute-start.1 = (f32[608,128]{1,0:T(8,128)S(1)}, f32[608,128]{1,0:T(8,128)S(1)}, u32[]{:S(2)}, u32[]{:S(2)}) collective-permute-start(f32[608,128]{1,0:T(8,128)S(1)} %bitcast.24), channel_id=1, source_target_pairs={{1,0},{2,1},{3,2},{5,4},{6,5},{7,6},{9,8},{10,9},{11,10},{13,12},{... | collective-permute-start | bytes 933896 | tf_op jit(solution)/shard_map/ppermute | solution.py:34
  14.1 1.3 %collective-permute-start.2 = (f32[608,128]{1,0:T(8,128)S(1)}, f32[608,128]{1,0:T(8,128)S(1)}, u32[]{:S(2)}, u32[]{:S(2)}) collective-permute-start(f32[608,128]{1,0:T(8,128)S(1)} %bitcast.23), channel_id=1, source_target_pairs={{0,1},{1,2},{2,3},{4,5},{5,6},{6,7},{8,9},{9,10},{10,11},{12,13},{... | collective-permute-start | bytes 933896 | tf_op jit(solution)/shard_map/ppermute | solution.py:34
  15.4 0.0 copy-done.5
  15.5 0.0 copy-done.6
  15.5 0.6 %concatenate.21.table_ref = f32[8,8]{1,0:T(8,128)} concatenate(f32[1,8]{1,0:T(1,128)S(1)} %bitcast.27, f32[1,8]{1,0:T(1,128)S(1)} %bitcast.28, f32[2,8]{1,0:T(2,128)S(1)} %copy-done.5, f32[2,8]{1,0:T(2,128)S(1)} %get-tuple-element.14, f32[2,8]{1,0:T(2,128)S(1)} %get-tuple-element.13), dimensions={0} | concatenate | bytes 512 | tf_op jit(solution)/shard_map/concatenate | solution.py:238
  16.1 0.2 fusion.3
  16.3 3.5 %collective-permute-done.1 = f32[608,128]{1,0:T(8,128)S(1)} collective-permute-done((f32[608,128]{1,0:T(8,128)S(1)}, f32[608,128]{1,0:T(8,128)S(1)}, u32[]{:S(2)}, u32[]{:S(2)}) %collective-permute-start.1) | collective-permute-done | bytes 311328 | tf_op jit(solution)/shard_map/ppermute | solution.py:34
  19.8 4.1 %collective-permute-done.2 = f32[608,128]{1,0:T(8,128)S(1)} collective-permute-done((f32[608,128]{1,0:T(8,128)S(1)}, f32[608,128]{1,0:T(8,128)S(1)}, u32[]{:S(2)}, u32[]{:S(2)}) %collective-permute-start.2) | collective-permute-done | bytes 311328 | tf_op jit(solution)/shard_map/ppermute | solution.py:34
  23.9 0.4 %fusion.1 = (f32[19,8,8,4]{3,2,1,0:T(8,128)S(1)}, f32[19,8,8,4]{3,2,1,0:T(8,128)S(1)}) fusion(f32[19,8,4,128]{3,2,1,0:T(4,128)S(1)} %bitcast.15, f32[19,8,4,128]{3,2,1,0:T(4,128)S(1)} %bitcast.17), kind=kLoop, calls=%fused_computation.8 | loop fusion | flops 9728 | bytes 661504 | tf_op jit(solution)/shard_map/concatenate | solution.py:207
  24.4 0.2 pad_maximum_fusion
  24.7 0.4 copy.28
  25.1 1.9 %collective-permute-start.3 = (f32[8,2432]{1,0:T(8,128)S(1)}, f32[8,2432]{1,0:T(8,128)S(1)}, u32[]{:S(2)}, u32[]{:S(2)}) collective-permute-start(f32[8,2432]{1,0:T(8,128)S(1)} %pad.8), channel_id=1, source_target_pairs={{4,0},{8,4},{12,8},{5,1},{9,5},{13,9},{6,2},{10,6},{14,10},{7,3},{... | collective-permute-start | bytes 233480 | tf_op jit(solution)/shard_map/ppermute | solution.py:34
  27.0 0.4 copy.29
  27.4 2.4 %collective-permute-start.4 = (f32[8,2432]{1,0:T(8,128)S(1)}, f32[8,2432]{1,0:T(8,128)S(1)}, u32[]{:S(2)}, u32[]{:S(2)}) collective-permute-start(f32[8,2432]{1,0:T(8,128)S(1)} %pad.9), channel_id=1, source_target_pairs={{0,4},{4,8},{8,12},{1,5},{5,9},{9,13},{2,6},{6,10},{10,14},{3,7},{... | collective-permute-start | bytes 233480 | tf_op jit(solution)/shard_map/ppermute | solution.py:34
  29.8 1.0 %pad_maximum_fusion.2.side_ref = f32[19,8,8,128]{3,2,1,0:T(8,128)} fusion(f32[19,8,4,128]{3,2,1,0:T(4,128)S(1)} %bitcast.18, f32[19,8,4,128]{3,2,1,0:T(4,128)S(1)} %bitcast.16), kind=kLoop, calls=%fused_computation.4 | loop fusion | flops 155648 | bytes 1245184 | tf_op jit(solution)/shard_map/concatenate | solution.py:207
  30.8 0.0 collective-permute-done.3.right_ref
  30.8 2.3 %collective-permute-done.4.left_ref = f32[8,2432]{1,0:T(8,128)S(1)} collective-permute-done((f32[8,2432]{1,0:T(8,128)S(1)}, f32[8,2432]{1,0:T(8,128)S(1)}, u32[]{:S(2)}, u32[]{:S(2)}) %collective-permute-start.4) | collective-permute-done | bytes 77856 | tf_op jit(solution)/shard_map/ppermute | solution.py:34
  33.1 0.6 %copy-done.2 = f32[8,2432]{1,0:T(8,128)} copy-done((f32[8,2432]{1,0:T(8,128)}, f32[8,2432]{1,0:T(8,128)S(1)}, u32[]{:S(2)}) %copy-start.2) | copy-done | bytes 77848
  33.8 4.6 %shard_map.146 = (f32[3,4,8,128]{3,2,1,0:T(8,128)}, f32[3,4,8,128]{3,2,1,0:T(8,128)}, f32[2,3,4,8,128]{4,3,2,1,0:T(8,128)}, f32[2,3,4,8,128]{4,3,2,1,0:T(8,128)}, f32[4,8,128]{2,1,0:T(8,128)}) custom-call(s32[4]{0:T(128)} %advance_ref.1, s32[1]{0:T(128)} %bitcast.own_ref, f32[8,8]{1,0:T(8,128)} %concatenate.21.table_ref, f32[19,8,8,128]{3,2,1,0:T(8,128)} %copy-done, ...), custom_call_target="tpu_custom_call" | custom-call | tf_op jit(solution)/shard_map/pallas_call | solution.py:252
  (16 shorter events, 0.2 us)
Async XLA Ops:
  1.6 8.8 %collective-permute-start = (f32[18,4,8,128]{3,2,1,0:T(8,128)S(1)}, f32[18,4,8,128]{3,2,1,0:T(8,128)S(1)}, u32[]{:S(2)}, u32[]{:S(2)}) collective-permute-start(f32[18,4,8,128]{3,2,1,0:T(8,128)S(1)} %pad_maximum_fusion.4), channel_id=1, source_target_pairs={{0,16},{16,0},{1,17},{17,1},{2,18},{18,2},{3,19},{19,3},{4,20},{20... | collective-permute-start | bytes 884744 | tf_op jit(solution)/shard_map/ppermute | solution.py:29
  11.5 4.0 %copy-start.3 = (f32[2,8]{1,0:T(2,128)S(1)}, f32[2,8]{1,0:T(2,128)}, u32[]{:S(2)}) copy-start(f32[2,8]{1,0:T(2,128)} %param.20) | copy-start | bytes 196
  11.5 4.0 %copy-start.4 = (f32[2,8]{1,0:T(2,128)S(1)}, f32[2,8]{1,0:T(2,128)}, u32[]{:S(2)}) copy-start(f32[2,8]{1,0:T(2,128)} %param.21) | copy-start | bytes 196
  11.5 4.0 %copy-start.5 = (f32[2,8]{1,0:T(2,128)S(1)}, f32[2,8]{1,0:T(2,128)}, u32[]{:S(2)}) copy-start(f32[2,8]{1,0:T(2,128)} %param.19) | copy-start | bytes 196
  11.5 4.0 %copy-start.6 = (f32[8]{0:T(128)S(1)}, f32[8]{0:T(128)}, u32[]{:S(2)}) copy-start(f32[8]{0:T(128)} %param.17) | copy-start | bytes 100
  11.5 4.0 %copy-start.7 = (f32[8]{0:T(128)S(1)}, f32[8]{0:T(128)}, u32[]{:S(2)}) copy-start(f32[8]{0:T(128)} %param.18) | copy-start | bytes 100
  11.6 4.7 %copy-start = (f32[19,8,8,128]{3,2,1,0:T(8,128)}, f32[19,8,8,128]{3,2,1,0:T(8,128)S(1)}, u32[]{:S(2)}) copy-start(f32[19,8,8,128]{3,2,1,0:T(8,128)S(1)} %pad_maximum_fusion.3.state_ref) | copy-start | bytes 1867780
  11.7 8.1 %collective-permute-start.1 = (f32[608,128]{1,0:T(8,128)S(1)}, f32[608,128]{1,0:T(8,128)S(1)}, u32[]{:S(2)}, u32[]{:S(2)}) collective-permute-start(f32[608,128]{1,0:T(8,128)S(1)} %bitcast.24), channel_id=1, source_target_pairs={{1,0},{2,1},{3,2},{5,4},{6,5},{7,6},{9,8},{10,9},{11,10},{13,12},{... | collective-permute-start | bytes 933896 | tf_op jit(solution)/shard_map/ppermute | solution.py:34
  14.1 9.8 %collective-permute-start.2 = (f32[608,128]{1,0:T(8,128)S(1)}, f32[608,128]{1,0:T(8,128)S(1)}, u32[]{:S(2)}, u32[]{:S(2)}) collective-permute-start(f32[608,128]{1,0:T(8,128)S(1)} %bitcast.23), channel_id=1, source_target_pairs={{0,1},{1,2},{2,3},{4,5},{5,6},{6,7},{8,9},{9,10},{10,11},{12,13},{... | collective-permute-start | bytes 933896 | tf_op jit(solution)/shard_map/ppermute | solution.py:34
  25.1 5.8 %collective-permute-start.3 = (f32[8,2432]{1,0:T(8,128)S(1)}, f32[8,2432]{1,0:T(8,128)S(1)}, u32[]{:S(2)}, u32[]{:S(2)}) collective-permute-start(f32[8,2432]{1,0:T(8,128)S(1)} %pad.8), channel_id=1, source_target_pairs={{4,0},{8,4},{12,8},{5,1},{9,5},{13,9},{6,2},{10,6},{14,10},{7,3},{... | collective-permute-start | bytes 233480 | tf_op jit(solution)/shard_map/ppermute | solution.py:34
  27.4 5.7 %collective-permute-start.4 = (f32[8,2432]{1,0:T(8,128)S(1)}, f32[8,2432]{1,0:T(8,128)S(1)}, u32[]{:S(2)}, u32[]{:S(2)}) collective-permute-start(f32[8,2432]{1,0:T(8,128)S(1)} %pad.9), channel_id=1, source_target_pairs={{0,4},{4,8},{8,12},{1,5},{5,9},{9,13},{2,6},{6,10},{10,14},{3,7},{... | collective-permute-start | bytes 233480 | tf_op jit(solution)/shard_map/ppermute | solution.py:34
  30.8 2.3 %copy-start.1 = (f32[8,2432]{1,0:T(8,128)}, f32[8,2432]{1,0:T(8,128)S(1)}, u32[]{:S(2)}) copy-start(f32[8,2432]{1,0:T(8,128)S(1)} %collective-permute-done.3.right_ref) | copy-start | bytes 233476
  33.1 0.6 %copy-start.2 = (f32[8,2432]{1,0:T(8,128)}, f32[8,2432]{1,0:T(8,128)S(1)}, u32[]{:S(2)}) copy-start(f32[8,2432]{1,0:T(8,128)S(1)} %collective-permute-done.4.left_ref) | copy-start | bytes 233476

commit v12 on v11

--- a/solution.py
+++ b/solution.py
@@ -173,7 +173,14 @@
     below = -(-STEPS // planes)
     above = -(-(STEPS + STEPS * WSHIFT) // planes)
     whole_column = (below + above + 1) * planes >= total_z
-    if whole_column:
+    if whole_column and n_prop == 2:
+        partner = lax.ppermute(state, "prop", [(0, 1), (1, 0)])
+        kernel_blocks = [state, partner]
+        block_at = jnp.stack([at_z * planes, (1 - at_z) * planes]).astype(jnp.int32)
+        state = jnp.concatenate(kernel_blocks, axis=1)
+        base_z = jnp.int32(0)
+        own_z = at_z * planes
+    elif whole_column:
         offsets = [k for k in range(-(n_prop - 1), n_prop) if k != 0]
         pieces = from_offsets(state, "prop", offsets)
         pieces[0] = state
@@ -193,9 +200,13 @@
         state = jnp.concatenate([pieces[k] for k in range(-below, above + 1)], axis=1)
         base_z = (at_z - below) * planes
         own_z = below * planes
+    if not (whole_column and n_prop == 2):
+        kernel_blocks = [state]
+        block_at = jnp.zeros((1,), jnp.int32)
     depth = state.shape[1]
 
     kinds = material.astype(jnp.float32)
+    kinds_own = kinds
     state = jnp.concatenate([state, jnp.broadcast_to(kinds[None, None], (1, depth, rows, columns))], axis=0)
     ring_rows = rows + 2 * halo
     tile = -(-2 * halo // 128) * 128
@@ -251,7 +262,8 @@
     block = (planes, rows, columns)
     outs = pl.pallas_call(
         functools.partial(
-            steps_kernel, planes=planes, rows=rows, columns=columns, whole=whole_column, total=total_z
+            steps_kernel, planes=planes, rows=rows, columns=columns, whole=whole_column, total=total_z,
+            blocks=len(kernel_blocks),
         ),
         out_shape=(
             jax.ShapeDtypeStruct((3,) + block, jnp.float32),
@@ -264,8 +276,9 @@
             pl.BlockSpec(memory_space=pltpu.SMEM),
             pl.BlockSpec(memory_space=pltpu.SMEM),
             pl.BlockSpec(memory_space=pltpu.SMEM),
+            pl.BlockSpec(memory_space=pltpu.SMEM),
         ]
-        + [pl.BlockSpec(memory_space=pltpu.VMEM) for _ in range(5)],
+        + [pl.BlockSpec(memory_space=pltpu.VMEM) for _ in range(len(kernel_blocks) + 5)],
         out_specs=tuple(pl.BlockSpec(memory_space=pltpu.VMEM) for _ in range(5)),
         scratch_shapes=[
             pltpu.VMEM((fields, depth + WSHIFT, ring_rows, ring_columns), jnp.float32),
@@ -273,7 +286,7 @@
             pltpu.VMEM((tile, strip_length), jnp.float32),
             pltpu.VMEM((strip_length, tile), jnp.float32),
         ],
-    )(advance, own_at, table, state, side, from_right, from_left, keep_mask)
+    )(advance, own_at, block_at, table, kinds_own, *kernel_blocks, side, from_right, from_left, keep_mask)
     electric_o, magnetic_o, polarization_o, current_o, column_energy = outs
     if not whole_column:
         prefix = entering(jnp.sum(column_energy, axis=0), "prop")
@@ -282,10 +295,12 @@
 
 
 def steps_kernel(
-    advance_ref, own_ref, table_ref, state_ref, side_ref, right_ref, left_ref, mask_ref,
-    electric_ref, magnetic_ref, polarization_ref, current_ref, energy_ref,
-    work_ref, running_ref, strips_ref, turned_ref, *, planes, rows, columns, whole, total,
+    advance_ref, own_ref, block_at_ref, table_ref, kinds_ref, *refs, planes, rows, columns, whole, total, blocks,
 ):
+    block_refs = refs[:blocks]
+    (side_ref, right_ref, left_ref, mask_ref,
+     electric_ref, magnetic_ref, polarization_ref, current_ref, energy_ref,
+     work_ref, running_ref, strips_ref, turned_ref) = refs[blocks:]
     fields, depth = (work_ref.shape[0], work_ref.shape[1] - WSHIFT)
     ring_rows = work_ref.shape[2]
     tile = strips_ref.shape[0]
@@ -295,12 +310,19 @@
     strips_ref[0:strip_rows] = right_ref[...]
     strips_ref[tile - strip_rows:tile] = left_ref[...]
     turned_ref[...] = strips_ref[...].T
-    for c in range(fields):
-        work_ref[c, 0:depth, 0:rows, 0:columns] = state_ref[c]
-        work_ref[c, 0:depth, rows:, 0:columns] = side_ref[c]
-        for z in range(depth):
-            first_row = (c * depth + z) * ring_rows
-            work_ref[c, z, :, columns:] = turned_ref[first_row:first_row + ring_rows]
+    work_ref[fields - 1, 0, 0:rows, 0:columns] = kinds_ref[...]
+    local = 0
+    for b, block_ref in enumerate(block_refs):
+        size = block_ref.shape[1]
+        at = block_at_ref[b]
+        for c in range(fields):
+            if c < fields - 1:
+                work_ref[c, pl.ds(at, size), 0:rows, 0:columns] = block_ref[c]
+            work_ref[c, pl.ds(at, size), rows:, 0:columns] = side_ref[c, local:local + size]
+            for z in range(size):
+                first_row = (c * depth + local + z) * ring_rows
+                work_ref[c, at + z, :, columns:] = turned_ref[first_row:first_row + ring_rows]
+        local += size
     kinds = work_ref[fields - 1, 0]
 
     def lookup(row):

time: 38.7 us -> 38.9 us (level)
  other arithmetic: 5.24 us -> 6.62 us
  waiting for transfers between devices: 15.7 us -> 14.4 us
    concatenate x1, other arithmetic: 0.04 us -> 1.1 us  [body(): jnp.concatenate([state, jnp.broadcast_to(kinds[None, None], (1, depth, ro...]
    select_n x1 -> x0, other arithmetic: 1.02 us -> none  [body(): block = jnp.where(at_z + k == j, piece, block)]
    ppermute x1, waiting for transfers between devices: 5.71 us -> 5.02 us  [body(): partner = lax.ppermute(state, 'prop', [(0, 1), (1, 0)])]
    div x1, other arithmetic: 0.01 us -> 0.7 us  [body(): time_step * pole_frequency * pole_frequency / (1.0 + half_damp)]
    another operation x0 -> x1, other arithmetic: none -> 0.66 us  [body(): block_at = jnp.stack([at_z * planes, (1 - at_z) * planes]).astype(jnp.int32)]
    ppermute x4, waiting for transfers between devices: 9.95 us -> 9.35 us  [from_offsets(): got[k] = lax.ppermute(value, axis, pairs)]
  transfers between devices with their start and end apart: 5 -> 5, of which waited for: 4 -> 4; matrix products, arithmetic and copies ran while one was open for 10% -> 13% of each run, Pallas kernels for 0% -> 0%
where the time goes in v12:
time: 38.9 us; the launch traced here: 38.6 us
  waiting for transfers between devices  14.4 us (37%)
  starting transfers between devices  9.55 us (25%)
  other arithmetic  6.62 us (17%)
  Pallas kernels  4.79 us (12%)
  local copies, waits for them, and re-layouts  2.48 us (6%)
  between operations  0.79 us (2%)
    ppermute x4, waiting for transfers between devices, from_offsets(): got[k] = lax.ppermute(value, axis, pairs)  9.35 us
    ppermute x4, starting transfers between devices, from_offsets(): got[k] = lax.ppermute(value, axis, pairs)  7.99 us
    ppermute x1, waiting for transfers between devices, body(): partner = lax.ppermute(state, 'prop', [(0, 1), (1, 0)])  5.02 us
    pallas_call x1, Pallas kernels, body(): pl.pallas_call(functools.partial(steps_kernel, planes=planes, rows=rows,...  4.79 us
    ppermute x1, starting transfers between devices, body(): partner = lax.ppermute(state, 'prop', [(0, 1), (1, 0)])  1.56 us
    concatenate x2, other arithmetic, body(): side = jnp.concatenate([above, below], axis=2)  1.42 us
    concatenate x1, other arithmetic, body(): jnp.concatenate([state, jnp.broadcast_to(kinds[None, None], (1, depth, ro...  1.1 us
    concatenate x1, other arithmetic, body(): jnp.concatenate([electric, magnetic, polarization.reshape((-1,) + electri...  0.97 us
  transfers between devices with their start and end apart: 5, of which 4 were waited for; matrix products, arithmetic and copies ran while one was open for 13% of the time, Pallas kernels for 0%

profile of v12, /device:TPU:28, one launch (start us, length us, event | category | flops | bytes accessed | tf_op | source)
XLA Modules:
  0.0 38.6 jit_solution(17582275947071580762)
XLA Ops:
  0.6 1.0 %pad_maximum_fusion.4.refs_0_ = f32[18,4,8,128]{3,2,1,0:T(8,128)S(1)} fusion(f32[6,4,8,128]{3,2,1,0:T(8,128)} %bitcast.20, f32[6,4,8,128]{3,2,1,0:T(8,128)} %bitcast.22, f32[3,4,8,128]{3,2,1,0:T(8,128)} %param.12, f32[3,4,8,128]{3,2,1,0:T(8,128)} %param.11), kind=kLoop, calls=%fused_computation.10 | loop fusion | flops 221184 | bytes 589824 | tf_op jit(solution)/shard_map/concatenate | solution.py:163
  1.6 0.0 copy-start.1
  1.6 1.6 %collective-permute-start = (f32[18,4,8,128]{3,2,1,0:T(8,128)S(1)}, f32[18,4,8,128]{3,2,1,0:T(8,128)S(1)}, u32[]{:S(2)}, u32[]{:S(2)}) collective-permute-start(f32[18,4,8,128]{3,2,1,0:T(8,128)S(1)} %pad_maximum_fusion.4.refs_0_), channel_id=1, source_target_pairs={{0,16},{16,0},{1,17},{17,1},{2,18},{18,2},{3,19},{19,3},{4,20},{20... | collective-permute-start | bytes 884744 | tf_op jit(solution)/shard_map/ppermute | solution.py:177
  3.2 0.7 %convert_element_type.10.kinds_ref = f32[8,128]{1,0:T(8,128)S(1)} convert(s32[8,128]{1,0:T(8,128)} %param.15) | non-fusion elementwise | flops 1024 | bytes 8192 | tf_op jit(solution)/shard_map/convert_element_type | solution.py:208
  3.9 0.1 broadcast_and_fusion
  4.0 0.7 %fusion.2 = (f32[2,8]{1,0:T(2,128)S(1)}, f32[2,8]{1,0:T(2,128)S(1)}) fusion(f32[2,8]{1,0:T(2,128)} %param.20, f32[2,8]{1,0:T(2,128)} %param.21), kind=kLoop, calls=%fused_computation.20 | loop fusion | flops 112 | bytes 256 | tf_op jit(solution)/shard_map/div | solution.py:255
  4.7 0.7 %and_convert_fusion.refs_5_ = f32[8,16,256]{2,1,0:T(8,128)} fusion(pred[256]{0:T(512)(128)(4,1)S(1)} %compare_and_fusion, pred[8,16]{1,0:T(8,128)(4,1)S(1)} %broadcast_and_fusion), kind=kLoop, calls=%fused_computation.11 | loop fusion | flops 65536 | bytes 131456 | tf_op jit(solution)/shard_map/convert_element_type | solution.py:246
  5.4 5.0 %collective-permute-done.refs_1_ = f32[18,4,8,128]{3,2,1,0:T(8,128)S(1)} collective-permute-done((f32[18,4,8,128]{3,2,1,0:T(8,128)S(1)}, f32[18,4,8,128]{3,2,1,0:T(8,128)S(1)}, u32[]{:S(2)}, u32[]{:S(2)}) %collective-permute-start) | collective-permute-done | bytes 294944 | tf_op jit(solution)/shard_map/ppermute | solution.py:177
  10.4 0.0 copy-start.5
  10.4 0.0 copy-start.6
  10.5 0.0 copy-start.7
  10.5 1.1 %pad_maximum_fusion.3 = f32[19,8,8,128]{3,2,1,0:T(8,128)S(1)} fusion(f32[1,8,8,128]{3,2,1,0:T(8,128)S(1)} %broadcast_in_dim.25, f32[18,4,8,128]{3,2,1,0:T(8,128)S(1)} %collective-permute-done.refs_1_, f32[6,4,8,128]{3,2,1,0:T(8,128)} %bitcast.21, f32[6,4,8,128]{3,2,1,0:T(8,128)} %bitcast.23, f32[3,4,8,128]{3,2,1,0:T(8,128)} %param.12, f32[3,4,8,128]{3,2,1,0:T(8,128)} %param.11), kind=kLoop, calls=%fused_computation.9 | loop fusion | flops 778240 | bytes 1245184 | tf_op jit(solution)/shard_map/concatenate | solution.py:210
  11.6 0.1 fusion.4
  11.8 2.4 %collective-permute-start.1 = (f32[608,128]{1,0:T(8,128)S(1)}, f32[608,128]{1,0:T(8,128)S(1)}, u32[]{:S(2)}, u32[]{:S(2)}) collective-permute-start(f32[608,128]{1,0:T(8,128)S(1)} %bitcast.25), channel_id=1, source_target_pairs={{1,0},{2,1},{3,2},{5,4},{6,5},{7,6},{9,8},{10,9},{11,10},{13,12},{... | collective-permute-start | bytes 933896 | tf_op jit(solution)/shard_map/ppermute | solution.py:34
  14.1 1.3 %collective-permute-start.2 = (f32[608,128]{1,0:T(8,128)S(1)}, f32[608,128]{1,0:T(8,128)S(1)}, u32[]{:S(2)}, u32[]{:S(2)}) collective-permute-start(f32[608,128]{1,0:T(8,128)S(1)} %bitcast.24), channel_id=1, source_target_pairs={{0,1},{1,2},{2,3},{4,5},{5,6},{6,7},{8,9},{9,10},{10,11},{12,13},{... | collective-permute-start | bytes 933896 | tf_op jit(solution)/shard_map/ppermute | solution.py:34
  15.4 0.7 %pad_add_fusion.block_at_ref = s32[2]{0:T(128)} fusion(s32[1]{0:T(128)} %bitcast.1, s32[1]{0:T(128)} %bitcast.own_ref), kind=kLoop, calls=%fused_computation.22 | loop fusion | flops 2 | bytes 16 | tf_op jit(solution)/shard_map/stack | solution.py:179
  16.1 0.0 copy-done.7
  16.1 0.6 %concatenate.21.table_ref = f32[8,8]{1,0:T(8,128)} concatenate(f32[1,8]{1,0:T(1,128)S(1)} %bitcast.28, f32[1,8]{1,0:T(1,128)S(1)} %bitcast.29, f32[2,8]{1,0:T(2,128)S(1)} %copy-done.5, f32[2,8]{1,0:T(2,128)S(1)} %get-tuple-element.12, f32[2,8]{1,0:T(2,128)S(1)} %get-tuple-element.11), dimensions={0} | concatenate | bytes 512 | tf_op jit(solution)/shard_map/concatenate | solution.py:249
  16.7 0.2 fusion.3
  16.9 2.9 %collective-permute-done.1 = f32[608,128]{1,0:T(8,128)S(1)} collective-permute-done((f32[608,128]{1,0:T(8,128)S(1)}, f32[608,128]{1,0:T(8,128)S(1)}, u32[]{:S(2)}, u32[]{:S(2)}) %collective-permute-start.1) | collective-permute-done | bytes 311328 | tf_op jit(solution)/shard_map/ppermute | solution.py:34
  19.8 4.1 %collective-permute-done.2 = f32[608,128]{1,0:T(8,128)S(1)} collective-permute-done((f32[608,128]{1,0:T(8,128)S(1)}, f32[608,128]{1,0:T(8,128)S(1)}, u32[]{:S(2)}, u32[]{:S(2)}) %collective-permute-start.2) | collective-permute-done | bytes 311328 | tf_op jit(solution)/shard_map/ppermute | solution.py:34
  24.0 0.4 %fusion.1 = (f32[19,8,8,4]{3,2,1,0:T(8,128)S(1)}, f32[19,8,8,4]{3,2,1,0:T(8,128)S(1)}) fusion(f32[19,8,4,128]{3,2,1,0:T(4,128)S(1)} %bitcast.16, f32[19,8,4,128]{3,2,1,0:T(4,128)S(1)} %bitcast.18), kind=kLoop, calls=%fused_computation.8 | loop fusion | flops 9728 | bytes 661504 | tf_op jit(solution)/shard_map/concatenate | solution.py:218
  24.4 0.2 pad_maximum_fusion
  24.7 0.4 copy.28
  25.1 1.9 %collective-permute-start.3 = (f32[8,2432]{1,0:T(8,128)S(1)}, f32[8,2432]{1,0:T(8,128)S(1)}, u32[]{:S(2)}, u32[]{:S(2)}) collective-permute-start(f32[8,2432]{1,0:T(8,128)S(1)} %pad.8), channel_id=1, source_target_pairs={{4,0},{8,4},{12,8},{5,1},{9,5},{13,9},{6,2},{10,6},{14,10},{7,3},{... | collective-permute-start | bytes 233480 | tf_op jit(solution)/shard_map/ppermute | solution.py:34
  27.0 0.4 copy.29
  27.5 2.4 %collective-permute-start.4 = (f32[8,2432]{1,0:T(8,128)S(1)}, f32[8,2432]{1,0:T(8,128)S(1)}, u32[]{:S(2)}, u32[]{:S(2)}) collective-permute-start(f32[8,2432]{1,0:T(8,128)S(1)} %pad.9), channel_id=1, source_target_pairs={{0,4},{4,8},{8,12},{1,5},{5,9},{9,13},{2,6},{6,10},{10,14},{3,7},{... | collective-permute-start | bytes 233480 | tf_op jit(solution)/shard_map/ppermute | solution.py:34
  29.9 1.0 %pad_maximum_fusion.2.refs_2_ = f32[19,8,8,128]{3,2,1,0:T(8,128)} fusion(f32[19,8,4,128]{3,2,1,0:T(4,128)S(1)} %bitcast.19, f32[19,8,4,128]{3,2,1,0:T(4,128)S(1)} %bitcast.17), kind=kLoop, calls=%fused_computation.4 | loop fusion | flops 155648 | bytes 1245184 | tf_op jit(solution)/shard_map/concatenate | solution.py:218
  30.8 0.0 collective-permute-done.3.refs_3_
  30.8 2.3 %collective-permute-done.4.refs_4_ = f32[8,2432]{1,0:T(8,128)S(1)} collective-permute-done((f32[8,2432]{1,0:T(8,128)S(1)}, f32[8,2432]{1,0:T(8,128)S(1)}, u32[]{:S(2)}, u32[]{:S(2)}) %collective-permute-start.4) | collective-permute-done | bytes 77856 | tf_op jit(solution)/shard_map/ppermute | solution.py:34
  33.2 0.6 %copy-done.3 = f32[8,2432]{1,0:T(8,128)} copy-done((f32[8,2432]{1,0:T(8,128)}, f32[8,2432]{1,0:T(8,128)S(1)}, u32[]{:S(2)}) %copy-start.3) | copy-done | bytes 77848
  33.8 4.8 %shard_map.146 = (f32[3,4,8,128]{3,2,1,0:T(8,128)}, f32[3,4,8,128]{3,2,1,0:T(8,128)}, f32[2,3,4,8,128]{4,3,2,1,0:T(8,128)}, f32[2,3,4,8,128]{4,3,2,1,0:T(8,128)}, f32[4,8,128]{2,1,0:T(8,128)}) custom-call(s32[4]{0:T(128)} %advance_ref.1, s32[1]{0:T(128)} %bitcast.own_ref, s32[2]{0:T(128)} %pad_add_fusion.block_at_ref, f32[8,8]{1,0:T(8,128)} %concatenate.21.table_ref, ...), custom_call_target="tpu_custom_call" | custom-call | tf_op jit(solution)/shard_map/pallas_call | solution.py:263
  (16 shorter events, 0.1 us)
Async XLA Ops:
  1.6 8.8 %copy-start.1 = (f32[18,4,8,128]{3,2,1,0:T(8,128)}, f32[18,4,8,128]{3,2,1,0:T(8,128)S(1)}, u32[]{:S(2)}) copy-start(f32[18,4,8,128]{3,2,1,0:T(8,128)S(1)} %pad_maximum_fusion.4.refs_0_) | copy-start | bytes 884740
  1.6 8.8 %collective-permute-start = (f32[18,4,8,128]{3,2,1,0:T(8,128)S(1)}, f32[18,4,8,128]{3,2,1,0:T(8,128)S(1)}, u32[]{:S(2)}, u32[]{:S(2)}) collective-permute-start(f32[18,4,8,128]{3,2,1,0:T(8,128)S(1)} %pad_maximum_fusion.4.refs_0_), channel_id=1, source_target_pairs={{0,16},{16,0},{1,17},{17,1},{2,18},{18,2},{3,19},{19,3},{4,20},{20... | collective-permute-start | bytes 884744 | tf_op jit(solution)/shard_map/ppermute | solution.py:177
  3.9 7.9 %copy-start.4 = (f32[8,128]{1,0:T(8,128)}, f32[8,128]{1,0:T(8,128)S(1)}, u32[]{:S(2)}) copy-start(f32[8,128]{1,0:T(8,128)S(1)} %convert_element_type.10.kinds_ref) | copy-start | bytes 12292
  10.4 1.3 %copy-start = (f32[18,4,8,128]{3,2,1,0:T(8,128)}, f32[18,4,8,128]{3,2,1,0:T(8,128)S(1)}, u32[]{:S(2)}) copy-start(f32[18,4,8,128]{3,2,1,0:T(8,128)S(1)} %collective-permute-done.refs_1_) | copy-start | bytes 884740
  10.4 5.7 %copy-start.5 = (f32[2,8]{1,0:T(2,128)S(1)}, f32[2,8]{1,0:T(2,128)}, u32[]{:S(2)}) copy-start(f32[2,8]{1,0:T(2,128)} %param.19) | copy-start | bytes 196
  10.4 5.7 %copy-start.6 = (f32[8]{0:T(128)S(1)}, f32[8]{0:T(128)}, u32[]{:S(2)}) copy-start(f32[8]{0:T(128)} %param.17) | copy-start | bytes 100
  10.5 5.6 %copy-start.7 = (f32[8]{0:T(128)S(1)}, f32[8]{0:T(128)}, u32[]{:S(2)}) copy-start(f32[8]{0:T(128)} %param.18) | copy-start | bytes 100
  11.8 8.1 %collective-permute-start.1 = (f32[608,128]{1,0:T(8,128)S(1)}, f32[608,128]{1,0:T(8,128)S(1)}, u32[]{:S(2)}, u32[]{:S(2)}) collective-permute-start(f32[608,128]{1,0:T(8,128)S(1)} %bitcast.25), channel_id=1, source_target_pairs={{1,0},{2,1},{3,2},{5,4},{6,5},{7,6},{9,8},{10,9},{11,10},{13,12},{... | collective-permute-start | bytes 933896 | tf_op jit(solution)/shard_map/ppermute | solution.py:34
  14.1 9.8 %collective-permute-start.2 = (f32[608,128]{1,0:T(8,128)S(1)}, f32[608,128]{1,0:T(8,128)S(1)}, u32[]{:S(2)}, u32[]{:S(2)}) collective-permute-start(f32[608,128]{1,0:T(8,128)S(1)} %bitcast.24), channel_id=1, source_target_pairs={{0,1},{1,2},{2,3},{4,5},{5,6},{6,7},{8,9},{9,10},{10,11},{12,13},{... | collective-permute-start | bytes 933896 | tf_op jit(solution)/shard_map/ppermute | solution.py:34
  25.1 5.7 %collective-permute-start.3 = (f32[8,2432]{1,0:T(8,128)S(1)}, f32[8,2432]{1,0:T(8,128)S(1)}, u32[]{:S(2)}, u32[]{:S(2)}) collective-permute-start(f32[8,2432]{1,0:T(8,128)S(1)} %pad.8), channel_id=1, source_target_pairs={{4,0},{8,4},{12,8},{5,1},{9,5},{13,9},{6,2},{10,6},{14,10},{7,3},{... | collective-permute-start | bytes 233480 | tf_op jit(solution)/shard_map/ppermute | solution.py:34
  27.5 5.7 %collective-permute-start.4 = (f32[8,2432]{1,0:T(8,128)S(1)}, f32[8,2432]{1,0:T(8,128)S(1)}, u32[]{:S(2)}, u32[]{:S(2)}) collective-permute-start(f32[8,2432]{1,0:T(8,128)S(1)} %pad.9), channel_id=1, source_target_pairs={{0,4},{4,8},{8,12},{1,5},{5,9},{9,13},{2,6},{6,10},{10,14},{3,7},{... | collective-permute-start | bytes 233480 | tf_op jit(solution)/shard_map/ppermute | solution.py:34
  30.8 2.3 %copy-start.2 = (f32[8,2432]{1,0:T(8,128)}, f32[8,2432]{1,0:T(8,128)S(1)}, u32[]{:S(2)}) copy-start(f32[8,2432]{1,0:T(8,128)S(1)} %collective-permute-done.3.refs_3_) | copy-start | bytes 233476
  33.2 0.6 %copy-start.3 = (f32[8,2432]{1,0:T(8,128)}, f32[8,2432]{1,0:T(8,128)S(1)}, u32[]{:S(2)}) copy-start(f32[8,2432]{1,0:T(8,128)S(1)} %collective-permute-done.4.refs_4_) | copy-start | bytes 233476

commit v13 on v11

--- a/solution.py
+++ b/solution.py
@@ -290,8 +290,8 @@
     ring_rows = work_ref.shape[2]
     tile = strips_ref.shape[0]
     strip_rows = right_ref.shape[0]
-    work_ref[:, depth:] = jnp.zeros((fields, WSHIFT) + work_ref.shape[2:], jnp.float32)
-    strips_ref[...] = jnp.zeros(strips_ref.shape, jnp.float32)
+    work_ref[0:fields - 1, depth:] = jnp.zeros((fields - 1, WSHIFT) + work_ref.shape[2:], jnp.float32)
+    strips_ref[strip_rows:tile - strip_rows] = jnp.zeros((tile - 2 * strip_rows, strips_ref.shape[1]), jnp.float32)
     strips_ref[0:strip_rows] = right_ref[...]
     strips_ref[tile - strip_rows:tile] = left_ref[...]
     turned_ref[...] = strips_ref[...].T

time: 38.7 us -> 38.7 us (level)
  no operation moved by 1% of the time
where the time goes in v13:
time: 38.7 us; the launch traced here: 38.4 us
  waiting for transfers between devices  15.7 us (41%)
  starting transfers between devices  9.55 us (25%)
  other arithmetic  5.24 us (14%)
  Pallas kernels  4.6 us (12%)
  local copies, waits for them, and re-layouts  2.48 us (6%)
  between operations  0.85 us (2%)
    ppermute x4, waiting for transfers between devices, from_offsets(): got[k] = lax.ppermute(value, axis, pairs)  9.95 us
    ppermute x4, starting transfers between devices, from_offsets(): got[k] = lax.ppermute(value, axis, pairs)  7.99 us
    ppermute x1, waiting for transfers between devices, from_offsets(): received = lax.ppermute(value, axis, pairs)  5.71 us
    pallas_call x1, Pallas kernels, body(): pl.pallas_call(functools.partial(steps_kernel, planes=planes, rows=rows,...  4.6 us
    ppermute x1, starting transfers between devices, from_offsets(): received = lax.ppermute(value, axis, pairs)  1.56 us
    concatenate x2, other arithmetic, body(): side = jnp.concatenate([above, below], axis=2)  1.43 us
    select_n x1, other arithmetic, body(): block = jnp.where(at_z + k == j, piece, block)  1.02 us
    concatenate x1, other arithmetic, body(): jnp.concatenate([electric, magnetic, polarization.reshape((-1,) + electri...  0.97 us
  transfers between devices with their start and end apart: 5, of which 4 were waited for; matrix products, arithmetic and copies ran while one was open for 10% of the time, Pallas kernels for 0%

profile of v13, /device:TPU:28, one launch (start us, length us, event | category | flops | bytes accessed | tf_op | source)
XLA Modules:
  0.0 38.4 jit_solution(10278072089711724478)
XLA Ops:
  0.6 1.0 %pad_maximum_fusion.4 = f32[18,4,8,128]{3,2,1,0:T(8,128)S(1)} fusion(f32[6,4,8,128]{3,2,1,0:T(8,128)} %bitcast.19, f32[6,4,8,128]{3,2,1,0:T(8,128)} %bitcast.21, f32[3,4,8,128]{3,2,1,0:T(8,128)} %param.12, f32[3,4,8,128]{3,2,1,0:T(8,128)} %param.11), kind=kLoop, calls=%fused_computation.10 | loop fusion | flops 221184 | bytes 589824 | tf_op jit(solution)/shard_map/concatenate | solution.py:163
  1.6 1.6 %collective-permute-start = (f32[18,4,8,128]{3,2,1,0:T(8,128)S(1)}, f32[18,4,8,128]{3,2,1,0:T(8,128)S(1)}, u32[]{:S(2)}, u32[]{:S(2)}) collective-permute-start(f32[18,4,8,128]{3,2,1,0:T(8,128)S(1)} %pad_maximum_fusion.4), channel_id=1, source_target_pairs={{0,16},{16,0},{1,17},{17,1},{2,18},{18,2},{3,19},{19,3},{4,20},{20... | collective-permute-start | bytes 884744 | tf_op jit(solution)/shard_map/ppermute | solution.py:29
  3.2 0.7 %convert_element_type.10 = f32[8,128]{1,0:T(8,128)S(1)} convert(s32[8,128]{1,0:T(8,128)} %param.15) | non-fusion elementwise | flops 1024 | bytes 8192 | tf_op jit(solution)/shard_map/convert_element_type | solution.py:198
  3.9 0.1 broadcast_and_fusion
  4.0 0.7 %and_convert_fusion.mask_ref = f32[8,16,256]{2,1,0:T(8,128)} fusion(pred[256]{0:T(512)(128)(4,1)S(1)} %compare_and_fusion, pred[8,16]{1,0:T(8,128)(4,1)S(1)} %broadcast_and_fusion), kind=kLoop, calls=%fused_computation.13 | loop fusion | flops 65536 | bytes 131456 | tf_op jit(solution)/shard_map/convert_element_type | solution.py:235
  4.7 5.7 %collective-permute-done = f32[18,4,8,128]{3,2,1,0:T(8,128)S(1)} collective-permute-done((f32[18,4,8,128]{3,2,1,0:T(8,128)S(1)}, f32[18,4,8,128]{3,2,1,0:T(8,128)S(1)}, u32[]{:S(2)}, u32[]{:S(2)}) %collective-permute-start) | collective-permute-done | bytes 294944 | tf_op jit(solution)/shard_map/ppermute | solution.py:29
  10.4 1.0 %select_select_fusion.1 = (f32[18,4,8,128]{3,2,1,0:T(8,128)S(1)}, f32[18,4,8,128]{3,2,1,0:T(8,128)S(1)}) fusion(f32[18,4,8,128]{3,2,1,0:T(8,128)S(1)} %collective-permute-done, pred[]{:T(512)S(6)} %and.56, pred[]{:T(512)S(6)} %eq.20, pred[]{:T(512)S(6)} %and.55, pred[]{:T(512)S(6)} %eq.19, pred[]{:T(512)S(6)} %eq.18, f32[6,4,8,128]{3,2,1,0:T(8,128)} %bitcast.20, ...), kind=kLoop, calls=%fused_computation.12 | loop fusion | flops 811008 | bytes 1179656 | tf_op jit(solution)/shard_map/jit(_where)/select_n | solution.py:184
  11.5 0.0 copy-start.3
  11.5 0.0 copy-start.4
  11.5 0.0 copy-start.5
  11.5 0.0 copy-start.6
  11.5 0.0 copy-start.7
  11.6 0.1 fusion.4
  11.7 2.4 %collective-permute-start.1 = (f32[608,128]{1,0:T(8,128)S(1)}, f32[608,128]{1,0:T(8,128)S(1)}, u32[]{:S(2)}, u32[]{:S(2)}) collective-permute-start(f32[608,128]{1,0:T(8,128)S(1)} %bitcast.24), channel_id=1, source_target_pairs={{1,0},{2,1},{3,2},{5,4},{6,5},{7,6},{9,8},{10,9},{11,10},{13,12},{... | collective-permute-start | bytes 933896 | tf_op jit(solution)/shard_map/ppermute | solution.py:34
  14.1 1.3 %collective-permute-start.2 = (f32[608,128]{1,0:T(8,128)S(1)}, f32[608,128]{1,0:T(8,128)S(1)}, u32[]{:S(2)}, u32[]{:S(2)}) collective-permute-start(f32[608,128]{1,0:T(8,128)S(1)} %bitcast.23), channel_id=1, source_target_pairs={{0,1},{1,2},{2,3},{4,5},{5,6},{6,7},{8,9},{9,10},{10,11},{12,13},{... | collective-permute-start | bytes 933896 | tf_op jit(solution)/shard_map/ppermute | solution.py:34
  15.4 0.0 copy-done.5
  15.5 0.0 copy-done.6
  15.5 0.6 %concatenate.21.table_ref = f32[8,8]{1,0:T(8,128)} concatenate(f32[1,8]{1,0:T(1,128)S(1)} %bitcast.27, f32[1,8]{1,0:T(1,128)S(1)} %bitcast.28, f32[2,8]{1,0:T(2,128)S(1)} %copy-done.5, f32[2,8]{1,0:T(2,128)S(1)} %get-tuple-element.14, f32[2,8]{1,0:T(2,128)S(1)} %get-tuple-element.13), dimensions={0} | concatenate | bytes 512 | tf_op jit(solution)/shard_map/concatenate | solution.py:238
  16.1 0.2 fusion.3
  16.3 3.5 %collective-permute-done.1 = f32[608,128]{1,0:T(8,128)S(1)} collective-permute-done((f32[608,128]{1,0:T(8,128)S(1)}, f32[608,128]{1,0:T(8,128)S(1)}, u32[]{:S(2)}, u32[]{:S(2)}) %collective-permute-start.1) | collective-permute-done | bytes 311328 | tf_op jit(solution)/shard_map/ppermute | solution.py:34
  19.8 4.1 %collective-permute-done.2 = f32[608,128]{1,0:T(8,128)S(1)} collective-permute-done((f32[608,128]{1,0:T(8,128)S(1)}, f32[608,128]{1,0:T(8,128)S(1)}, u32[]{:S(2)}, u32[]{:S(2)}) %collective-permute-start.2) | collective-permute-done | bytes 311328 | tf_op jit(solution)/shard_map/ppermute | solution.py:34
  23.9 0.4 %fusion.1 = (f32[19,8,8,4]{3,2,1,0:T(8,128)S(1)}, f32[19,8,8,4]{3,2,1,0:T(8,128)S(1)}) fusion(f32[19,8,4,128]{3,2,1,0:T(4,128)S(1)} %bitcast.15, f32[19,8,4,128]{3,2,1,0:T(4,128)S(1)} %bitcast.17), kind=kLoop, calls=%fused_computation.8 | loop fusion | flops 9728 | bytes 661504 | tf_op jit(solution)/shard_map/concatenate | solution.py:207
  24.4 0.2 pad_maximum_fusion
  24.7 0.4 copy.28
  25.1 1.9 %collective-permute-start.3 = (f32[8,2432]{1,0:T(8,128)S(1)}, f32[8,2432]{1,0:T(8,128)S(1)}, u32[]{:S(2)}, u32[]{:S(2)}) collective-permute-start(f32[8,2432]{1,0:T(8,128)S(1)} %pad.8), channel_id=1, source_target_pairs={{4,0},{8,4},{12,8},{5,1},{9,5},{13,9},{6,2},{10,6},{14,10},{7,3},{... | collective-permute-start | bytes 233480 | tf_op jit(solution)/shard_map/ppermute | solution.py:34
  27.0 0.4 copy.29
  27.4 2.4 %collective-permute-start.4 = (f32[8,2432]{1,0:T(8,128)S(1)}, f32[8,2432]{1,0:T(8,128)S(1)}, u32[]{:S(2)}, u32[]{:S(2)}) collective-permute-start(f32[8,2432]{1,0:T(8,128)S(1)} %pad.9), channel_id=1, source_target_pairs={{0,4},{4,8},{8,12},{1,5},{5,9},{9,13},{2,6},{6,10},{10,14},{3,7},{... | collective-permute-start | bytes 233480 | tf_op jit(solution)/shard_map/ppermute | solution.py:34
  29.8 1.0 %pad_maximum_fusion.2.side_ref = f32[19,8,8,128]{3,2,1,0:T(8,128)} fusion(f32[19,8,4,128]{3,2,1,0:T(4,128)S(1)} %bitcast.18, f32[19,8,4,128]{3,2,1,0:T(4,128)S(1)} %bitcast.16), kind=kLoop, calls=%fused_computation.4 | loop fusion | flops 155648 | bytes 1245184 | tf_op jit(solution)/shard_map/concatenate | solution.py:207
  30.8 0.0 collective-permute-done.3.right_ref
  30.8 2.3 %collective-permute-done.4.left_ref = f32[8,2432]{1,0:T(8,128)S(1)} collective-permute-done((f32[8,2432]{1,0:T(8,128)S(1)}, f32[8,2432]{1,0:T(8,128)S(1)}, u32[]{:S(2)}, u32[]{:S(2)}) %collective-permute-start.4) | collective-permute-done | bytes 77856 | tf_op jit(solution)/shard_map/ppermute | solution.py:34
  33.1 0.6 %copy-done.2 = f32[8,2432]{1,0:T(8,128)} copy-done((f32[8,2432]{1,0:T(8,128)}, f32[8,2432]{1,0:T(8,128)S(1)}, u32[]{:S(2)}) %copy-start.2) | copy-done | bytes 77848
  33.8 4.6 %shard_map.146 = (f32[3,4,8,128]{3,2,1,0:T(8,128)}, f32[3,4,8,128]{3,2,1,0:T(8,128)}, f32[2,3,4,8,128]{4,3,2,1,0:T(8,128)}, f32[2,3,4,8,128]{4,3,2,1,0:T(8,128)}, f32[4,8,128]{2,1,0:T(8,128)}) custom-call(s32[4]{0:T(128)} %advance_ref.1, s32[1]{0:T(128)} %bitcast.own_ref, f32[8,8]{1,0:T(8,128)} %concatenate.21.table_ref, f32[19,8,8,128]{3,2,1,0:T(8,128)} %copy-done, ...), custom_call_target="tpu_custom_call" | custom-call | tf_op jit(solution)/shard_map/pallas_call | solution.py:252
  (16 shorter events, 0.2 us)
Async XLA Ops:
  1.6 8.8 %collective-permute-start = (f32[18,4,8,128]{3,2,1,0:T(8,128)S(1)}, f32[18,4,8,128]{3,2,1,0:T(8,128)S(1)}, u32[]{:S(2)}, u32[]{:S(2)}) collective-permute-start(f32[18,4,8,128]{3,2,1,0:T(8,128)S(1)} %pad_maximum_fusion.4), channel_id=1, source_target_pairs={{0,16},{16,0},{1,17},{17,1},{2,18},{18,2},{3,19},{19,3},{4,20},{20... | collective-permute-start | bytes 884744 | tf_op jit(solution)/shard_map/ppermute | solution.py:29
  11.5 4.0 %copy-start.3 = (f32[2,8]{1,0:T(2,128)S(1)}, f32[2,8]{1,0:T(2,128)}, u32[]{:S(2)}) copy-start(f32[2,8]{1,0:T(2,128)} %param.20) | copy-start | bytes 196
  11.5 4.0 %copy-start.4 = (f32[2,8]{1,0:T(2,128)S(1)}, f32[2,8]{1,0:T(2,128)}, u32[]{:S(2)}) copy-start(f32[2,8]{1,0:T(2,128)} %param.21) | copy-start | bytes 196
  11.5 4.0 %copy-start.5 = (f32[2,8]{1,0:T(2,128)S(1)}, f32[2,8]{1,0:T(2,128)}, u32[]{:S(2)}) copy-start(f32[2,8]{1,0:T(2,128)} %param.19) | copy-start | bytes 196
  11.5 4.0 %copy-start.6 = (f32[8]{0:T(128)S(1)}, f32[8]{0:T(128)}, u32[]{:S(2)}) copy-start(f32[8]{0:T(128)} %param.17) | copy-start | bytes 100
  11.5 4.0 %copy-start.7 = (f32[8]{0:T(128)S(1)}, f32[8]{0:T(128)}, u32[]{:S(2)}) copy-start(f32[8]{0:T(128)} %param.18) | copy-start | bytes 100
  11.6 4.7 %copy-start = (f32[19,8,8,128]{3,2,1,0:T(8,128)}, f32[19,8,8,128]{3,2,1,0:T(8,128)S(1)}, u32[]{:S(2)}) copy-start(f32[19,8,8,128]{3,2,1,0:T(8,128)S(1)} %pad_maximum_fusion.3.state_ref) | copy-start | bytes 1867780
  11.7 8.1 %collective-permute-start.1 = (f32[608,128]{1,0:T(8,128)S(1)}, f32[608,128]{1,0:T(8,128)S(1)}, u32[]{:S(2)}, u32[]{:S(2)}) collective-permute-start(f32[608,128]{1,0:T(8,128)S(1)} %bitcast.24), channel_id=1, source_target_pairs={{1,0},{2,1},{3,2},{5,4},{6,5},{7,6},{9,8},{10,9},{11,10},{13,12},{... | collective-permute-start | bytes 933896 | tf_op jit(solution)/shard_map/ppermute | solution.py:34
  14.1 9.8 %collective-permute-start.2 = (f32[608,128]{1,0:T(8,128)S(1)}, f32[608,128]{1,0:T(8,128)S(1)}, u32[]{:S(2)}, u32[]{:S(2)}) collective-permute-start(f32[608,128]{1,0:T(8,128)S(1)} %bitcast.23), channel_id=1, source_target_pairs={{0,1},{1,2},{2,3},{4,5},{5,6},{6,7},{8,9},{9,10},{10,11},{12,13},{... | collective-permute-start | bytes 933896 | tf_op jit(solution)/shard_map/ppermute | solution.py:34
  25.1 5.8 %collective-permute-start.3 = (f32[8,2432]{1,0:T(8,128)S(1)}, f32[8,2432]{1,0:T(8,128)S(1)}, u32[]{:S(2)}, u32[]{:S(2)}) collective-permute-start(f32[8,2432]{1,0:T(8,128)S(1)} %pad.8), channel_id=1, source_target_pairs={{4,0},{8,4},{12,8},{5,1},{9,5},{13,9},{6,2},{10,6},{14,10},{7,3},{... | collective-permute-start | bytes 233480 | tf_op jit(solution)/shard_map/ppermute | solution.py:34
  27.4 5.7 %collective-permute-start.4 = (f32[8,2432]{1,0:T(8,128)S(1)}, f32[8,2432]{1,0:T(8,128)S(1)}, u32[]{:S(2)}, u32[]{:S(2)}) collective-permute-start(f32[8,2432]{1,0:T(8,128)S(1)} %pad.9), channel_id=1, source_target_pairs={{0,4},{4,8},{8,12},{1,5},{5,9},{9,13},{2,6},{6,10},{10,14},{3,7},{... | collective-permute-start | bytes 233480 | tf_op jit(solution)/shard_map/ppermute | solution.py:34
  30.8 2.3 %copy-start.1 = (f32[8,2432]{1,0:T(8,128)}, f32[8,2432]{1,0:T(8,128)S(1)}, u32[]{:S(2)}) copy-start(f32[8,2432]{1,0:T(8,128)S(1)} %collective-permute-done.3.right_ref) | copy-start | bytes 233476
  33.1 0.6 %copy-start.2 = (f32[8,2432]{1,0:T(8,128)}, f32[8,2432]{1,0:T(8,128)S(1)}, u32[]{:S(2)}) copy-start(f32[8,2432]{1,0:T(8,128)S(1)} %collective-permute-done.4.left_ref) | copy-start | bytes 233476
